TPU v7x, 512 devices: a whole 4x8x8 slice. The times are simulated.
512 devices in a mesh: cell: 64 (over z, y), tm: 8 (over x, core).
Axes of the slice: x: 4, y: 8, z: 8, core: 2. Of those that a mesh axis runs over, the one named last changes fastest.
Arguments:
- flux: bfloat16 [32, 16, 32768], P('tm', None, 'cell'), may hold values from -6 to 6
- foot: bfloat16 [4096, 64, 128], P('cell', 'tm'), may hold values from 0 to 0.029907227
- block_slot: int32 [4096, 64], P('cell', 'tm'), may hold values from 0 to 127, as said below
- block_time: int32 [4096, 64], P('cell', 'tm'), may hold values from 0 to 3
- block_count: int32 [4096, 8], P('cell', 'tm'), may hold values from 1 to 8, as said below
- request_tiles: int32 [64, 64, 2], P('cell'), may hold values from 0 to 3
- obs_weight: float32 [4096], P('cell'), may hold values from 1 to 10
- prior: float32 [32, 32], replicated
Outputs:
- obs_image: float32 [4096, 16], P('cell')
- hess: float32 [32, 16, 32768], P('tm', None, 'cell')
Inputs may be any that keep to these rules, and one draw needn't show every extreme that they name: `block_count`: every index along cell holds a sounding with 8 live blocks in every time group. Among the blocks of one device (its 64 soundings' slots of one time group), one source block_slot // 2 is named by exactly 16 blocks and no source by more.
All inputs are finite; a program needn't handle non-finite values.
Results may differ from a plain program's by a relative error of at most 0.00085.
Values may be sent and summed in bfloat16 or wider, within the bound.
No kernel may reach another device: no remote copies, remote signals or barrier semaphores. Data moves between devices by JAX's collectives and lax.ppermute only.
A program may use at most 64 MiB of HBM per device.

v0:
```python
import jax
import jax.numpy as jnp
from jax import lax
from jax.sharding import PartitionSpec as P


def local(flux, foot, block_slot, block_time, block_count, request_tiles, obs_weight, prior):
    slices, directions, cell_count = flux.shape
    tile_count = cell_count // 128
    sound_rows, blocks, _ = foot.shape
    per_source = request_tiles.shape[2]
    n_source = request_tiles.shape[1]
    block_live = jnp.arange(blocks, dtype=jnp.int32)[None, :] < block_count
    weights = jnp.where(block_live[:, :, None], foot, jnp.zeros_like(foot))
    requested = lax.all_to_all(request_tiles[0], "cell", split_axis=0, concat_axis=0, tiled=True)
    tiled = flux.reshape(slices, directions, tile_count, 128)
    outgoing = jnp.take(tiled, requested.reshape(-1), axis=2)
    received = lax.all_to_all(outgoing, "cell", split_axis=2, concat_axis=2, tiled=True)
    picked = received[block_time, :, block_slot, :]
    partial_value = jnp.einsum("sjc,sjkc->sk", weights, picked, preferred_element_type=jnp.float32)
    images = lax.psum(partial_value, "tm")
    weighted = obs_weight[:, None] * images
    update = weights.astype(jnp.float32)[:, :, None, :] * weighted[:, None, :, None]
    outbound = jnp.zeros((slices, directions, n_source * per_source, 128), jnp.float32)
    outbound = outbound.at[block_time, :, block_slot, :].add(update)
    returned = lax.all_to_all(
        outbound.astype(jnp.bfloat16), "cell", split_axis=2, concat_axis=2, tiled=True
    ).astype(outbound.dtype)
    adjoint = jnp.zeros((slices, directions, tile_count, 128), jnp.float32)
    adjoint = adjoint.at[:, :, requested.reshape(-1), :].add(returned)
    adjoint = adjoint.reshape(slices, directions, cell_count)
    my_group = lax.axis_index("tm")
    flux_wide = flux.astype(jnp.float32)
    panel = lax.dynamic_slice(prior, (0, my_group * slices), (lax.axis_size("tm") * slices, slices))
    coupled = lax.psum_scatter(
        jnp.einsum("ts,skn->tkn", panel, flux_wide, precision=lax.Precision.HIGHEST),
        "tm",
        scatter_dimension=0,
        tiled=True,
    )
    hess = adjoint + coupled
    return (images, hess)


def solution(mesh):
    in_specs = (
        P("tm", None, "cell"),
        P("cell", "tm", None),
        P("cell", "tm"),
        P("cell", "tm"),
        P("cell", "tm"),
        P("cell", None, None),
        P("cell"),
        P(),
    )
    out_specs = (P("cell", None), P("tm", None, "cell"))
    return jax.shard_map(local, mesh=mesh, in_specs=in_specs, out_specs=out_specs, check_vma=False)
```

profile of v0, /device:TPU:1, one launch (start us, length us, event | category | flops | bytes accessed | tf_op | source)
XLA Modules:
  0.0 271.4 jit_solution(17405927778641216264)
XLA Ops:
  7.2 1.4 copy.51
  8.6 17.1 %all-to-all-start = ((s32[64,1,2]{2,1,0:T(1,128)}), s32[64,1,2]{2,1,0:T(1,128)S(1)}, u32[]{:S(2)}, u32[]{:S(2)}) async-start(s32[64,1,2]{2,1,0:T(1,128)} %copy.51), calls=%async_computation | async-start | bytes 65536 | tf_op jit(solution)/shard_map/all_to_all | solution.py:15
  25.8 10.7 %all-to-all-done = s32[64,1,2]{2,1,0:T(1,128)S(1)} async-done(((s32[64,1,2]{2,1,0:T(1,128)}), s32[64,1,2]{2,1,0:T(1,128)S(1)}, u32[]{:S(2)}, u32[]{:S(2)}) %all-to-all-start) | async-done | bytes 544 | tf_op jit(solution)/shard_map/all_to_all | solution.py:15
  36.5 0.1 reshape.82
  36.7 0.5 broadcast.124
  37.2 0.7 reduce.5
  37.9 0.1 reshape.80
  38.1 1.1 gather_fusion
  39.1 1.6 select_bitcast_fusion
  40.8 4.8 %all-to-all-start.1 = ((bf16[4,16,128,128]{3,1,0,2:T(8,128)(2,1)}), bf16[4,16,128,128]{3,1,0,2:T(8,128)(2,1)S(1)}, u32[]{:S(2)}, u32[]{:S(2)}) async-start(bf16[4,16,128,128]{3,1,0,2:T(8,128)(2,1)} %select_bitcast_fusion), calls=%async_computation.1 | async-start | bytes 4194304 | tf_op jit(solution)/shard_map/all_to_all | solution.py:18
  45.6 0.1 copy.53
  45.7 0.1 reshape.92
  45.8 0.1 copy.55
  45.9 0.1 reshape.98
  46.1 0.1 fusion.2
  46.2 47.7 %all-to-all-done.1 = bf16[4,16,128,128]{3,1,0,2:T(8,128)(2,1)S(1)} async-done(((bf16[4,16,128,128]{3,1,0,2:T(8,128)(2,1)}), bf16[4,16,128,128]{3,1,0,2:T(8,128)(2,1)S(1)}, u32[]{:S(2)}, u32[]{:S(2)}) %all-to-all-start.1) | async-done | bytes 2097184 | tf_op jit(solution)/shard_map/all_to_all | solution.py:18
  93.9 1.7 copy.54
  95.6 4.3 %gather_fusion.1 = bf16[512,16,128]{2,1,0:T(8,128)(2,1)S(1)} fusion(bf16[4,16,128,128]{3,1,2,0:T(8,128)(2,1)} %copy.54, s32[512]{0:T(512)S(1)} %reshape.92), kind=kCustom, calls=%fused_computation.1 | custom fusion | bytes 4198400 | tf_op jit(solution)/shard_map/gather | solution.py:19
  99.9 1.0 fusion
  100.9 17.4 %psum.7 = f32[64,16]{0,1:T(8,128)S(1)} all-reduce(f32[64,16]{0,1:T(8,128)S(1)} %bitcast.52), channel_id=1, replica_groups=mesh['cell'=64,'tm'=8] {'tm'}, use_global_device_ids=true, to_apply=%region_0.1 | all-reduce | flops 1024 | bytes 8192 | tf_op jit(solution)/shard_map/psum | solution.py:21
  118.4 2.3 broadcast_multiply_fusion
  120.7 2.3 broadcast_in_dim.48
  123.0 63.0 %scatter_fusion = f32[4,16,128,128]{3,1,2,0:T(8,128)} fusion(f32[4,16,128,128]{3,1,2,0:T(8,128)} %broadcast_in_dim.48, s32[512]{0:T(512)S(1)} %reshape.98, f32[512,16,128]{2,1,0:T(8,128)} %bitcast.49), kind=kCustom, calls=%fused_computation.2 | custom fusion | flops 1048576 | bytes 12587008 | tf_op jit(solution)/shard_map/scatter-add | solution.py:25
  186.0 2.5 convert_element_type.11
  188.5 2.0 copy.57
  190.5 6.5 %all-to-all-start.2 = ((bf16[4,16,128,128]{3,1,0,2:T(8,128)(2,1)}), bf16[4,16,128,128]{3,1,0,2:T(8,128)(2,1)S(1)}, u32[]{:S(2)}, u32[]{:S(2)}) async-start(bf16[4,16,128,128]{3,1,0,2:T(8,128)(2,1)} %copy.57), calls=%async_computation.2 | async-start | bytes 4194304 | tf_op jit(solution)/shard_map/all_to_all | solution.py:26
  197.1 0.6 fusion.4
  197.7 1.6 copy.61
  199.3 46.9 %all-to-all-done.2 = bf16[4,16,128,128]{3,1,0,2:T(8,128)(2,1)S(1)} async-done(((bf16[4,16,128,128]{3,1,0,2:T(8,128)(2,1)}), bf16[4,16,128,128]{3,1,0,2:T(8,128)(2,1)S(1)}, u32[]{:S(2)}, u32[]{:S(2)}) %all-to-all-start.2) | async-done | bytes 2097184 | tf_op jit(solution)/shard_map/all_to_all | solution.py:26
  246.2 2.4 convert_bitcast_fusion
  248.6 14.3 %scatter_fusion.1 = f32[4,16,4,128]{3,1,2,0:T(8,128)S(1)} fusion(f32[4,16,4,128]{3,1,2,0:T(8,128)S(1)} %broadcast_in_dim.47, s32[128]{0:T(128)S(1)} %fusion.13, f32[128,4,16,128]{3,2,1,0:T(8,128)} %convert_bitcast_fusion), kind=kCustom, calls=%fused_computation.3 | custom fusion | flops 1048576 | bytes 12583424 | tf_op jit(solution)/shard_map/scatter-add | solution.py:30
  263.0 1.6 bitcast_add_fusion
  (29 shorter events, 0.4 us)
Async XLA Ops:
  7.2 18.6 %copy-start = (bf16[4,16,512]{2,1,0:T(8,128)(2,1)S(1)}, bf16[4,16,512]{2,1,0:T(8,128)(2,1)}, u32[]{:S(2)}) copy-start(bf16[4,16,512]{2,1,0:T(8,128)(2,1)} %param.8) | copy-start | bytes 196612
  8.6 27.9 %all-to-all-start = ((s32[64,1,2]{2,1,0:T(1,128)}), s32[64,1,2]{2,1,0:T(1,128)S(1)}, u32[]{:S(2)}, u32[]{:S(2)}) async-start(s32[64,1,2]{2,1,0:T(1,128)} %copy.51), calls=%async_computation | async-start | bytes 65536 | tf_op jit(solution)/shard_map/all_to_all | solution.py:15
  40.7 4.9 %copy-start.4 = (s32[64,8]{0,1:T(8,128)S(1)}, s32[64,8]{0,1:T(8,128)}, u32[]{:S(2)}) copy-start(s32[64,8]{0,1:T(8,128)} %param.10) | copy-start | bytes 6148
  40.7 4.9 %copy-start.5 = (s32[64,8]{0,1:T(8,128)S(1)}, s32[64,8]{0,1:T(8,128)}, u32[]{:S(2)}) copy-start(s32[64,8]{0,1:T(8,128)} %param.11) | copy-start | bytes 6148
  40.7 5.2 %copy-start.6 = (s32[64,1]{0,1:T(1,128)S(1)}, s32[64,1]{0,1:T(1,128)}, u32[]{:S(2)}) copy-start(s32[64,1]{0,1:T(1,128)} %param.12) | copy-start | bytes 772
  40.7 5.3 %copy-start.1 = (bf16[64,8,128]{2,1,0:T(8,128)(2,1)S(1)}, bf16[64,8,128]{2,1,0:T(8,128)(2,1)}, u32[]{:S(2)}) copy-start(bf16[64,8,128]{2,1,0:T(8,128)(2,1)} %param.9) | copy-start | bytes 393220
  40.8 53.1 %all-to-all-start.1 = ((bf16[4,16,128,128]{3,1,0,2:T(8,128)(2,1)}), bf16[4,16,128,128]{3,1,0,2:T(8,128)(2,1)S(1)}, u32[]{:S(2)}, u32[]{:S(2)}) async-start(bf16[4,16,128,128]{3,1,0,2:T(8,128)(2,1)} %select_bitcast_fusion), calls=%async_computation.1 | async-start | bytes 4194304 | tf_op jit(solution)/shard_map/all_to_all | solution.py:18
  99.9 18.4 %copy-start.7 = (f32[64]{0:T(128)S(1)}, f32[64]{0:T(128)}, u32[]{:S(2)}) copy-start(f32[64]{0:T(128)} %param.14) | copy-start | bytes 772
  118.3 2.4 copy-start.2
  190.5 6.6 %copy-start.3 = (f32[32,32]{1,0:T(8,128)S(1)}, f32[32,32]{1,0:T(8,128)}, u32[]{:S(2)}) copy-start(f32[32,32]{1,0:T(8,128)} %param.15) | copy-start | bytes 12292
  190.5 55.7 %all-to-all-start.2 = ((bf16[4,16,128,128]{3,1,0,2:T(8,128)(2,1)}), bf16[4,16,128,128]{3,1,0,2:T(8,128)(2,1)S(1)}, u32[]{:S(2)}, u32[]{:S(2)}) async-start(bf16[4,16,128,128]{3,1,0,2:T(8,128)(2,1)} %copy.57), calls=%async_computation.2 | async-start | bytes 4194304 | tf_op jit(solution)/shard_map/all_to_all | solution.py:26
  197.0 66.0 %reduce-scatter.2.cloned.1.call-start = ((), (), s32[]{:S(2)}) async-start(), calls=%async_computation.4 | async-start | bytes 1179648 | tf_op jit(solution)/shard_map/reduce_scatter | solution.py:35
Sparse Core Ops, SparseCore 0:
  200.6 35.0 reduce-scatter.1
where the time goes:
time: 276 us; the launch traced here: 271 us
  waiting for transfers between devices  105 us (38%)
  other arithmetic  88.7 us (32%)
  starting transfers between devices  28.5 us (10%)
  blocking collectives  17.4 us (6%)
  local copies, waits for them, and re-layouts  15.7 us (6%)
  between operations  14.3 us (5%)
    scatter-add x1, other arithmetic, local(): outbound = outbound.at[block_time, :, block_slot, :].add(update)  63 us
    all_to_all x1, waiting for transfers between devices, local(): lax.all_to_all(outgoing, 'cell', split_axis=2, concat_axis=2, tiled=True)  47.7 us
    all_to_all x1, waiting for transfers between devices, local(): lax.all_to_all(outbound.astype(jnp.bfloat16), 'cell', split_axis=2, conca...  46.9 us
    psum x1, blocking collectives, local(): images = lax.psum(partial_value, 'tm')  17.4 us
    all_to_all x1, starting transfers between devices, local(): lax.all_to_all(request_tiles[0], 'cell', split_axis=0, concat_axis=0, til...  17.1 us
    scatter-add x1, other arithmetic, local(): adjoint = adjoint.at[:, :, requested.reshape(-1), :].add(returned)  14.3 us
    all_to_all x1, waiting for transfers between devices, local(): lax.all_to_all(request_tiles[0], 'cell', split_axis=0, concat_axis=0, til...  10.7 us
    all_to_all x1, starting transfers between devices, local(): lax.all_to_all(outbound.astype(jnp.bfloat16), 'cell', split_axis=2, conca...  6.5 us
  transfers between devices with their start and end apart: 4, of which 3 were waited for; matrix products, arithmetic and copies ran while one was open for 7% of the time, Pallas kernels for 0%

commit v1 on v0

v1 whole, which is shorter than its diff:
```python
import jax
import jax.numpy as jnp
from jax import lax
from jax.sharding import PartitionSpec as P

TILE = 128
HI = lax.Precision.HIGHEST


def local(flux, foot, block_slot, block_time, block_count, request_tiles, obs_weight, prior):
    slices, directions, cell_count = flux.shape
    tiles = cell_count // TILE
    sounds, nb, _ = foot.shape
    n_source = request_tiles.shape[1]
    per_source = request_tiles.shape[2]
    n_blocks = sounds * nb
    cap = 16
    n_slot = n_source * cap
    n_meta = tiles * slices
    f32 = jnp.float32

    live = (jnp.arange(nb, dtype=jnp.int32)[None, :] < block_count).reshape(n_blocks)
    slot_ids = block_slot.reshape(n_blocks)
    source = slot_ids // per_source
    position = slot_ids % per_source
    local_tile = request_tiles[0].reshape(n_source * per_source)[source * per_source + position]
    meta = local_tile * slices + block_time.reshape(n_blocks)
    src_hot = (source[:, None] == jnp.arange(n_source, dtype=jnp.int32)[None, :]) & live[:, None]
    src_hot_b = src_hot.astype(jnp.bfloat16)
    row = jnp.arange(n_blocks, dtype=jnp.int32)
    lower = (row[None, :] < row[:, None]).astype(jnp.bfloat16)
    before = jnp.dot(lower, src_hot_b, preferred_element_type=f32)
    rank = jnp.sum(before * src_hot_b.astype(f32), axis=1).astype(jnp.int32)
    dest = jnp.where(live, source * cap + rank, n_slot)
    place = (dest[None, :] == jnp.arange(n_slot, dtype=jnp.int32)[:, None])
    place_b = place.astype(jnp.bfloat16)
    foot_flat = foot.reshape(n_blocks, TILE)
    foot_send = jnp.dot(place_b, foot_flat, preferred_element_type=f32).astype(jnp.bfloat16)
    meta_send = jnp.dot(place_b, meta.astype(jnp.bfloat16)[:, None], preferred_element_type=f32)
    meta_send = meta_send.reshape(n_source, cap).astype(jnp.bfloat16)
    meta_pad = jnp.zeros((n_source, TILE - cap), jnp.bfloat16)
    send = jnp.concatenate([foot_send.reshape(n_source, cap * TILE), meta_send, meta_pad], axis=1)
    recv = lax.all_to_all(send, "cell", split_axis=0, concat_axis=0, tiled=True)

    foot_r = recv[:, : cap * TILE].reshape(n_slot, TILE)
    meta_r = recv[:, cap * TILE : cap * TILE + cap].reshape(n_slot).astype(jnp.int32)
    meta_hot = (meta_r[:, None] == jnp.arange(n_meta, dtype=jnp.int32)[None, :]).astype(f32)
    panels = flux.reshape(slices, directions, tiles, TILE).transpose(3, 2, 0, 1)
    panels = panels.reshape(TILE, n_meta * directions)
    every = jnp.dot(foot_r, panels, preferred_element_type=f32).reshape(n_slot, n_meta, directions)
    partial = jnp.sum(every * meta_hot[:, :, None], axis=1)
    back = lax.all_to_all(
        partial.reshape(n_source, cap * directions), "cell", split_axis=0, concat_axis=0, tiled=True
    ).reshape(n_slot, directions)

    place_f = place.astype(f32)
    per_block = jnp.dot(place_f.T, back, precision=HI, preferred_element_type=f32)
    partial_value = per_block.reshape(sounds, nb, directions).sum(axis=1)
    images = lax.psum(partial_value, "tm")
    weighted = obs_weight[:, None] * images
    w_block = jnp.repeat(weighted, nb, axis=0)
    w_send = jnp.dot(place_f, w_block, precision=HI, preferred_element_type=f32)
    w_recv = lax.all_to_all(
        w_send.reshape(n_source, cap * directions), "cell", split_axis=0, concat_axis=0, tiled=True
    ).reshape(n_slot, directions)

    w_meta = (meta_hot[:, :, None] * w_recv[:, None, :]).reshape(n_slot, n_meta * directions)
    adj = jnp.dot(w_meta.T, foot_r.astype(f32), precision=HI, preferred_element_type=f32)
    adj = adj.reshape(tiles, slices, directions, TILE).transpose(1, 2, 0, 3)
    adjoint = adj.reshape(slices, directions, cell_count)

    my_group = lax.axis_index("tm")
    flux_wide = flux.astype(f32)
    panel = lax.dynamic_slice(prior, (0, my_group * slices), (lax.axis_size("tm") * slices, slices))
    coupled = lax.psum_scatter(
        jnp.einsum("ts,skn->tkn", panel, flux_wide, precision=HI),
        "tm",
        scatter_dimension=0,
        tiled=True,
    )
    hess = adjoint + coupled
    return (images, hess)


def solution(mesh):
    in_specs = (
        P("tm", None, "cell"),
        P("cell", "tm", None),
        P("cell", "tm"),
        P("cell", "tm"),
        P("cell", "tm"),
        P("cell", None, None),
        P("cell"),
        P(),
    )
    out_specs = (P("cell", None), P("tm", None, "cell"))
    return jax.shard_map(local, mesh=mesh, in_specs=in_specs, out_specs=out_specs, check_vma=False)
```

time: 276 us -> 123 us (0.45)
  the two profiles are of different devices: /device:TPU:1 before, /device:TPU:8 now
where the time goes in v1:
time: 123 us
  waiting for transfers between devices  34.6 us (28%)
  starting transfers between devices  27.2 us (22%)
  blocking collectives  23.6 us (19%)
  between operations  14.4 us (12%)
  local copies, waits for them, and re-layouts  13.6 us (11%)
  matrix products  5.85 us (5%)
  other arithmetic  3.75 us (3%)
    psum x1, blocking collectives, local(): images = lax.psum(partial_value, 'tm')  23.6 us
    all_to_all x1, starting transfers between devices, local(): recv = lax.all_to_all(send, 'cell', split_axis=0, concat_axis=0, tiled=True)  16.6 us
    all_to_all x1, waiting for transfers between devices, local(): recv = lax.all_to_all(send, 'cell', split_axis=0, concat_axis=0, tiled=True)  12.5 us
    all_to_all x1, waiting for transfers between devices, local(): lax.all_to_all(partial.reshape(n_source, cap * directions), 'cell', split...  11.4 us
    all_to_all x1, waiting for transfers between devices, local(): lax.all_to_all(w_send.reshape(n_source, cap * directions), 'cell', split_...  10.7 us
    all_to_all x1, starting transfers between devices, local(): lax.all_to_all(w_send.reshape(n_source, cap * directions), 'cell', split_...  5.35 us
    all_to_all x1, starting transfers between devices, local(): lax.all_to_all(partial.reshape(n_source, cap * directions), 'cell', split...  5.18 us
    unnamed x17, local copies, waits for them, and re-layouts  4.43 us
  transfers between devices with their start and end apart: 4, of which 3 were waited for; matrix products, arithmetic and copies ran while one was open for 7% of the time, Pallas kernels for 0%

profile of v1, /device:TPU:8, one launch (start us, length us, event | category | flops | bytes accessed | tf_op | source)
XLA Modules:
  0.0 123.0 jit_solution(5616337347978239559)
XLA Ops:
  7.2 0.8 copy.71
  8.2 0.7 iota_compare_fusion.10
  9.0 0.3 fusion.12
  9.4 0.8 copy.78
  10.2 0.8 copy.76
  11.1 3.3 %gather_fusion = s32[512]{0:T(512)S(1)} fusion(s32[128]{0:T(128)S(1)} %reshape_squeeze.3, s32[1024]{0:T(1024)S(1)} %pad_clamp_fusion), kind=kCustom, calls=%fused_computation | custom fusion | bytes 6144 | tf_op jit(solution)/shard_map/gather | solution.py:26
  14.6 1.4 %fusion.5 = f32[1,64,16]{2,0,1:T(1,128)S(1)} fusion(bf16[512,1,1]{0,1,2:T(2,128)(2,1)S(1)} %reshape.332, s32[64,16]{1,0:T(8,128)S(1)} %multiply_add_fusion, s32[512]{0:T(512)S(1)} %add_select_fusion.2), kind=kOutput, calls=%fused_computation.7 | convolution fusion | flops 1572864 | bytes 11264 | tf_op jit(solution)/shard_map/dot_general | solution.py:39
  16.1 0.5 fusion.8
  16.8 0.5 broadcast.232
  17.3 0.8 reduce.2
  18.1 1.0 reshape.343
  19.1 16.6 %all-to-all-start = ((bf16[64,2,1088]{2,1,0:T(2,128)(2,1)}), bf16[64,2,1088]{2,1,0:T(2,128)(2,1)S(1)}, u32[]{:S(2)}, u32[]{:S(2)}) async-start(bf16[64,2,1088]{2,1,0:T(2,128)(2,1)} %reshape.343), calls=%async_computation | async-start | bytes 589824 | tf_op jit(solution)/shard_map/all_to_all | solution.py:43
  35.7 0.6 fusion.26
  36.4 1.6 %copy.90 = f32[32,16,512]{2,1,0:T(8,128)} copy(f32[32,16,512]{2,0,1:T(8,128)S(1)} %fusion.26) | data formatting | bytes 2097152 | tf_op jit(solution)/shard_map/ts,skn->tkn/dot_general | solution.py:76
  38.2 12.5 %all-to-all-done = bf16[64,2,1088]{2,1,0:T(2,128)(2,1)S(1)} async-done(((bf16[64,2,1088]{2,1,0:T(2,128)(2,1)}), bf16[64,2,1088]{2,1,0:T(2,128)(2,1)S(1)}, u32[]{:S(2)}, u32[]{:S(2)}) %all-to-all-start) | async-done | bytes 278560 | tf_op jit(solution)/shard_map/all_to_all | solution.py:43
  50.6 0.3 reshape.344
  51.3 0.3 fusion.7
  51.6 0.2 copy.81
  51.8 0.9 all_to_all.27
  52.7 5.2 %all-to-all-start.1 = ((f32[64,1,256]{2,1,0:T(1,128)}), f32[64,1,256]{2,1,0:T(1,128)S(1)}, u32[]{:S(2)}, u32[]{:S(2)}) async-start(f32[64,1,256]{2,1,0:T(1,128)} %all_to_all.27), calls=%async_computation.1 | async-start | bytes 131072 | tf_op jit(solution)/shard_map/all_to_all | solution.py:52
  57.9 11.4 %all-to-all-done.1 = f32[64,1,256]{2,1,0:T(1,128)S(1)} async-done(((f32[64,1,256]{2,1,0:T(1,128)}), f32[64,1,256]{2,1,0:T(1,128)S(1)}, u32[]{:S(2)}, u32[]{:S(2)}) %all-to-all-start.1) | async-done | bytes 65568 | tf_op jit(solution)/shard_map/all_to_all | solution.py:52
  69.5 0.2 reshape.320
  69.7 1.1 fusion.9
  70.8 23.6 %psum.7 = f32[64,16]{1,0:T(8,128)S(1)} all-reduce(f32[64,16]{1,0:T(8,128)S(1)} %fusion.9), channel_id=1, replica_groups=mesh['cell'=64,'tm'=8] {'tm'}, use_global_device_ids=true, to_apply=%region_3.4 | all-reduce | flops 1024 | bytes 8192 | tf_op jit(solution)/shard_map/psum | solution.py:59
  94.5 1.0 fusion
  95.6 0.9 all_to_all.28
  96.4 5.3 %all-to-all-start.2 = ((f32[64,1,256]{2,1,0:T(1,128)}), f32[64,1,256]{2,1,0:T(1,128)S(1)}, u32[]{:S(2)}, u32[]{:S(2)}) async-start(f32[64,1,256]{2,1,0:T(1,128)} %all_to_all.28), calls=%async_computation.2 | async-start | bytes 131072 | tf_op jit(solution)/shard_map/all_to_all | solution.py:63
  101.9 0.7 copy.91
  102.6 10.7 %all-to-all-done.2 = f32[64,1,256]{2,1,0:T(1,128)S(1)} async-done(((f32[64,1,256]{2,1,0:T(1,128)}), f32[64,1,256]{2,1,0:T(1,128)S(1)}, u32[]{:S(2)}, u32[]{:S(2)}) %all-to-all-start.2) | async-done | bytes 65568 | tf_op jit(solution)/shard_map/all_to_all | solution.py:63
  113.4 0.2 mul.90
  113.9 0.6 convolution_bitcast_fusion
  114.6 1.6 %bitcast_add_fusion = f32[4,16,512]{2,1,0:T(8,128)} fusion(f32[4,16,512]{2,1,0:T(8,128)} %reduce-scatter.2.cloned.1.call-done, f32[4,4,2,8,128]{4,3,2,1,0:T(8,128)S(1)} %convolution_bitcast_fusion), kind=kLoop, calls=%fused_computation.27 | loop fusion | flops 32768 | bytes 393216 | tf_op jit(solution)/shard_map/add | solution.py:81
  (47 shorter events, 2.3 us)
Async XLA Ops:
  7.2 8.9 %copy-start = (bf16[64,8,128]{2,1,0:T(8,128)(2,1)S(1)}, bf16[64,8,128]{2,1,0:T(8,128)(2,1)}, u32[]{:S(2)}) copy-start(bf16[64,8,128]{2,1,0:T(8,128)(2,1)} %param.9) | copy-start | bytes 393220
  16.7 19.1 %copy-start.1 = (bf16[4,16,512]{2,1,0:T(8,128)(2,1)S(1)}, bf16[4,16,512]{2,1,0:T(8,128)(2,1)}, u32[]{:S(2)}) copy-start(bf16[4,16,512]{2,1,0:T(8,128)(2,1)} %param.8) | copy-start | bytes 196612
  16.7 19.1 %copy-start.2 = (f32[32,32]{1,0:T(8,128)S(1)}, f32[32,32]{1,0:T(8,128)}, u32[]{:S(2)}) copy-start(f32[32,32]{1,0:T(8,128)} %param.15) | copy-start | bytes 12292
  19.1 31.6 %all-to-all-start = ((bf16[64,2,1088]{2,1,0:T(2,128)(2,1)}), bf16[64,2,1088]{2,1,0:T(2,128)(2,1)S(1)}, u32[]{:S(2)}, u32[]{:S(2)}) async-start(bf16[64,2,1088]{2,1,0:T(2,128)(2,1)} %reshape.343), calls=%async_computation | async-start | bytes 589824 | tf_op jit(solution)/shard_map/all_to_all | solution.py:43
  35.7 78.9 %reduce-scatter.2.cloned.1.call-start = ((), (), s32[]{:S(2)}) async-start(), calls=%async_computation.4 | async-start | bytes 1179648 | tf_op jit(solution)/shard_map/reduce_scatter | solution.py:75
  51.3 6.6 %copy-start.3 = (s32[64,1]{0,1:T(1,128)S(1)}, s32[64,1]{0,1:T(1,128)}, u32[]{:S(2)}) copy-start(s32[64,1]{0,1:T(1,128)} %param.12) | copy-start | bytes 772
  52.7 41.8 %copy-start.4 = (f32[64]{0:T(128)S(1)}, f32[64]{0:T(128)}, u32[]{:S(2)}) copy-start(f32[64]{0:T(128)} %param.14) | copy-start | bytes 772
  52.7 16.7 %all-to-all-start.1 = ((f32[64,1,256]{2,1,0:T(1,128)}), f32[64,1,256]{2,1,0:T(1,128)S(1)}, u32[]{:S(2)}, u32[]{:S(2)}) async-start(f32[64,1,256]{2,1,0:T(1,128)} %all_to_all.27), calls=%async_computation.1 | async-start | bytes 131072 | tf_op jit(solution)/shard_map/all_to_all | solution.py:52
  96.4 16.9 %all-to-all-start.2 = ((f32[64,1,256]{2,1,0:T(1,128)}), f32[64,1,256]{2,1,0:T(1,128)S(1)}, u32[]{:S(2)}, u32[]{:S(2)}) async-start(f32[64,1,256]{2,1,0:T(1,128)} %all_to_all.28), calls=%async_computation.2 | async-start | bytes 131072 | tf_op jit(solution)/shard_map/all_to_all | solution.py:63
Sparse Core Ops, SparseCore 0:
  39.3 38.0 reduce-scatter.1

commit v2 on v1

--- a/solution.py
+++ b/solution.py
@@ -23,7 +23,9 @@
     slot_ids = block_slot.reshape(n_blocks)
     source = slot_ids // per_source
     position = slot_ids % per_source
-    local_tile = request_tiles[0].reshape(n_source * per_source)[source * per_source + position]
+    table = request_tiles[0].reshape(n_source * per_source)
+    pick = slot_ids[:, None] == jnp.arange(n_source * per_source, dtype=jnp.int32)[None, :]
+    local_tile = jnp.sum(jnp.where(pick, table[None, :], 0), axis=1)
     meta = local_tile * slices + block_time.reshape(n_blocks)
     src_hot = (source[:, None] == jnp.arange(n_source, dtype=jnp.int32)[None, :]) & live[:, None]
     src_hot_b = src_hot.astype(jnp.bfloat16)
@@ -70,14 +72,12 @@
     adjoint = adj.reshape(slices, directions, cell_count)
 
     my_group = lax.axis_index("tm")
-    flux_wide = flux.astype(f32)
-    panel = lax.dynamic_slice(prior, (0, my_group * slices), (lax.axis_size("tm") * slices, slices))
-    coupled = lax.psum_scatter(
-        jnp.einsum("ts,skn->tkn", panel, flux_wide, precision=HI),
-        "tm",
-        scatter_dimension=0,
-        tiled=True,
-    )
+    groups = lax.axis_size("tm")
+    copies = jnp.broadcast_to(flux[None], (groups,) + flux.shape)
+    flux_all = lax.all_to_all(copies, "tm", split_axis=0, concat_axis=0, tiled=True)
+    flux_all = flux_all.reshape(groups * slices, directions, cell_count).astype(f32)
+    panel = lax.dynamic_slice(prior, (my_group * slices, 0), (slices, groups * slices))
+    coupled = jnp.einsum("ts,skn->tkn", panel, flux_all, precision=HI)
     hess = adjoint + coupled
     return (images, hess)
 

time: 123 us -> 114 us (0.927)
  between operations: 14.4 us -> 1 us
  local copies, waits for them, and re-layouts: 13.6 us -> 9.41 us
  starting transfers between devices: 27.2 us -> 31.3 us
  blocking collectives: 23.6 us -> 27.1 us
  waiting for transfers between devices: 34.6 us -> 36.5 us
  other arithmetic: 3.75 us -> 2.39 us
    all_to_all x0 -> x1, starting transfers between devices: none -> 4.29 us  [local(): lax.all_to_all(copies, 'tm', split_axis=0, concat_axis=0, tiled=True)]
    psum x1, blocking collectives: 23.6 us -> 27.1 us  [local(): images = lax.psum(partial_value, 'tm')]
    gather x1 -> x0, local copies, waits for them, and re-layouts: 3.35 us -> none  [local(): request_tiles[0].reshape(n_source * per_source)]
    all_to_all x1, waiting for transfers between devices: 12.5 us -> 14.8 us  [local(): recv = lax.all_to_all(send, 'cell', split_axis=0, concat_axis=0, tiled=True)]
    dot_general x1 -> x0, local copies, waits for them, and re-layouts: 1.6 us -> none  [local(): jnp.einsum('ts,skn->tkn', panel, flux_wide, precision=HI)]
    add x1 -> x0, other arithmetic: 1.58 us -> none  [local(): hess = adjoint + coupled]
    unnamed x17 -> x21, local copies, waits for them, and re-layouts: 4.43 us -> 3.8 us
  transfers between devices with their start and end apart: 4 -> 4, of which waited for: 3 -> 3; matrix products, arithmetic and copies ran while one was open for 7% -> 4% of each run, Pallas kernels for 0% -> 0%
where the time goes in v2:
time: 114 us
  waiting for transfers between devices  36.5 us (32%)
  starting transfers between devices  31.3 us (27%)
  blocking collectives  27.1 us (24%)
  local copies, waits for them, and re-layouts  9.41 us (8%)
  matrix products  6.24 us (5%)
  other arithmetic  2.39 us (2%)
    psum x1, blocking collectives, local(): images = lax.psum(partial_value, 'tm')  27.1 us
    all_to_all x1, starting transfers between devices, local(): recv = lax.all_to_all(send, 'cell', split_axis=0, concat_axis=0, tiled=True)  16.6 us
    all_to_all x1, waiting for transfers between devices, local(): recv = lax.all_to_all(send, 'cell', split_axis=0, concat_axis=0, tiled=True)  14.8 us
    all_to_all x1, waiting for transfers between devices, local(): lax.all_to_all(partial.reshape(n_source, cap * directions), 'cell', split...  11.4 us
    all_to_all x1, waiting for transfers between devices, local(): lax.all_to_all(w_send.reshape(n_source, cap * directions), 'cell', split_...  10.3 us
    all_to_all x1, starting transfers between devices, local(): lax.all_to_all(w_send.reshape(n_source, cap * directions), 'cell', split_...  5.35 us
    all_to_all x1, starting transfers between devices, local(): lax.all_to_all(partial.reshape(n_source, cap * directions), 'cell', split...  5.05 us
    all_to_all x1, starting transfers between devices, local(): lax.all_to_all(copies, 'tm', split_axis=0, concat_axis=0, tiled=True)  4.29 us
  transfers between devices with their start and end apart: 4, of which 3 were waited for; matrix products, arithmetic and copies ran while one was open for 4% of the time, Pallas kernels for 0%

profile of v2, /device:TPU:8, one launch (start us, length us, event | category | flops | bytes accessed | tf_op | source)
XLA Modules:
  0.0 113.9 jit_solution(2561145646055867425)
XLA Ops:
  0.7 0.8 copy.87
  1.6 0.7 iota_compare_fusion.11
  2.4 0.3 fusion.12
  2.7 0.5 fusion.8
  3.6 0.2 select_reduce_fusion
  4.1 1.4 %fusion.5 = f32[1,64,16]{2,0,1:T(1,128)S(1)} fusion(bf16[512,1,1]{0,1,2:T(2,128)(2,1)S(1)} %reshape.237, s32[64,16]{1,0:T(8,128)S(1)} %multiply_add_fusion, s32[512]{0:T(512)S(1)} %add_select_fusion.2), kind=kOutput, calls=%fused_computation.6 | convolution fusion | flops 1572864 | bytes 11264 | tf_op jit(solution)/shard_map/dot_general | solution.py:41
  5.7 0.5 broadcast.141
  6.2 0.8 reduce.2
  6.9 1.0 reshape.249
  7.9 16.6 %all-to-all-start = ((bf16[64,2,1088]{2,1,0:T(2,128)(2,1)}), bf16[64,2,1088]{2,1,0:T(2,128)(2,1)S(1)}, u32[]{:S(2)}, u32[]{:S(2)}) async-start(bf16[64,2,1088]{2,1,0:T(2,128)(2,1)} %reshape.249), calls=%async_computation | async-start | bytes 589824 | tf_op jit(solution)/shard_map/all_to_all | solution.py:45
  24.7 14.8 %all-to-all-done = bf16[64,2,1088]{2,1,0:T(2,128)(2,1)S(1)} async-done(((bf16[64,2,1088]{2,1,0:T(2,128)(2,1)}), bf16[64,2,1088]{2,1,0:T(2,128)(2,1)S(1)}, u32[]{:S(2)}, u32[]{:S(2)}) %all-to-all-start) | async-done | bytes 278560 | tf_op jit(solution)/shard_map/all_to_all | solution.py:45
  39.5 0.3 reshape.250
  40.1 0.3 fusion.7
  40.4 0.2 copy.96
  40.6 0.9 all_to_all.31
  41.5 5.0 %all-to-all-start.1 = ((f32[64,1,256]{2,1,0:T(1,128)}), f32[64,1,256]{2,1,0:T(1,128)S(1)}, u32[]{:S(2)}, u32[]{:S(2)}) async-start(f32[64,1,256]{2,1,0:T(1,128)} %all_to_all.31), calls=%async_computation.1 | async-start | bytes 131072 | tf_op jit(solution)/shard_map/all_to_all | solution.py:54
  46.7 11.4 %all-to-all-done.1 = f32[64,1,256]{2,1,0:T(1,128)S(1)} async-done(((f32[64,1,256]{2,1,0:T(1,128)}), f32[64,1,256]{2,1,0:T(1,128)S(1)}, u32[]{:S(2)}, u32[]{:S(2)}) %all-to-all-start.1) | async-done | bytes 65568 | tf_op jit(solution)/shard_map/all_to_all | solution.py:54
  58.1 0.9 broadcast_in_dim.53
  59.0 4.3 %all-to-all-start.3 = ((bf16[8,4,16,512]{3,1,2,0:T(4,128)(2,1)}), bf16[8,4,16,512]{3,1,2,0:T(4,128)(2,1)S(1)}, u32[]{:S(2)}, u32[]{:S(2)}) async-start(bf16[8,4,16,512]{3,1,2,0:T(4,128)(2,1)} %broadcast_in_dim.53), calls=%async_computation.3 | async-start | bytes 1048576 | tf_op jit(solution)/shard_map/all_to_all | solution.py:77
  63.4 0.2 reshape.232
  63.6 1.1 fusion.9
  64.8 27.1 %psum.7 = f32[64,16]{1,0:T(8,128)S(1)} all-reduce(f32[64,16]{1,0:T(8,128)S(1)} %fusion.9), channel_id=1, replica_groups=mesh['cell'=64,'tm'=8] {'tm'}, use_global_device_ids=true, to_apply=%region_4.5 | all-reduce | flops 1024 | bytes 8192 | tf_op jit(solution)/shard_map/psum | solution.py:61
  92.0 1.0 fusion
  93.0 0.9 all_to_all.32
  93.9 5.3 %all-to-all-start.2 = ((f32[64,1,256]{2,1,0:T(1,128)}), f32[64,1,256]{2,1,0:T(1,128)S(1)}, u32[]{:S(2)}, u32[]{:S(2)}) async-start(f32[64,1,256]{2,1,0:T(1,128)} %all_to_all.32), calls=%async_computation.2 | async-start | bytes 131072 | tf_op jit(solution)/shard_map/all_to_all | solution.py:65
  99.2 0.2 copy.104
  99.7 0.7 copy.106
  100.4 10.3 %all-to-all-done.2 = f32[64,1,256]{2,1,0:T(1,128)S(1)} async-done(((f32[64,1,256]{2,1,0:T(1,128)}), f32[64,1,256]{2,1,0:T(1,128)S(1)}, u32[]{:S(2)}, u32[]{:S(2)}) %all-to-all-start.2) | async-done | bytes 65568 | tf_op jit(solution)/shard_map/all_to_all | solution.py:65
  110.9 0.2 mul.78
  111.4 0.6 convolution_bitcast_fusion
  112.2 1.0 convolution_add_fusion
  113.2 0.7 copy.107
  (50 shorter events, 2.6 us)
Async XLA Ops:
  0.6 2.1 %copy-start = (bf16[64,8,128]{2,1,0:T(8,128)(2,1)S(1)}, bf16[64,8,128]{2,1,0:T(8,128)(2,1)}, u32[]{:S(2)}) copy-start(bf16[64,8,128]{2,1,0:T(8,128)(2,1)} %param.9) | copy-start | bytes 393220
  1.5 1.9 %copy-start.4 = (s32[1,64,2]{1,2,0:T(2,128)S(1)}, s32[1,64,2]{1,2,0:T(2,128)}, u32[]{:S(2)}) copy-start(s32[1,64,2]{1,2,0:T(2,128)} %param.13) | copy-start | bytes 1540
  2.4 1.5 %copy-start.2 = (s32[64,8]{0,1:T(8,128)S(1)}, s32[64,8]{0,1:T(8,128)}, u32[]{:S(2)}) copy-start(s32[64,8]{0,1:T(8,128)} %param.11) | copy-start | bytes 6148
  5.5 19.0 %copy-start.1 = (bf16[4,16,512]{2,1,0:T(8,128)(2,1)S(1)}, bf16[4,16,512]{2,1,0:T(8,128)(2,1)}, u32[]{:S(2)}) copy-start(bf16[4,16,512]{2,1,0:T(8,128)(2,1)} %param.8) | copy-start | bytes 196612
  7.9 31.6 %all-to-all-start = ((bf16[64,2,1088]{2,1,0:T(2,128)(2,1)}), bf16[64,2,1088]{2,1,0:T(2,128)(2,1)S(1)}, u32[]{:S(2)}, u32[]{:S(2)}) async-start(bf16[64,2,1088]{2,1,0:T(2,128)(2,1)} %reshape.249), calls=%async_computation | async-start | bytes 589824 | tf_op jit(solution)/shard_map/all_to_all | solution.py:45
  40.1 6.4 %copy-start.3 = (s32[64,1]{0,1:T(1,128)S(1)}, s32[64,1]{0,1:T(1,128)}, u32[]{:S(2)}) copy-start(s32[64,1]{0,1:T(1,128)} %param.12) | copy-start | bytes 772
  41.5 16.5 %all-to-all-start.1 = ((f32[64,1,256]{2,1,0:T(1,128)}), f32[64,1,256]{2,1,0:T(1,128)S(1)}, u32[]{:S(2)}, u32[]{:S(2)}) async-start(f32[64,1,256]{2,1,0:T(1,128)} %all_to_all.31), calls=%async_computation.1 | async-start | bytes 131072 | tf_op jit(solution)/shard_map/all_to_all | solution.py:54
  59.0 34.9 %all-to-all-start.3 = ((bf16[8,4,16,512]{3,1,2,0:T(4,128)(2,1)}), bf16[8,4,16,512]{3,1,2,0:T(4,128)(2,1)S(1)}, u32[]{:S(2)}, u32[]{:S(2)}) async-start(bf16[8,4,16,512]{3,1,2,0:T(4,128)(2,1)} %broadcast_in_dim.53), calls=%async_computation.3 | async-start | bytes 1048576 | tf_op jit(solution)/shard_map/all_to_all | solution.py:77
  63.3 28.6 %copy-start.5 = (f32[64]{0:T(128)S(1)}, f32[64]{0:T(128)}, u32[]{:S(2)}) copy-start(f32[64]{0:T(128)} %param.14) | copy-start | bytes 772
  93.9 16.9 %all-to-all-start.2 = ((f32[64,1,256]{2,1,0:T(1,128)}), f32[64,1,256]{2,1,0:T(1,128)S(1)}, u32[]{:S(2)}, u32[]{:S(2)}) async-start(f32[64,1,256]{2,1,0:T(1,128)} %all_to_all.32), calls=%async_computation.2 | async-start | bytes 131072 | tf_op jit(solution)/shard_map/all_to_all | solution.py:65

commit v3 on v2

--- a/solution.py
+++ b/solution.py
@@ -44,6 +44,12 @@
     send = jnp.concatenate([foot_send.reshape(n_source, cap * TILE), meta_send, meta_pad], axis=1)
     recv = lax.all_to_all(send, "cell", split_axis=0, concat_axis=0, tiled=True)
 
+    my_group = lax.axis_index("tm")
+    groups = lax.axis_size("tm")
+    copies = jnp.broadcast_to(flux[None], (groups,) + flux.shape)
+    flux_all = lax.all_to_all(copies, "tm", split_axis=0, concat_axis=0, tiled=True)
+    flux_all = flux_all.reshape(groups * slices, directions, cell_count).astype(f32)
+
     foot_r = recv[:, : cap * TILE].reshape(n_slot, TILE)
     meta_r = recv[:, cap * TILE : cap * TILE + cap].reshape(n_slot).astype(jnp.int32)
     meta_hot = (meta_r[:, None] == jnp.arange(n_meta, dtype=jnp.int32)[None, :]).astype(f32)
@@ -51,6 +57,7 @@
     panels = panels.reshape(TILE, n_meta * directions)
     every = jnp.dot(foot_r, panels, preferred_element_type=f32).reshape(n_slot, n_meta, directions)
     partial = jnp.sum(every * meta_hot[:, :, None], axis=1)
+    flux_all, partial = lax.optimization_barrier((flux_all, partial))
     back = lax.all_to_all(
         partial.reshape(n_source, cap * directions), "cell", split_axis=0, concat_axis=0, tiled=True
     ).reshape(n_slot, directions)
@@ -71,11 +78,6 @@
     adj = adj.reshape(tiles, slices, directions, TILE).transpose(1, 2, 0, 3)
     adjoint = adj.reshape(slices, directions, cell_count)
 
-    my_group = lax.axis_index("tm")
-    groups = lax.axis_size("tm")
-    copies = jnp.broadcast_to(flux[None], (groups,) + flux.shape)
-    flux_all = lax.all_to_all(copies, "tm", split_axis=0, concat_axis=0, tiled=True)
-    flux_all = flux_all.reshape(groups * slices, directions, cell_count).astype(f32)
     panel = lax.dynamic_slice(prior, (my_group * slices, 0), (slices, groups * slices))
     coupled = jnp.einsum("ts,skn->tkn", panel, flux_all, precision=HI)
     hess = adjoint + coupled

time: 114 us -> 116 us (1.018)
  waiting for transfers between devices: 36.5 us -> 40.9 us
  blocking collectives: 27.1 us -> 23.6 us
    all_to_all x1, waiting for transfers between devices: 0.01 us -> 4.44 us  [local(): lax.all_to_all(copies, 'tm', split_axis=0, concat_axis=0, tiled=True)]
    psum x1, blocking collectives: 27.1 us -> 23.6 us  [local(): images = lax.psum(partial_value, 'tm')]
    unnamed x21 -> x23, local copies, waits for them, and re-layouts: 3.8 us -> 3.95 us
  transfers between devices with their start and end apart: 4 -> 4, of which waited for: 3 -> 4; matrix products, arithmetic and copies ran while one was open for 4% -> 6% of each run, Pallas kernels for 0% -> 0%
where the time goes in v3:
time: 116 us; the launch traced here: 115 us
  waiting for transfers between devices  40.9 us (35%)
  starting transfers between devices  31.5 us (27%)
  blocking collectives  23.6 us (20%)
  local copies, waits for them, and re-layouts  9.31 us (8%)
  matrix products  7.1 us (6%)
  other arithmetic  1.88 us (2%)
    psum x1, blocking collectives, local(): images = lax.psum(partial_value, 'tm')  23.6 us
    all_to_all x1, starting transfers between devices, local(): recv = lax.all_to_all(send, 'cell', split_axis=0, concat_axis=0, tiled=True)  16.6 us
    all_to_all x1, waiting for transfers between devices, local(): recv = lax.all_to_all(send, 'cell', split_axis=0, concat_axis=0, tiled=True)  14.3 us
    all_to_all x1, waiting for transfers between devices, local(): lax.all_to_all(partial.reshape(n_source, cap * directions), 'cell', split...  11.4 us
    all_to_all x1, waiting for transfers between devices, local(): lax.all_to_all(w_send.reshape(n_source, cap * directions), 'cell', split_...  10.7 us
    all_to_all x1, starting transfers between devices, local(): lax.all_to_all(w_send.reshape(n_source, cap * directions), 'cell', split_...  5.35 us
    all_to_all x1, starting transfers between devices, local(): lax.all_to_all(partial.reshape(n_source, cap * directions), 'cell', split...  5.22 us
    all_to_all x1, waiting for transfers between devices, local(): lax.all_to_all(copies, 'tm', split_axis=0, concat_axis=0, tiled=True)  4.44 us
  transfers between devices with their start and end apart: 4, of which 4 were waited for; matrix products, arithmetic and copies ran while one was open for 6% of the time, Pallas kernels for 0%

profile of v3, /device:TPU:8, one launch (start us, length us, event | category | flops | bytes accessed | tf_op | source)
XLA Modules:
  0.0 115.2 jit_solution(13881612199264638160)
XLA Ops:
  0.7 0.9 copy.92
  1.6 0.9 broadcast_in_dim.27
  2.5 4.3 %all-to-all-start = ((bf16[8,4,16,512]{3,1,2,0:T(4,128)(2,1)}), bf16[8,4,16,512]{3,1,2,0:T(4,128)(2,1)S(1)}, u32[]{:S(2)}, u32[]{:S(2)}) async-start(bf16[8,4,16,512]{3,1,2,0:T(4,128)(2,1)} %broadcast_in_dim.27), calls=%async_computation | async-start | bytes 1048576 | tf_op jit(solution)/shard_map/all_to_all | solution.py:50
  7.2 0.3 fusion.12
  7.9 0.2 select_reduce_fusion
  8.3 1.4 %fusion.5 = f32[1,64,16]{2,0,1:T(1,128)S(1)} fusion(bf16[512,1,1]{0,1,2:T(2,128)(2,1)S(1)} %reshape.237, s32[64,16]{1,0:T(8,128)S(1)} %multiply_add_fusion, s32[512]{0:T(512)S(1)} %add_select_fusion.2), kind=kOutput, calls=%fused_computation.6 | convolution fusion | flops 1572864 | bytes 11264 | tf_op jit(solution)/shard_map/dot_general | solution.py:41
  9.8 0.5 fusion.8
  10.5 0.5 broadcast.141
  11.0 0.8 reduce.2
  11.8 1.0 reshape.249
  12.8 4.4 %all-to-all-done = bf16[8,4,16,512]{3,1,2,0:T(4,128)(2,1)S(1)} async-done(((bf16[8,4,16,512]{3,1,2,0:T(4,128)(2,1)}), bf16[8,4,16,512]{3,1,2,0:T(4,128)(2,1)S(1)}, u32[]{:S(2)}, u32[]{:S(2)}) %all-to-all-start) | async-done | bytes 524320 | tf_op jit(solution)/shard_map/all_to_all | solution.py:50
  17.2 16.6 %all-to-all-start.1 = ((bf16[64,2,1088]{2,1,0:T(2,128)(2,1)}), bf16[64,2,1088]{2,1,0:T(2,128)(2,1)S(1)}, u32[]{:S(2)}, u32[]{:S(2)}) async-start(bf16[64,2,1088]{2,1,0:T(2,128)(2,1)} %reshape.249), calls=%async_computation.1 | async-start | bytes 589824 | tf_op jit(solution)/shard_map/all_to_all | solution.py:45
  34.2 14.3 %all-to-all-done.1 = bf16[64,2,1088]{2,1,0:T(2,128)(2,1)S(1)} async-done(((bf16[64,2,1088]{2,1,0:T(2,128)(2,1)}), bf16[64,2,1088]{2,1,0:T(2,128)(2,1)S(1)}, u32[]{:S(2)}, u32[]{:S(2)}) %all-to-all-start.1) | async-done | bytes 278560 | tf_op jit(solution)/shard_map/all_to_all | solution.py:45
  48.6 0.3 reshape.250
  49.2 0.3 fusion.7
  49.5 0.2 copy.98
  49.7 0.9 all_to_all.31
  50.6 5.2 %all-to-all-start.2 = ((f32[64,1,256]{2,1,0:T(1,128)}), f32[64,1,256]{2,1,0:T(1,128)S(1)}, u32[]{:S(2)}, u32[]{:S(2)}) async-start(f32[64,1,256]{2,1,0:T(1,128)} %all_to_all.31), calls=%async_computation.2 | async-start | bytes 131072 | tf_op jit(solution)/shard_map/all_to_all | solution.py:61
  55.9 11.4 %all-to-all-done.2 = f32[64,1,256]{2,1,0:T(1,128)S(1)} async-done(((f32[64,1,256]{2,1,0:T(1,128)}), f32[64,1,256]{2,1,0:T(1,128)S(1)}, u32[]{:S(2)}, u32[]{:S(2)}) %all-to-all-start.2) | async-done | bytes 65568 | tf_op jit(solution)/shard_map/all_to_all | solution.py:61
  67.5 0.2 reshape.232
  67.7 1.1 fusion.9
  68.8 23.6 %psum.7 = f32[64,16]{1,0:T(8,128)S(1)} all-reduce(f32[64,16]{1,0:T(8,128)S(1)} %fusion.9), channel_id=1, replica_groups=mesh['cell'=64,'tm'=8] {'tm'}, use_global_device_ids=true, to_apply=%region_4.5 | all-reduce | flops 1024 | bytes 8192 | tf_op jit(solution)/shard_map/psum | solution.py:68
  92.5 1.0 fusion
  93.5 0.9 all_to_all.32
  94.4 5.4 %all-to-all-start.3 = ((f32[64,1,256]{2,1,0:T(1,128)}), f32[64,1,256]{2,1,0:T(1,128)S(1)}, u32[]{:S(2)}, u32[]{:S(2)}) async-start(f32[64,1,256]{2,1,0:T(1,128)} %all_to_all.32), calls=%async_computation.3 | async-start | bytes 131072 | tf_op jit(solution)/shard_map/all_to_all | solution.py:72
  99.9 0.7 copy.107
  100.5 10.7 %all-to-all-done.3 = f32[64,1,256]{2,1,0:T(1,128)S(1)} async-done(((f32[64,1,256]{2,1,0:T(1,128)}), f32[64,1,256]{2,1,0:T(1,128)S(1)}, u32[]{:S(2)}, u32[]{:S(2)}) %all-to-all-start.3) | async-done | bytes 65568 | tf_op jit(solution)/shard_map/all_to_all | solution.py:72
  111.4 0.2 mul.78
  111.6 0.2 copy.103
  111.9 0.6 convolution_bitcast_fusion
  112.7 1.9 %convolution_add_fusion = f32[4,16,512]{2,0,1:T(4,128)S(1)} fusion(f32[4,16,512]{2,0,1:T(4,128)S(1)} %reshape.246, f32[32,16,512]{2,1,0:T(8,128)S(1)} %bitcast_convert_fusion, f32[32,32]{1,0:T(8,128)} %param.15, s32[]{:T(128)S(6)} %select_n.39), kind=kOutput, calls=%fused_computation.14 | convolution fusion | flops 12615680 | bytes 1312772 | tf_op jit(solution)/shard_map/ts,skn->tkn/dot_general | solution.py:82
  114.5 0.7 copy.108
  (52 shorter events, 2.7 us)
Async XLA Ops:
  0.6 9.1 %copy-start = (bf16[64,8,128]{2,1,0:T(8,128)(2,1)S(1)}, bf16[64,8,128]{2,1,0:T(8,128)(2,1)}, u32[]{:S(2)}) copy-start(bf16[64,8,128]{2,1,0:T(8,128)(2,1)} %param.9) | copy-start | bytes 393220
  0.6 6.2 %copy-start.4 = (s32[64,1]{0,1:T(1,128)S(1)}, s32[64,1]{0,1:T(1,128)}, u32[]{:S(2)}) copy-start(s32[64,1]{0,1:T(1,128)} %param.12) | copy-start | bytes 772
  0.7 6.4 %copy-start.2 = (s32[64,8]{0,1:T(8,128)S(1)}, s32[64,8]{0,1:T(8,128)}, u32[]{:S(2)}) copy-start(s32[64,8]{0,1:T(8,128)} %param.10) | copy-start | bytes 6148
  1.6 6.0 %copy-start.3 = (s32[64,8]{0,1:T(8,128)S(1)}, s32[64,8]{0,1:T(8,128)}, u32[]{:S(2)}) copy-start(s32[64,8]{0,1:T(8,128)} %param.11) | copy-start | bytes 6148
  1.6 6.0 %copy-start.5 = (s32[1,64,2]{1,2,0:T(2,128)S(1)}, s32[1,64,2]{1,2,0:T(2,128)}, u32[]{:S(2)}) copy-start(s32[1,64,2]{1,2,0:T(2,128)} %param.13) | copy-start | bytes 1540
  2.5 14.6 %all-to-all-start = ((bf16[8,4,16,512]{3,1,2,0:T(4,128)(2,1)}), bf16[8,4,16,512]{3,1,2,0:T(4,128)(2,1)S(1)}, u32[]{:S(2)}, u32[]{:S(2)}) async-start(bf16[8,4,16,512]{3,1,2,0:T(4,128)(2,1)} %broadcast_in_dim.27), calls=%async_computation | async-start | bytes 1048576 | tf_op jit(solution)/shard_map/all_to_all | solution.py:50
  10.4 23.4 %copy-start.1 = (bf16[4,16,512]{2,1,0:T(8,128)(2,1)S(1)}, bf16[4,16,512]{2,1,0:T(8,128)(2,1)}, u32[]{:S(2)}) copy-start(bf16[4,16,512]{2,1,0:T(8,128)(2,1)} %param.8) | copy-start | bytes 196612
  17.2 31.4 %all-to-all-start.1 = ((bf16[64,2,1088]{2,1,0:T(2,128)(2,1)}), bf16[64,2,1088]{2,1,0:T(2,128)(2,1)S(1)}, u32[]{:S(2)}, u32[]{:S(2)}) async-start(bf16[64,2,1088]{2,1,0:T(2,128)(2,1)} %reshape.249), calls=%async_computation.1 | async-start | bytes 589824 | tf_op jit(solution)/shard_map/all_to_all | solution.py:45
  50.6 41.8 %copy-start.6 = (f32[64]{0:T(128)S(1)}, f32[64]{0:T(128)}, u32[]{:S(2)}) copy-start(f32[64]{0:T(128)} %param.14) | copy-start | bytes 772
  50.6 16.7 %all-to-all-start.2 = ((f32[64,1,256]{2,1,0:T(1,128)}), f32[64,1,256]{2,1,0:T(1,128)S(1)}, u32[]{:S(2)}, u32[]{:S(2)}) async-start(f32[64,1,256]{2,1,0:T(1,128)} %all_to_all.31), calls=%async_computation.2 | async-start | bytes 131072 | tf_op jit(solution)/shard_map/all_to_all | solution.py:61
  94.4 16.8 %all-to-all-start.3 = ((f32[64,1,256]{2,1,0:T(1,128)}), f32[64,1,256]{2,1,0:T(1,128)S(1)}, u32[]{:S(2)}, u32[]{:S(2)}) async-start(f32[64,1,256]{2,1,0:T(1,128)} %all_to_all.32), calls=%async_computation.3 | async-start | bytes 131072 | tf_op jit(solution)/shard_map/all_to_all | solution.py:72

commit v4 on v3

--- a/solution.py
+++ b/solution.py
@@ -65,7 +65,8 @@
     place_f = place.astype(f32)
     per_block = jnp.dot(place_f.T, back, precision=HI, preferred_element_type=f32)
     partial_value = per_block.reshape(sounds, nb, directions).sum(axis=1)
-    images = lax.psum(partial_value, "tm")
+    stack = jnp.broadcast_to(partial_value[None], (groups,) + partial_value.shape)
+    images = lax.all_to_all(stack, "tm", split_axis=0, concat_axis=0, tiled=True).sum(axis=0)
     weighted = obs_weight[:, None] * images
     w_block = jnp.repeat(weighted, nb, axis=0)
     w_send = jnp.dot(place_f, w_block, precision=HI, preferred_element_type=f32)

time: 116 us -> 102 us (0.88)
  the two profiles are of different devices: /device:TPU:8 before, /device:TPU:1 now
where the time goes in v4:
time: 102 us; the launch traced here: 101 us
  waiting for transfers between devices  38.1 us (37%)
  starting transfers between devices  32.7 us (32%)
  blocking collectives  10.4 us (10%)
  local copies, waits for them, and re-layouts  9.5 us (9%)
  matrix products  7.09 us (7%)
  other arithmetic  2.55 us (2%)
  between operations  1.06 us (1%)
    all_to_all x1, waiting for transfers between devices, local(): recv = lax.all_to_all(send, 'cell', split_axis=0, concat_axis=0, tiled=True)  12.7 us
    all_to_all x1, starting transfers between devices, local(): recv = lax.all_to_all(send, 'cell', split_axis=0, concat_axis=0, tiled=True)  11.8 us
    all_to_all x1, waiting for transfers between devices, local(): lax.all_to_all(partial.reshape(n_source, cap * directions), 'cell', split...  11 us
    all_to_all x1, waiting for transfers between devices, local(): lax.all_to_all(w_send.reshape(n_source, cap * directions), 'cell', split_...  10.8 us
    all_to_all x1, blocking collectives, local(): lax.all_to_all(stack, 'tm', split_axis=0, concat_axis=0, tiled=True)  10.4 us
    all_to_all x1, starting transfers between devices, local(): lax.all_to_all(copies, 'tm', split_axis=0, concat_axis=0, tiled=True)  10.3 us
    all_to_all x1, starting transfers between devices, local(): lax.all_to_all(partial.reshape(n_source, cap * directions), 'cell', split...  5.83 us
    all_to_all x1, starting transfers between devices, local(): lax.all_to_all(w_send.reshape(n_source, cap * directions), 'cell', split_...  4.8 us
  transfers between devices with their start and end apart: 4, of which 4 were waited for; matrix products, arithmetic and copies ran while one was open for 6% of the time, Pallas kernels for 0%

profile of v4, /device:TPU:1, one launch (start us, length us, event | category | flops | bytes accessed | tf_op | source)
XLA Modules:
  0.0 101.4 jit_solution(1207941638402757993)
XLA Ops:
  0.7 0.9 copy.115
  1.6 0.9 broadcast_in_dim.29
  2.5 10.3 %all-to-all-start = ((bf16[8,4,16,512]{3,1,2,0:T(4,128)(2,1)}), bf16[8,4,16,512]{3,1,2,0:T(4,128)(2,1)S(1)}, u32[]{:S(2)}, u32[]{:S(2)}) async-start(bf16[8,4,16,512]{3,1,2,0:T(4,128)(2,1)} %broadcast_in_dim.29), calls=%async_computation | async-start | bytes 1048576 | tf_op jit(solution)/shard_map/all_to_all | solution.py:50
  13.2 0.3 fusion.12
  13.9 0.2 select_reduce_fusion
  14.3 1.4 %fusion.5 = f32[1,64,16]{2,0,1:T(1,128)S(1)} fusion(bf16[512,1,1]{0,1,2:T(2,128)(2,1)S(1)} %reshape.238, s32[64,16]{1,0:T(8,128)S(1)} %multiply_add_fusion, s32[512]{0:T(512)S(1)} %add_select_fusion.2), kind=kOutput, calls=%fused_computation.6 | convolution fusion | flops 1572864 | bytes 11264 | tf_op jit(solution)/shard_map/dot_general | solution.py:41
  15.7 0.5 fusion.8
  16.4 0.5 broadcast.142
  17.0 0.8 reduce.2
  17.7 1.0 reshape.250
  18.7 3.6 %all-to-all-done = bf16[8,4,16,512]{3,1,2,0:T(4,128)(2,1)S(1)} async-done(((bf16[8,4,16,512]{3,1,2,0:T(4,128)(2,1)}), bf16[8,4,16,512]{3,1,2,0:T(4,128)(2,1)S(1)}, u32[]{:S(2)}, u32[]{:S(2)}) %all-to-all-start) | async-done | bytes 524320 | tf_op jit(solution)/shard_map/all_to_all | solution.py:50
  22.3 11.8 %all-to-all-start.1 = ((bf16[64,2,1088]{2,1,0:T(2,128)(2,1)}), bf16[64,2,1088]{2,1,0:T(2,128)(2,1)S(1)}, u32[]{:S(2)}, u32[]{:S(2)}) async-start(bf16[64,2,1088]{2,1,0:T(2,128)(2,1)} %reshape.250), calls=%async_computation.1 | async-start | bytes 589824 | tf_op jit(solution)/shard_map/all_to_all | solution.py:45
  34.6 12.7 %all-to-all-done.1 = bf16[64,2,1088]{2,1,0:T(2,128)(2,1)S(1)} async-done(((bf16[64,2,1088]{2,1,0:T(2,128)(2,1)}), bf16[64,2,1088]{2,1,0:T(2,128)(2,1)S(1)}, u32[]{:S(2)}, u32[]{:S(2)}) %all-to-all-start.1) | async-done | bytes 278560 | tf_op jit(solution)/shard_map/all_to_all | solution.py:45
  47.3 0.3 reshape.251
  47.9 0.3 fusion.7
  48.2 0.2 copy.121
  48.4 0.9 all_to_all.35
  49.3 5.8 %all-to-all-start.2 = ((f32[64,1,256]{2,1,0:T(1,128)}), f32[64,1,256]{2,1,0:T(1,128)S(1)}, u32[]{:S(2)}, u32[]{:S(2)}) async-start(f32[64,1,256]{2,1,0:T(1,128)} %all_to_all.35), calls=%async_computation.2 | async-start | bytes 131072 | tf_op jit(solution)/shard_map/all_to_all | solution.py:61
  55.2 11.0 %all-to-all-done.2 = f32[64,1,256]{2,1,0:T(1,128)S(1)} async-done(((f32[64,1,256]{2,1,0:T(1,128)}), f32[64,1,256]{2,1,0:T(1,128)S(1)}, u32[]{:S(2)}, u32[]{:S(2)}) %all-to-all-start.2) | async-done | bytes 65568 | tf_op jit(solution)/shard_map/all_to_all | solution.py:61
  66.4 0.2 reshape.233
  66.6 1.1 %fusion.9 = f32[64,16]{1,0:T(8,128)S(1)} fusion(s32[64,8]{1,0:T(8,128)S(1)} %fusion.33, f32[1024,16]{1,0:T(8,128)S(1)} %reshape.233), kind=kOutput, calls=%fused_computation.11 | convolution fusion | flops 101194752 | bytes 71680 | tf_op jit(solution)/shard_map/dot_general | solution.py:66
  67.9 10.4 %all_to_all.42 = f32[8,1,1024]{2,1,0:T(1,128)S(1)} all-to-all(f32[8,1,1024]{2,1,0:T(1,128)S(1)} %reshape.252), channel_id=1, replica_groups=mesh['cell'=64,'tm'=8] {'tm'}, dimensions={0} | all-to-all | bytes 65536 | tf_op jit(solution)/shard_map/all_to_all | solution.py:69
  78.3 0.5 broadcast.143
  78.8 0.7 reduce.3
  79.7 1.0 %fusion = f32[1024,16]{1,0:T(8,128)S(1)} fusion(s32[512]{0:T(512)S(1)} %add_select_fusion.2, f32[64,16]{1,0:T(8,128)S(1)} %copy.125), kind=kOutput, calls=%fused_computation.1 | convolution fusion | flops 101187584 | bytes 71680 | tf_op jit(solution)/shard_map/dot_general | solution.py:72
  80.8 0.9 all_to_all.36
  81.6 4.8 %all-to-all-start.4 = ((f32[64,1,256]{2,1,0:T(1,128)}), f32[64,1,256]{2,1,0:T(1,128)S(1)}, u32[]{:S(2)}, u32[]{:S(2)}) async-start(f32[64,1,256]{2,1,0:T(1,128)} %all_to_all.36), calls=%async_computation.4 | async-start | bytes 131072 | tf_op jit(solution)/shard_map/all_to_all | solution.py:73
  86.6 10.8 %all-to-all-done.4 = f32[64,1,256]{2,1,0:T(1,128)S(1)} async-done(((f32[64,1,256]{2,1,0:T(1,128)}), f32[64,1,256]{2,1,0:T(1,128)S(1)}, u32[]{:S(2)}, u32[]{:S(2)}) %all-to-all-start.4) | async-done | bytes 65568 | tf_op jit(solution)/shard_map/all_to_all | solution.py:73
  97.6 0.2 mul.78
  98.1 0.6 convolution_bitcast_fusion
  98.9 1.9 %convolution_add_fusion = f32[4,16,512]{2,0,1:T(4,128)S(1)} fusion(f32[4,16,512]{2,0,1:T(4,128)S(1)} %reshape.247, f32[32,16,512]{2,1,0:T(8,128)S(1)} %bitcast_convert_fusion, f32[32,32]{1,0:T(8,128)} %param.15, s32[]{:T(128)S(6)} %select_n.39), kind=kOutput, calls=%fused_computation.14 | convolution fusion | flops 12615680 | bytes 1312772 | tf_op jit(solution)/shard_map/ts,skn->tkn/dot_general | solution.py:83
  100.7 0.7 copy.132
  (61 shorter events, 3.2 us)
Async XLA Ops:
  0.6 15.1 %copy-start = (bf16[64,8,128]{2,1,0:T(8,128)(2,1)S(1)}, bf16[64,8,128]{2,1,0:T(8,128)(2,1)}, u32[]{:S(2)}) copy-start(bf16[64,8,128]{2,1,0:T(8,128)(2,1)} %param.9) | copy-start | bytes 393220
  0.6 12.2 %copy-start.5 = (s32[64,1]{0,1:T(1,128)S(1)}, s32[64,1]{0,1:T(1,128)}, u32[]{:S(2)}) copy-start(s32[64,1]{0,1:T(1,128)} %param.12) | copy-start | bytes 772
  0.7 12.4 %copy-start.3 = (s32[64,8]{0,1:T(8,128)S(1)}, s32[64,8]{0,1:T(8,128)}, u32[]{:S(2)}) copy-start(s32[64,8]{0,1:T(8,128)} %param.10) | copy-start | bytes 6148
  1.6 11.9 %copy-start.4 = (s32[64,8]{0,1:T(8,128)S(1)}, s32[64,8]{0,1:T(8,128)}, u32[]{:S(2)}) copy-start(s32[64,8]{0,1:T(8,128)} %param.11) | copy-start | bytes 6148
  1.6 12.0 %copy-start.6 = (s32[1,64,2]{1,2,0:T(2,128)S(1)}, s32[1,64,2]{1,2,0:T(2,128)}, u32[]{:S(2)}) copy-start(s32[1,64,2]{1,2,0:T(2,128)} %param.13) | copy-start | bytes 1540
  2.5 19.8 %all-to-all-start = ((bf16[8,4,16,512]{3,1,2,0:T(4,128)(2,1)}), bf16[8,4,16,512]{3,1,2,0:T(4,128)(2,1)S(1)}, u32[]{:S(2)}, u32[]{:S(2)}) async-start(bf16[8,4,16,512]{3,1,2,0:T(4,128)(2,1)} %broadcast_in_dim.29), calls=%async_computation | async-start | bytes 1048576 | tf_op jit(solution)/shard_map/all_to_all | solution.py:50
  16.3 17.8 %copy-start.1 = (bf16[4,16,512]{2,1,0:T(8,128)(2,1)S(1)}, bf16[4,16,512]{2,1,0:T(8,128)(2,1)}, u32[]{:S(2)}) copy-start(bf16[4,16,512]{2,1,0:T(8,128)(2,1)} %param.8) | copy-start | bytes 196612
  22.3 25.0 %all-to-all-start.1 = ((bf16[64,2,1088]{2,1,0:T(2,128)(2,1)}), bf16[64,2,1088]{2,1,0:T(2,128)(2,1)S(1)}, u32[]{:S(2)}, u32[]{:S(2)}) async-start(bf16[64,2,1088]{2,1,0:T(2,128)(2,1)} %reshape.250), calls=%async_computation.1 | async-start | bytes 589824 | tf_op jit(solution)/shard_map/all_to_all | solution.py:45
  49.3 16.9 %all-to-all-start.2 = ((f32[64,1,256]{2,1,0:T(1,128)}), f32[64,1,256]{2,1,0:T(1,128)S(1)}, u32[]{:S(2)}, u32[]{:S(2)}) async-start(f32[64,1,256]{2,1,0:T(1,128)} %all_to_all.35), calls=%async_computation.2 | async-start | bytes 131072 | tf_op jit(solution)/shard_map/all_to_all | solution.py:61
  66.4 13.3 %copy-start.7 = (f32[64]{0:T(128)S(1)}, f32[64]{0:T(128)}, u32[]{:S(2)}) copy-start(f32[64]{0:T(128)} %param.14) | copy-start | bytes 772
  79.6 7.0 %copy-start.2 = (f32[64,16]{0,1:T(8,128)}, f32[64,16]{0,1:T(8,128)S(1)}, u32[]{:S(2)}) copy-start(f32[64,16]{0,1:T(8,128)S(1)} %bitcast_reduce_fusion) | copy-start | bytes 12292
  81.6 15.8 %all-to-all-start.4 = ((f32[64,1,256]{2,1,0:T(1,128)}), f32[64,1,256]{2,1,0:T(1,128)S(1)}, u32[]{:S(2)}, u32[]{:S(2)}) async-start(f32[64,1,256]{2,1,0:T(1,128)} %all_to_all.36), calls=%async_computation.4 | async-start | bytes 131072 | tf_op jit(solution)/shard_map/all_to_all | solution.py:73

commit v5 on v4

--- a/solution.py
+++ b/solution.py
@@ -46,9 +46,10 @@
 
     my_group = lax.axis_index("tm")
     groups = lax.axis_size("tm")
-    copies = jnp.broadcast_to(flux[None], (groups,) + flux.shape)
-    flux_all = lax.all_to_all(copies, "tm", split_axis=0, concat_axis=0, tiled=True)
-    flux_all = flux_all.reshape(groups * slices, directions, cell_count).astype(f32)
+    shifted = []
+    for shift in range(1, groups):
+        pairs = [(j, (j + shift) % groups) for j in range(groups)]
+        shifted.append(lax.ppermute(flux, "tm", perm=pairs))
 
     foot_r = recv[:, : cap * TILE].reshape(n_slot, TILE)
     meta_r = recv[:, cap * TILE : cap * TILE + cap].reshape(n_slot).astype(jnp.int32)
@@ -57,7 +58,6 @@
     panels = panels.reshape(TILE, n_meta * directions)
     every = jnp.dot(foot_r, panels, preferred_element_type=f32).reshape(n_slot, n_meta, directions)
     partial = jnp.sum(every * meta_hot[:, :, None], axis=1)
-    flux_all, partial = lax.optimization_barrier((flux_all, partial))
     back = lax.all_to_all(
         partial.reshape(n_source, cap * directions), "cell", split_axis=0, concat_axis=0, tiled=True
     ).reshape(n_slot, directions)
@@ -79,8 +79,13 @@
     adj = adj.reshape(tiles, slices, directions, TILE).transpose(1, 2, 0, 3)
     adjoint = adj.reshape(slices, directions, cell_count)
 
-    panel = lax.dynamic_slice(prior, (my_group * slices, 0), (slices, groups * slices))
-    coupled = jnp.einsum("ts,skn->tkn", panel, flux_all, precision=HI)
+    rows = lax.dynamic_slice(prior, (my_group * slices, 0), (slices, groups * slices))
+    own = lax.dynamic_slice(rows, (0, my_group * slices), (slices, slices))
+    coupled = jnp.einsum("ts,skn->tkn", own, flux.astype(f32), precision=HI)
+    for shift in range(1, groups):
+        origin = (my_group - shift) % groups
+        block = lax.dynamic_slice(rows, (0, origin * slices), (slices, slices))
+        coupled = coupled + jnp.einsum("ts,skn->tkn", block, shifted[shift - 1].astype(f32), precision=HI)
     hess = adjoint + coupled
     return (images, hess)
 

time: 102 us -> 109 us (1.069)
  starting transfers between devices: 32.7 us -> 51.6 us
  blocking collectives: 10.4 us -> 0 us
  waiting for transfers between devices: 38.1 us -> 34.8 us
    ppermute x0 -> x7, starting transfers between devices: none -> 21.5 us  [local(): shifted.append(lax.ppermute(flux, 'tm', perm=pairs))]
    all_to_all x1 -> x0, blocking collectives: 10.4 us -> none  [local(): lax.all_to_all(stack, 'tm', split_axis=0, concat_axis=0, tiled=True)]
    all_to_all x1, starting transfers between devices: 10.3 us -> 6.43 us  [local(): lax.all_to_all(stack, 'tm', split_axis=0, concat_axis=0, tiled=True)]
    all_to_all x1, waiting for transfers between devices: 12.7 us -> 8.99 us  [local(): recv = lax.all_to_all(send, 'cell', split_axis=0, concat_axis=0, tiled=True)]
    all_to_all x1, starting transfers between devices: 11.8 us -> 14 us  [local(): recv = lax.all_to_all(send, 'cell', split_axis=0, concat_axis=0, tiled=True)]
    unnamed x27, local copies, waits for them, and re-layouts: 3.49 us -> 4.8 us
    dot_general x1 -> x8, matrix products: 1.86 us -> 2.7 us  [the longest x7 2.38 us: local(): jnp.einsum('ts,skn->tkn', block, shifted[shift - 1].astype(f32), precisio...]
  transfers between devices with their start and end apart: 4 -> 11, of which waited for: 4 -> 4; matrix products, arithmetic and copies ran while one was open for 6% -> 16% of each run, Pallas kernels for 0% -> 0%
where the time goes in v5:
time: 109 us
  starting transfers between devices  51.6 us (47%)
  waiting for transfers between devices  34.8 us (32%)
  local copies, waits for them, and re-layouts  9.78 us (9%)
  matrix products  7.92 us (7%)
  other arithmetic  3.05 us (3%)
  between operations  1.39 us (1%)
    ppermute x7, starting transfers between devices, local(): shifted.append(lax.ppermute(flux, 'tm', perm=pairs))  21.5 us
    all_to_all x1, starting transfers between devices, local(): recv = lax.all_to_all(send, 'cell', split_axis=0, concat_axis=0, tiled=True)  14 us
    all_to_all x1, waiting for transfers between devices, local(): lax.all_to_all(partial.reshape(n_source, cap * directions), 'cell', split...  10.7 us
    all_to_all x1, waiting for transfers between devices, local(): lax.all_to_all(w_send.reshape(n_source, cap * directions), 'cell', split_...  10.7 us
    all_to_all x1, waiting for transfers between devices, local(): recv = lax.all_to_all(send, 'cell', split_axis=0, concat_axis=0, tiled=True)  8.99 us
    all_to_all x1, starting transfers between devices, local(): lax.all_to_all(stack, 'tm', split_axis=0, concat_axis=0, tiled=True)  6.43 us
    all_to_all x1, starting transfers between devices, local(): lax.all_to_all(partial.reshape(n_source, cap * directions), 'cell', split...  5.02 us
    unnamed x27, local copies, waits for them, and re-layouts  4.8 us
  transfers between devices with their start and end apart: 11, of which 4 were waited for; matrix products, arithmetic and copies ran while one was open for 16% of the time, Pallas kernels for 0%

profile of v5, /device:TPU:1, one launch (start us, length us, event | category | flops | bytes accessed | tf_op | source)
XLA Modules:
  0.0 108.5 jit_solution(14724960538153878581)
XLA Ops:
  0.6 0.9 copy.166
  1.6 6.9 %collective-permute-start.6 = (bf16[4,16,512]{2,0,1:T(4,128)(2,1)S(1)}, bf16[4,16,512]{2,0,1:T(4,128)(2,1)S(1)}, u32[]{:S(2)}, u32[]{:S(2)}) collective-permute-start(bf16[4,16,512]{2,0,1:T(4,128)(2,1)S(1)} %copy.166), channel_id=1, source_target_pairs={{0,7},{1,0},{2,1},{3,2},{4,3},{5,4},{6,5},{7,6},{8,15},{9,8},{10,9... | collective-permute-start | bytes 196616 | tf_op jit(solution)/shard_map/ppermute | solution.py:52
  8.5 1.9 %collective-permute-start.5 = (bf16[4,16,512]{2,0,1:T(4,128)(2,1)S(1)}, bf16[4,16,512]{2,0,1:T(4,128)(2,1)S(1)}, u32[]{:S(2)}, u32[]{:S(2)}) collective-permute-start(bf16[4,16,512]{2,0,1:T(4,128)(2,1)S(1)} %copy.166), channel_id=1, source_target_pairs={{0,6},{1,7},{2,0},{3,1},{4,2},{5,3},{6,4},{7,5},{8,14},{9,15},{10,... | collective-permute-start | bytes 196616 | tf_op jit(solution)/shard_map/ppermute | solution.py:52
  10.4 1.9 %collective-permute-start.4 = (bf16[4,16,512]{2,0,1:T(4,128)(2,1)S(1)}, bf16[4,16,512]{2,0,1:T(4,128)(2,1)S(1)}, u32[]{:S(2)}, u32[]{:S(2)}) collective-permute-start(bf16[4,16,512]{2,0,1:T(4,128)(2,1)S(1)} %copy.166), channel_id=1, source_target_pairs={{0,5},{1,6},{2,7},{3,0},{4,1},{5,2},{6,3},{7,4},{8,13},{9,14},{10,... | collective-permute-start | bytes 196616 | tf_op jit(solution)/shard_map/ppermute | solution.py:52
  12.3 5.3 %collective-permute-start.3 = (bf16[4,16,512]{2,0,1:T(4,128)(2,1)S(1)}, bf16[4,16,512]{2,0,1:T(4,128)(2,1)S(1)}, u32[]{:S(2)}, u32[]{:S(2)}) collective-permute-start(bf16[4,16,512]{2,0,1:T(4,128)(2,1)S(1)} %copy.166), channel_id=1, source_target_pairs={{0,4},{1,5},{2,6},{3,7},{4,0},{5,1},{6,2},{7,3},{8,12},{9,13},{10,... | collective-permute-start | bytes 196616 | tf_op jit(solution)/shard_map/ppermute | solution.py:52
  17.6 1.9 %collective-permute-start.2 = (bf16[4,16,512]{2,0,1:T(4,128)(2,1)S(1)}, bf16[4,16,512]{2,0,1:T(4,128)(2,1)S(1)}, u32[]{:S(2)}, u32[]{:S(2)}) collective-permute-start(bf16[4,16,512]{2,0,1:T(4,128)(2,1)S(1)} %copy.166), channel_id=1, source_target_pairs={{0,3},{1,4},{2,5},{3,6},{4,7},{5,0},{6,1},{7,2},{8,11},{9,12},{10,... | collective-permute-start | bytes 196616 | tf_op jit(solution)/shard_map/ppermute | solution.py:52
  19.6 0.8 copy.148
  20.5 0.7 iota_compare_fusion.11
  21.6 0.5 fusion.8
  23.0 1.4 %fusion.5 = f32[1,64,16]{2,0,1:T(1,128)S(1)} fusion(bf16[512,1,1]{0,1,2:T(2,128)(2,1)S(1)} %reshape.233, s32[64,16]{1,0:T(8,128)S(1)} %multiply_add_fusion, s32[512]{0:T(512)S(1)} %add_select_fusion.2), kind=kOutput, calls=%fused_computation.6 | convolution fusion | flops 1572864 | bytes 11264 | tf_op jit(solution)/shard_map/dot_general | solution.py:41
  24.6 0.5 broadcast.158
  25.1 0.8 reduce.2
  25.8 1.0 reshape.252
  26.8 14.0 %all-to-all-start = ((bf16[64,2,1088]{2,1,0:T(2,128)(2,1)}), bf16[64,2,1088]{2,1,0:T(2,128)(2,1)S(1)}, u32[]{:S(2)}, u32[]{:S(2)}) async-start(bf16[64,2,1088]{2,1,0:T(2,128)(2,1)} %reshape.252), calls=%async_computation | async-start | bytes 589824 | tf_op jit(solution)/shard_map/all_to_all | solution.py:45
  42.0 3.6 %collective-permute-start.1 = (bf16[4,16,512]{2,0,1:T(4,128)(2,1)S(1)}, bf16[4,16,512]{2,0,1:T(4,128)(2,1)S(1)}, u32[]{:S(2)}, u32[]{:S(2)}) collective-permute-start(bf16[4,16,512]{2,0,1:T(4,128)(2,1)S(1)} %copy.166), channel_id=1, source_target_pairs={{0,2},{1,3},{2,4},{3,5},{4,6},{5,7},{6,0},{7,1},{8,10},{9,11},{10,... | collective-permute-start | bytes 196616 | tf_op jit(solution)/shard_map/ppermute | solution.py:52
  46.3 9.0 %all-to-all-done = bf16[64,2,1088]{2,1,0:T(2,128)(2,1)S(1)} async-done(((bf16[64,2,1088]{2,1,0:T(2,128)(2,1)}), bf16[64,2,1088]{2,1,0:T(2,128)(2,1)S(1)}, u32[]{:S(2)}, u32[]{:S(2)}) %all-to-all-start) | async-done | bytes 278560 | tf_op jit(solution)/shard_map/all_to_all | solution.py:45
  56.4 0.9 all_to_all.31
  57.3 5.0 %all-to-all-start.1 = ((f32[64,1,256]{2,1,0:T(1,128)}), f32[64,1,256]{2,1,0:T(1,128)S(1)}, u32[]{:S(2)}, u32[]{:S(2)}) async-start(f32[64,1,256]{2,1,0:T(1,128)} %all_to_all.31), calls=%async_computation.1 | async-start | bytes 131072 | tf_op jit(solution)/shard_map/all_to_all | solution.py:61
  62.7 10.7 %all-to-all-done.1 = f32[64,1,256]{2,1,0:T(1,128)S(1)} async-done(((f32[64,1,256]{2,1,0:T(1,128)}), f32[64,1,256]{2,1,0:T(1,128)S(1)}, u32[]{:S(2)}, u32[]{:S(2)}) %all-to-all-start.1) | async-done | bytes 65568 | tf_op jit(solution)/shard_map/all_to_all | solution.py:61
  73.8 1.1 %fusion.9 = f32[64,16]{1,0:T(8,128)S(1)} fusion(s32[64,8]{1,0:T(8,128)S(1)} %fusion.38, f32[1024,16]{1,0:T(8,128)S(1)} %reshape.229), kind=kOutput, calls=%fused_computation.11 | convolution fusion | flops 101194752 | bytes 71680 | tf_op jit(solution)/shard_map/dot_general | solution.py:66
  75.0 0.7 reshape.254
  75.7 6.4 %all-to-all-start.2 = ((f32[8,1,1024]{2,1,0:T(1,128)}), f32[8,1,1024]{2,1,0:T(1,128)S(1)}, u32[]{:S(2)}, u32[]{:S(2)}) async-start(f32[8,1,1024]{2,1,0:T(1,128)} %reshape.254), calls=%async_computation.2 | async-start | bytes 65536 | tf_op jit(solution)/shard_map/all_to_all | solution.py:69
  82.5 4.4 %all-to-all-done.2 = f32[8,1,1024]{2,1,0:T(1,128)S(1)} async-done(((f32[8,1,1024]{2,1,0:T(1,128)}), f32[8,1,1024]{2,1,0:T(1,128)S(1)}, u32[]{:S(2)}, u32[]{:S(2)}) %all-to-all-start.2) | async-done | bytes 32800 | tf_op jit(solution)/shard_map/all_to_all | solution.py:69
  86.8 0.5 broadcast.159
  87.4 0.7 reduce.3
  88.3 1.0 fusion
  89.3 0.9 all_to_all.32
  90.2 4.6 %all-to-all-start.3 = ((f32[64,1,256]{2,1,0:T(1,128)}), f32[64,1,256]{2,1,0:T(1,128)S(1)}, u32[]{:S(2)}, u32[]{:S(2)}) async-start(f32[64,1,256]{2,1,0:T(1,128)} %all_to_all.32), calls=%async_computation.3 | async-start | bytes 131072 | tf_op jit(solution)/shard_map/all_to_all | solution.py:73
  95.3 10.7 %all-to-all-done.3 = f32[64,1,256]{2,1,0:T(1,128)S(1)} async-done(((f32[64,1,256]{2,1,0:T(1,128)}), f32[64,1,256]{2,1,0:T(1,128)S(1)}, u32[]{:S(2)}, u32[]{:S(2)}) %all-to-all-start.3) | async-done | bytes 65568 | tf_op jit(solution)/shard_map/all_to_all | solution.py:73
  106.6 0.6 convolution_bitcast_fusion
  107.4 0.4 fusion.17
  107.8 0.7 copy.175
  (78 shorter events, 6.7 us)
Async XLA Ops:
  0.6 21.0 %copy-start = (bf16[64,8,128]{2,1,0:T(8,128)(2,1)S(1)}, bf16[64,8,128]{2,1,0:T(8,128)(2,1)}, u32[]{:S(2)}) copy-start(bf16[64,8,128]{2,1,0:T(8,128)(2,1)} %param.9) | copy-start | bytes 393220
  1.6 40.1 %collective-permute-start.6 = (bf16[4,16,512]{2,0,1:T(4,128)(2,1)S(1)}, bf16[4,16,512]{2,0,1:T(4,128)(2,1)S(1)}, u32[]{:S(2)}, u32[]{:S(2)}) collective-permute-start(bf16[4,16,512]{2,0,1:T(4,128)(2,1)S(1)} %copy.166), channel_id=1, source_target_pairs={{0,7},{1,0},{2,1},{3,2},{4,3},{5,4},{6,5},{7,6},{8,15},{9,8},{10,9... | collective-permute-start | bytes 196616 | tf_op jit(solution)/shard_map/ppermute | solution.py:52
  8.5 33.6 %collective-permute-start.5 = (bf16[4,16,512]{2,0,1:T(4,128)(2,1)S(1)}, bf16[4,16,512]{2,0,1:T(4,128)(2,1)S(1)}, u32[]{:S(2)}, u32[]{:S(2)}) collective-permute-start(bf16[4,16,512]{2,0,1:T(4,128)(2,1)S(1)} %copy.166), channel_id=1, source_target_pairs={{0,6},{1,7},{2,0},{3,1},{4,2},{5,3},{6,4},{7,5},{8,14},{9,15},{10,... | collective-permute-start | bytes 196616 | tf_op jit(solution)/shard_map/ppermute | solution.py:52
  10.4 51.9 %collective-permute-start.4 = (bf16[4,16,512]{2,0,1:T(4,128)(2,1)S(1)}, bf16[4,16,512]{2,0,1:T(4,128)(2,1)S(1)}, u32[]{:S(2)}, u32[]{:S(2)}) collective-permute-start(bf16[4,16,512]{2,0,1:T(4,128)(2,1)S(1)} %copy.166), channel_id=1, source_target_pairs={{0,5},{1,6},{2,7},{3,0},{4,1},{5,2},{6,3},{7,4},{8,13},{9,14},{10,... | collective-permute-start | bytes 196616 | tf_op jit(solution)/shard_map/ppermute | solution.py:52
  12.3 69.8 %collective-permute-start.3 = (bf16[4,16,512]{2,0,1:T(4,128)(2,1)S(1)}, bf16[4,16,512]{2,0,1:T(4,128)(2,1)S(1)}, u32[]{:S(2)}, u32[]{:S(2)}) collective-permute-start(bf16[4,16,512]{2,0,1:T(4,128)(2,1)S(1)} %copy.166), channel_id=1, source_target_pairs={{0,4},{1,5},{2,6},{3,7},{4,0},{5,1},{6,2},{7,3},{8,12},{9,13},{10,... | collective-permute-start | bytes 196616 | tf_op jit(solution)/shard_map/ppermute | solution.py:52
  17.6 77.2 %collective-permute-start.2 = (bf16[4,16,512]{2,0,1:T(4,128)(2,1)S(1)}, bf16[4,16,512]{2,0,1:T(4,128)(2,1)S(1)}, u32[]{:S(2)}, u32[]{:S(2)}) collective-permute-start(bf16[4,16,512]{2,0,1:T(4,128)(2,1)S(1)} %copy.166), channel_id=1, source_target_pairs={{0,3},{1,4},{2,5},{3,6},{4,7},{5,0},{6,1},{7,2},{8,11},{9,12},{10,... | collective-permute-start | bytes 196616 | tf_op jit(solution)/shard_map/ppermute | solution.py:52
  20.4 1.9 %copy-start.6 = (s32[1,64,2]{1,2,0:T(2,128)S(1)}, s32[1,64,2]{1,2,0:T(2,128)}, u32[]{:S(2)}) copy-start(s32[1,64,2]{1,2,0:T(2,128)} %param.13) | copy-start | bytes 1540
  21.3 1.5 %copy-start.4 = (s32[64,8]{0,1:T(8,128)S(1)}, s32[64,8]{0,1:T(8,128)}, u32[]{:S(2)}) copy-start(s32[64,8]{0,1:T(8,128)} %param.11) | copy-start | bytes 6148
  24.4 16.5 %copy-start.1 = (bf16[4,16,512]{2,1,0:T(8,128)(2,1)S(1)}, bf16[4,16,512]{2,1,0:T(8,128)(2,1)}, u32[]{:S(2)}) copy-start(bf16[4,16,512]{2,1,0:T(8,128)(2,1)} %param.8) | copy-start | bytes 196612
  24.4 16.5 %copy-start.3 = (f32[32,32]{1,0:T(8,128)S(1)}, f32[32,32]{1,0:T(8,128)}, u32[]{:S(2)}) copy-start(f32[32,32]{1,0:T(8,128)} %param.15) | copy-start | bytes 12292
  24.6 16.8 %copy-start.5 = (s32[64,1]{0,1:T(1,128)S(1)}, s32[64,1]{0,1:T(1,128)}, u32[]{:S(2)}) copy-start(s32[64,1]{0,1:T(1,128)} %param.12) | copy-start | bytes 772
  26.8 28.4 %all-to-all-start = ((bf16[64,2,1088]{2,1,0:T(2,128)(2,1)}), bf16[64,2,1088]{2,1,0:T(2,128)(2,1)S(1)}, u32[]{:S(2)}, u32[]{:S(2)}) async-start(bf16[64,2,1088]{2,1,0:T(2,128)(2,1)} %reshape.252), calls=%async_computation | async-start | bytes 589824 | tf_op jit(solution)/shard_map/all_to_all | solution.py:45
  41.7 4.3 %collective-permute-start = (bf16[4,16,512]{2,0,1:T(4,128)(2,1)S(1)}, bf16[4,16,512]{2,0,1:T(4,128)(2,1)S(1)}, u32[]{:S(2)}, u32[]{:S(2)}) collective-permute-start(bf16[4,16,512]{2,0,1:T(4,128)(2,1)S(1)} %copy.166), channel_id=1, source_target_pairs={{0,1},{1,2},{2,3},{3,4},{4,5},{5,6},{6,7},{7,0},{8,9},{9,10},{10,1... | collective-permute-start | bytes 196616 | tf_op jit(solution)/shard_map/ppermute | solution.py:52
  42.0 65.4 %collective-permute-start.1 = (bf16[4,16,512]{2,0,1:T(4,128)(2,1)S(1)}, bf16[4,16,512]{2,0,1:T(4,128)(2,1)S(1)}, u32[]{:S(2)}, u32[]{:S(2)}) collective-permute-start(bf16[4,16,512]{2,0,1:T(4,128)(2,1)S(1)} %copy.166), channel_id=1, source_target_pairs={{0,2},{1,3},{2,4},{3,5},{4,6},{5,7},{6,0},{7,1},{8,10},{9,11},{10,... | collective-permute-start | bytes 196616 | tf_op jit(solution)/shard_map/ppermute | solution.py:52
  57.3 16.1 %all-to-all-start.1 = ((f32[64,1,256]{2,1,0:T(1,128)}), f32[64,1,256]{2,1,0:T(1,128)S(1)}, u32[]{:S(2)}, u32[]{:S(2)}) async-start(f32[64,1,256]{2,1,0:T(1,128)} %all_to_all.31), calls=%async_computation.1 | async-start | bytes 131072 | tf_op jit(solution)/shard_map/all_to_all | solution.py:61
  73.7 14.4 %copy-start.7 = (f32[64]{0:T(128)S(1)}, f32[64]{0:T(128)}, u32[]{:S(2)}) copy-start(f32[64]{0:T(128)} %param.14) | copy-start | bytes 772
  75.7 11.1 %all-to-all-start.2 = ((f32[8,1,1024]{2,1,0:T(1,128)}), f32[8,1,1024]{2,1,0:T(1,128)S(1)}, u32[]{:S(2)}, u32[]{:S(2)}) async-start(f32[8,1,1024]{2,1,0:T(1,128)} %reshape.254), calls=%async_computation.2 | async-start | bytes 65536 | tf_op jit(solution)/shard_map/all_to_all | solution.py:69
  88.2 7.1 %copy-start.2 = (f32[64,16]{0,1:T(8,128)}, f32[64,16]{0,1:T(8,128)S(1)}, u32[]{:S(2)}) copy-start(f32[64,16]{0,1:T(8,128)S(1)} %bitcast_reduce_fusion) | copy-start | bytes 12292
  90.2 15.8 %all-to-all-start.3 = ((f32[64,1,256]{2,1,0:T(1,128)}), f32[64,1,256]{2,1,0:T(1,128)S(1)}, u32[]{:S(2)}, u32[]{:S(2)}) async-start(f32[64,1,256]{2,1,0:T(1,128)} %all_to_all.32), calls=%async_computation.3 | async-start | bytes 131072 | tf_op jit(solution)/shard_map/all_to_all | solution.py:73

commit v6 on v4

--- a/solution.py
+++ b/solution.py
@@ -57,7 +57,9 @@
     panels = panels.reshape(TILE, n_meta * directions)
     every = jnp.dot(foot_r, panels, preferred_element_type=f32).reshape(n_slot, n_meta, directions)
     partial = jnp.sum(every * meta_hot[:, :, None], axis=1)
-    flux_all, partial = lax.optimization_barrier((flux_all, partial))
+    panel = lax.dynamic_slice(prior, (my_group * slices, 0), (slices, groups * slices))
+    coupled = jnp.einsum("ts,skn->tkn", panel, flux_all, precision=HI)
+    coupled, partial = lax.optimization_barrier((coupled, partial))
     back = lax.all_to_all(
         partial.reshape(n_source, cap * directions), "cell", split_axis=0, concat_axis=0, tiled=True
     ).reshape(n_slot, directions)
@@ -74,13 +76,11 @@
         w_send.reshape(n_source, cap * directions), "cell", split_axis=0, concat_axis=0, tiled=True
     ).reshape(n_slot, directions)
 
-    w_meta = (meta_hot[:, :, None] * w_recv[:, None, :]).reshape(n_slot, n_meta * directions)
+    hot_tt = meta_hot.reshape(n_slot, tiles, slices).transpose(0, 2, 1)
+    w_meta = (hot_tt[:, :, None, :] * w_recv[:, None, :, None]).reshape(n_slot, n_meta * directions)
     adj = jnp.dot(w_meta.T, foot_r.astype(f32), precision=HI, preferred_element_type=f32)
-    adj = adj.reshape(tiles, slices, directions, TILE).transpose(1, 2, 0, 3)
     adjoint = adj.reshape(slices, directions, cell_count)
 
-    panel = lax.dynamic_slice(prior, (my_group * slices, 0), (slices, groups * slices))
-    coupled = jnp.einsum("ts,skn->tkn", panel, flux_all, precision=HI)
     hess = adjoint + coupled
     return (images, hess)
 

time: 102 us -> 102 us (level)
  blocking collectives: 10.4 us -> 0 us
  starting transfers between devices: 32.7 us -> 39.1 us
  waiting for transfers between devices: 38.1 us -> 41.8 us
  local copies, waits for them, and re-layouts: 9.5 us -> 10.6 us
    all_to_all x1 -> x0, blocking collectives: 10.4 us -> none  [local(): lax.all_to_all(stack, 'tm', split_axis=0, concat_axis=0, tiled=True)]
    all_to_all x0 -> x1, starting transfers between devices: none -> 6.56 us  [local(): lax.all_to_all(stack, 'tm', split_axis=0, concat_axis=0, tiled=True)]
    all_to_all x0 -> x1, waiting for transfers between devices: none -> 4.61 us  [local(): lax.all_to_all(stack, 'tm', split_axis=0, concat_axis=0, tiled=True)]
    all_to_all x1, waiting for transfers between devices: 12.7 us -> 11.6 us  [local(): recv = lax.all_to_all(send, 'cell', split_axis=0, concat_axis=0, tiled=True)]
  transfers between devices with their start and end apart: 4 -> 5, of which waited for: 4 -> 5; matrix products, arithmetic and copies ran while one was open for 6% -> 7% of each run, Pallas kernels for 0% -> 0%
where the time goes in v6:
time: 102 us
  waiting for transfers between devices  41.8 us (41%)
  starting transfers between devices  39.1 us (38%)
  local copies, waits for them, and re-layouts  10.6 us (10%)
  matrix products  6.25 us (6%)
  other arithmetic  2.72 us (3%)
  between operations  1.07 us (1%)
    all_to_all x1, starting transfers between devices, local(): recv = lax.all_to_all(send, 'cell', split_axis=0, concat_axis=0, tiled=True)  11.8 us
    all_to_all x1, waiting for transfers between devices, local(): recv = lax.all_to_all(send, 'cell', split_axis=0, concat_axis=0, tiled=True)  11.6 us
    all_to_all x1, waiting for transfers between devices, local(): lax.all_to_all(w_send.reshape(n_source, cap * directions), 'cell', split_...  11.1 us
    all_to_all x1, waiting for transfers between devices, local(): lax.all_to_all(partial.reshape(n_source, cap * directions), 'cell', split...  11 us
    all_to_all x1, starting transfers between devices, local(): lax.all_to_all(copies, 'tm', split_axis=0, concat_axis=0, tiled=True)  10.3 us
    all_to_all x1, starting transfers between devices, local(): lax.all_to_all(stack, 'tm', split_axis=0, concat_axis=0, tiled=True)  6.56 us
    all_to_all x1, starting transfers between devices, local(): lax.all_to_all(partial.reshape(n_source, cap * directions), 'cell', split...  5.83 us
    all_to_all x1, starting transfers between devices, local(): lax.all_to_all(w_send.reshape(n_source, cap * directions), 'cell', split_...  4.62 us
  transfers between devices with their start and end apart: 5, of which 5 were waited for; matrix products, arithmetic and copies ran while one was open for 7% of the time, Pallas kernels for 0%

profile of v6, /device:TPU:1, one launch (start us, length us, event | category | flops | bytes accessed | tf_op | source)
XLA Modules:
  0.0 101.5 jit_solution(2919501113627031417)
XLA Ops:
  0.7 0.9 copy.109
  1.6 0.9 broadcast_in_dim.29
  2.5 10.3 %all-to-all-start = ((bf16[8,4,16,512]{3,1,2,0:T(4,128)(2,1)}), bf16[8,4,16,512]{3,1,2,0:T(4,128)(2,1)S(1)}, u32[]{:S(2)}, u32[]{:S(2)}) async-start(bf16[8,4,16,512]{3,1,2,0:T(4,128)(2,1)} %broadcast_in_dim.29), calls=%async_computation | async-start | bytes 1048576 | tf_op jit(solution)/shard_map/all_to_all | solution.py:50
  13.2 0.3 fusion.12
  14.3 1.4 %fusion.5 = f32[1,64,16]{2,0,1:T(1,128)S(1)} fusion(bf16[512,1,1]{0,1,2:T(2,128)(2,1)S(1)} %reshape.262, s32[64,16]{1,0:T(8,128)S(1)} %multiply_add_fusion, s32[512]{0:T(512)S(1)} %add_select_fusion.2), kind=kOutput, calls=%fused_computation.6 | convolution fusion | flops 1572864 | bytes 11264 | tf_op jit(solution)/shard_map/dot_general | solution.py:41
  15.7 0.5 fusion.8
  16.5 0.5 broadcast.162
  17.0 0.8 reduce.2
  17.7 1.0 reshape.270
  18.7 3.6 %all-to-all-done = bf16[8,4,16,512]{3,1,2,0:T(4,128)(2,1)S(1)} async-done(((bf16[8,4,16,512]{3,1,2,0:T(4,128)(2,1)}), bf16[8,4,16,512]{3,1,2,0:T(4,128)(2,1)S(1)}, u32[]{:S(2)}, u32[]{:S(2)}) %all-to-all-start) | async-done | bytes 524320 | tf_op jit(solution)/shard_map/all_to_all | solution.py:50
  22.3 11.8 %all-to-all-start.1 = ((bf16[64,2,1088]{2,1,0:T(2,128)(2,1)}), bf16[64,2,1088]{2,1,0:T(2,128)(2,1)S(1)}, u32[]{:S(2)}, u32[]{:S(2)}) async-start(bf16[64,2,1088]{2,1,0:T(2,128)(2,1)} %reshape.270), calls=%async_computation.1 | async-start | bytes 589824 | tf_op jit(solution)/shard_map/all_to_all | solution.py:45
  34.7 1.0 fusion.34
  35.7 11.6 %all-to-all-done.1 = bf16[64,2,1088]{2,1,0:T(2,128)(2,1)S(1)} async-done(((bf16[64,2,1088]{2,1,0:T(2,128)(2,1)}), bf16[64,2,1088]{2,1,0:T(2,128)(2,1)S(1)}, u32[]{:S(2)}, u32[]{:S(2)}) %all-to-all-start.1) | async-done | bytes 278560 | tf_op jit(solution)/shard_map/all_to_all | solution.py:45
  47.3 0.3 reshape.271
  47.9 0.3 fusion.7
  48.4 0.9 all_to_all.35
  49.3 5.8 %all-to-all-start.2 = ((f32[64,1,256]{2,1,0:T(1,128)}), f32[64,1,256]{2,1,0:T(1,128)S(1)}, u32[]{:S(2)}, u32[]{:S(2)}) async-start(f32[64,1,256]{2,1,0:T(1,128)} %all_to_all.35), calls=%async_computation.2 | async-start | bytes 131072 | tf_op jit(solution)/shard_map/all_to_all | solution.py:63
  55.2 11.0 %all-to-all-done.2 = f32[64,1,256]{2,1,0:T(1,128)S(1)} async-done(((f32[64,1,256]{2,1,0:T(1,128)}), f32[64,1,256]{2,1,0:T(1,128)S(1)}, u32[]{:S(2)}, u32[]{:S(2)}) %all-to-all-start.2) | async-done | bytes 65568 | tf_op jit(solution)/shard_map/all_to_all | solution.py:63
  66.6 1.1 %fusion.9 = f32[64,16]{1,0:T(8,128)S(1)} fusion(s32[64,8]{1,0:T(8,128)S(1)} %fusion.31, f32[1024,16]{1,0:T(8,128)S(1)} %reshape.257), kind=kOutput, calls=%fused_computation.11 | convolution fusion | flops 101194752 | bytes 71680 | tf_op jit(solution)/shard_map/dot_general | solution.py:68
  67.8 0.7 reshape.272
  68.5 6.6 %all-to-all-start.3 = ((f32[8,1,1024]{2,1,0:T(1,128)}), f32[8,1,1024]{2,1,0:T(1,128)S(1)}, u32[]{:S(2)}, u32[]{:S(2)}) async-start(f32[8,1,1024]{2,1,0:T(1,128)} %reshape.272), calls=%async_computation.3 | async-start | bytes 65536 | tf_op jit(solution)/shard_map/all_to_all | solution.py:71
  75.2 4.6 %all-to-all-done.3 = f32[8,1,1024]{2,1,0:T(1,128)S(1)} async-done(((f32[8,1,1024]{2,1,0:T(1,128)}), f32[8,1,1024]{2,1,0:T(1,128)S(1)}, u32[]{:S(2)}, u32[]{:S(2)}) %all-to-all-start.3) | async-done | bytes 32800 | tf_op jit(solution)/shard_map/all_to_all | solution.py:71
  79.8 0.5 broadcast.163
  80.3 0.7 reduce.3
  81.3 1.0 %fusion = f32[1024,16]{1,0:T(8,128)S(1)} fusion(s32[512]{0:T(512)S(1)} %add_select_fusion.2, f32[64,16]{1,0:T(8,128)S(1)} %copy.119), kind=kOutput, calls=%fused_computation.1 | convolution fusion | flops 101187584 | bytes 71680 | tf_op jit(solution)/shard_map/dot_general | solution.py:74
  82.3 0.9 all_to_all.36
  83.2 4.6 %all-to-all-start.4 = ((f32[64,1,256]{2,1,0:T(1,128)}), f32[64,1,256]{2,1,0:T(1,128)S(1)}, u32[]{:S(2)}, u32[]{:S(2)}) async-start(f32[64,1,256]{2,1,0:T(1,128)} %all_to_all.36), calls=%async_computation.4 | async-start | bytes 131072 | tf_op jit(solution)/shard_map/all_to_all | solution.py:75
  87.9 11.1 %all-to-all-done.4 = f32[64,1,256]{2,1,0:T(1,128)S(1)} async-done(((f32[64,1,256]{2,1,0:T(1,128)}), f32[64,1,256]{2,1,0:T(1,128)S(1)}, u32[]{:S(2)}, u32[]{:S(2)}) %all-to-all-start.4) | async-done | bytes 65568 | tf_op jit(solution)/shard_map/all_to_all | solution.py:75
  99.4 0.3 broadcast_multiply_fusion
  99.7 0.4 mul.91
  100.1 0.6 fusion.39
  100.8 0.7 copy.124
  (65 shorter events, 3.9 us)
Async XLA Ops:
  0.6 15.1 %copy-start = (bf16[64,8,128]{2,1,0:T(8,128)(2,1)S(1)}, bf16[64,8,128]{2,1,0:T(8,128)(2,1)}, u32[]{:S(2)}) copy-start(bf16[64,8,128]{2,1,0:T(8,128)(2,1)} %param.9) | copy-start | bytes 393220
  0.6 12.2 %copy-start.5 = (s32[64,1]{0,1:T(1,128)S(1)}, s32[64,1]{0,1:T(1,128)}, u32[]{:S(2)}) copy-start(s32[64,1]{0,1:T(1,128)} %param.12) | copy-start | bytes 772
  0.7 12.4 %copy-start.3 = (s32[64,8]{0,1:T(8,128)S(1)}, s32[64,8]{0,1:T(8,128)}, u32[]{:S(2)}) copy-start(s32[64,8]{0,1:T(8,128)} %param.10) | copy-start | bytes 6148
  1.6 11.9 %copy-start.4 = (s32[64,8]{0,1:T(8,128)S(1)}, s32[64,8]{0,1:T(8,128)}, u32[]{:S(2)}) copy-start(s32[64,8]{0,1:T(8,128)} %param.11) | copy-start | bytes 6148
  1.6 12.0 %copy-start.6 = (s32[1,64,2]{1,2,0:T(2,128)S(1)}, s32[1,64,2]{1,2,0:T(2,128)}, u32[]{:S(2)}) copy-start(s32[1,64,2]{1,2,0:T(2,128)} %param.13) | copy-start | bytes 1540
  2.5 19.8 %all-to-all-start = ((bf16[8,4,16,512]{3,1,2,0:T(4,128)(2,1)}), bf16[8,4,16,512]{3,1,2,0:T(4,128)(2,1)S(1)}, u32[]{:S(2)}, u32[]{:S(2)}) async-start(bf16[8,4,16,512]{3,1,2,0:T(4,128)(2,1)} %broadcast_in_dim.29), calls=%async_computation | async-start | bytes 1048576 | tf_op jit(solution)/shard_map/all_to_all | solution.py:50
  16.3 17.8 %copy-start.1 = (bf16[4,16,512]{2,1,0:T(8,128)(2,1)S(1)}, bf16[4,16,512]{2,1,0:T(8,128)(2,1)}, u32[]{:S(2)}) copy-start(bf16[4,16,512]{2,1,0:T(8,128)(2,1)} %param.8) | copy-start | bytes 196612
  22.3 25.0 %all-to-all-start.1 = ((bf16[64,2,1088]{2,1,0:T(2,128)(2,1)}), bf16[64,2,1088]{2,1,0:T(2,128)(2,1)S(1)}, u32[]{:S(2)}, u32[]{:S(2)}) async-start(bf16[64,2,1088]{2,1,0:T(2,128)(2,1)} %reshape.270), calls=%async_computation.1 | async-start | bytes 589824 | tf_op jit(solution)/shard_map/all_to_all | solution.py:45
  49.3 16.9 %all-to-all-start.2 = ((f32[64,1,256]{2,1,0:T(1,128)}), f32[64,1,256]{2,1,0:T(1,128)S(1)}, u32[]{:S(2)}, u32[]{:S(2)}) async-start(f32[64,1,256]{2,1,0:T(1,128)} %all_to_all.35), calls=%async_computation.2 | async-start | bytes 131072 | tf_op jit(solution)/shard_map/all_to_all | solution.py:63
  66.6 14.6 %copy-start.7 = (f32[64]{0:T(128)S(1)}, f32[64]{0:T(128)}, u32[]{:S(2)}) copy-start(f32[64]{0:T(128)} %param.14) | copy-start | bytes 772
  68.5 11.3 %all-to-all-start.3 = ((f32[8,1,1024]{2,1,0:T(1,128)}), f32[8,1,1024]{2,1,0:T(1,128)S(1)}, u32[]{:S(2)}, u32[]{:S(2)}) async-start(f32[8,1,1024]{2,1,0:T(1,128)} %reshape.272), calls=%async_computation.3 | async-start | bytes 65536 | tf_op jit(solution)/shard_map/all_to_all | solution.py:71
  81.1 18.1 %copy-start.2 = (f32[64,16]{0,1:T(8,128)}, f32[64,16]{0,1:T(8,128)S(1)}, u32[]{:S(2)}) copy-start(f32[64,16]{0,1:T(8,128)S(1)} %bitcast_reduce_fusion) | copy-start | bytes 12292
  83.2 15.8 %all-to-all-start.4 = ((f32[64,1,256]{2,1,0:T(1,128)}), f32[64,1,256]{2,1,0:T(1,128)S(1)}, u32[]{:S(2)}, u32[]{:S(2)}) async-start(f32[64,1,256]{2,1,0:T(1,128)} %all_to_all.36), calls=%async_computation.4 | async-start | bytes 131072 | tf_op jit(solution)/shard_map/all_to_all | solution.py:75

commit v7 on v6

--- a/solution.py
+++ b/solution.py
@@ -40,8 +40,13 @@
     foot_send = jnp.dot(place_b, foot_flat, preferred_element_type=f32).astype(jnp.bfloat16)
     meta_send = jnp.dot(place_b, meta.astype(jnp.bfloat16)[:, None], preferred_element_type=f32)
     meta_send = meta_send.reshape(n_source, cap).astype(jnp.bfloat16)
-    meta_pad = jnp.zeros((n_source, TILE - cap), jnp.bfloat16)
-    send = jnp.concatenate([foot_send.reshape(n_source, cap * TILE), meta_send, meta_pad], axis=1)
+    sound_of = (row // nb).astype(jnp.bfloat16)[:, None]
+    sound_send = jnp.dot(place_b, sound_of, preferred_element_type=f32)
+    sound_send = sound_send.reshape(n_source, cap).astype(jnp.bfloat16)
+    meta_pad = jnp.zeros((n_source, TILE - 2 * cap), jnp.bfloat16)
+    send = jnp.concatenate(
+        [foot_send.reshape(n_source, cap * TILE), meta_send, sound_send, meta_pad], axis=1
+    )
     recv = lax.all_to_all(send, "cell", split_axis=0, concat_axis=0, tiled=True)
 
     my_group = lax.axis_index("tm")
@@ -60,21 +65,28 @@
     panel = lax.dynamic_slice(prior, (my_group * slices, 0), (slices, groups * slices))
     coupled = jnp.einsum("ts,skn->tkn", panel, flux_all, precision=HI)
     coupled, partial = lax.optimization_barrier((coupled, partial))
-    back = lax.all_to_all(
-        partial.reshape(n_source, cap * directions), "cell", split_axis=0, concat_axis=0, tiled=True
-    ).reshape(n_slot, directions)
+    sound_r = recv[:, cap * TILE + cap : cap * TILE + 2 * cap].astype(jnp.int32)
+    sound_hot = (sound_r[:, None, :] == jnp.arange(sounds, dtype=jnp.int32)[None, :, None]).astype(f32)
+    share = jnp.einsum(
+        "dsr,drk->dsk", sound_hot, partial.reshape(n_source, cap, directions), precision=HI
+    )
 
-    place_f = place.astype(f32)
-    per_block = jnp.dot(place_f.T, back, precision=HI, preferred_element_type=f32)
-    partial_value = per_block.reshape(sounds, nb, directions).sum(axis=1)
-    stack = jnp.broadcast_to(partial_value[None], (groups,) + partial_value.shape)
-    images = lax.all_to_all(stack, "tm", split_axis=0, concat_axis=0, tiled=True).sum(axis=0)
-    weighted = obs_weight[:, None] * images
-    w_block = jnp.repeat(weighted, nb, axis=0)
-    w_send = jnp.dot(place_f, w_block, precision=HI, preferred_element_type=f32)
-    w_recv = lax.all_to_all(
-        w_send.reshape(n_source, cap * directions), "cell", split_axis=0, concat_axis=0, tiled=True
-    ).reshape(n_slot, directions)
+    my_cell = lax.axis_index("cell")
+    own_weight = jnp.where(my_group == 0, obs_weight, jnp.zeros_like(obs_weight))
+    weight_share = lax.dynamic_update_slice(
+        jnp.zeros((n_source, sounds), f32), own_weight[None, :], (my_cell, 0)
+    )
+    total = jnp.concatenate(
+        [share.reshape(-1, TILE), weight_share.reshape(-1, TILE)], axis=0
+    )
+    total = lax.psum(total, ("cell", "tm"))
+    split = n_source * sounds * directions // TILE
+    obs_all = total[:split].reshape(n_source, sounds, directions)
+    weight_all = total[split:].reshape(n_source, sounds)
+    images = lax.dynamic_index_in_dim(obs_all, my_cell, axis=0, keepdims=False)
+    weighted_all = weight_all[:, :, None] * obs_all
+    w_recv = jnp.einsum("dsr,dsk->drk", sound_hot, weighted_all, precision=HI)
+    w_recv = w_recv.reshape(n_slot, directions)
 
     hot_tt = meta_hot.reshape(n_slot, tiles, slices).transpose(0, 2, 1)
     w_meta = (hot_tt[:, :, None, :] * w_recv[:, None, :, None]).reshape(n_slot, n_meta * directions)

time: 102 us -> 335 us (3.28)
  waiting for transfers between devices: 41.8 us -> 274 us
  starting transfers between devices: 39.1 us -> 22.1 us
  between operations: 1.07 us -> 14.4 us
    psum x0 -> x1, waiting for transfers between devices: none -> 263 us  [local(): total = lax.psum(total, ('cell', 'tm'))]
    all_to_all x3 -> x0, waiting for transfers between devices: 26.7 us -> none  [the longest x1 11.1 us: local(): lax.all_to_all(w_send.reshape(n_source, cap * directions), 'cell', split_...]
    all_to_all x3 -> x0, starting transfers between devices: 17 us -> none  [the longest x1 6.56 us: local(): lax.all_to_all(stack, 'tm', split_axis=0, concat_axis=0, tiled=True)]
    all_to_all x1, waiting for transfers between devices: 3.59 us -> 0.01 us  [local(): lax.all_to_all(copies, 'tm', split_axis=0, concat_axis=0, tiled=True)]
  transfers between devices with their start and end apart: 5 -> 3, of which waited for: 5 -> 2; matrix products, arithmetic and copies ran while one was open for 7% -> 3% of each run, Pallas kernels for 0% -> 0%
where the time goes in v7:
time: 335 us; the launch traced here: 334 us
  waiting for transfers between devices  274 us (82%)
  starting transfers between devices  22.1 us (7%)
  between operations  14.4 us (4%)
  local copies, waits for them, and re-layouts  11.5 us (3%)
  matrix products  8.63 us (3%)
    psum x1, waiting for transfers between devices, local(): total = lax.psum(total, ('cell', 'tm'))  263 us
    all_to_all x1, starting transfers between devices, local(): recv = lax.all_to_all(send, 'cell', split_axis=0, concat_axis=0, tiled=True)  11.8 us
    all_to_all x1, waiting for transfers between devices, local(): recv = lax.all_to_all(send, 'cell', split_axis=0, concat_axis=0, tiled=True)  11.5 us
    all_to_all x1, starting transfers between devices, local(): lax.all_to_all(copies, 'tm', split_axis=0, concat_axis=0, tiled=True)  10.3 us
  transfers between devices with their start and end apart: 3, of which 2 were waited for; matrix products, arithmetic and copies ran while one was open for 3% of the time, Pallas kernels for 0%

profile of v7, /device:TPU:1, one launch (start us, length us, event | category | flops | bytes accessed | tf_op | source)
XLA Modules:
  0.0 334.2 jit_solution(1137493657515781644)
XLA Ops:
  7.2 1.0 copy.66
  8.2 0.9 broadcast_in_dim.33
  9.1 10.3 %all-to-all-start.1 = ((bf16[8,4,16,512]{3,1,2,0:T(4,128)(2,1)}), bf16[8,4,16,512]{3,1,2,0:T(4,128)(2,1)S(1)}, u32[]{:S(2)}, u32[]{:S(2)}) async-start(bf16[8,4,16,512]{3,1,2,0:T(4,128)(2,1)} %broadcast_in_dim.33), calls=%async_computation.1 | async-start | bytes 1048576 | tf_op jit(solution)/shard_map/all_to_all | solution.py:55
  19.4 0.9 reshape.245
  20.2 0.7 iota_compare_fusion.11
  21.1 0.8 copy.62
  22.0 0.3 fusion.9
  22.3 0.5 fusion.8
  23.1 0.2 select_reduce_fusion
  23.7 1.4 fusion.2
  25.1 1.4 fusion
  26.6 0.5 broadcast.164
  27.1 0.8 reduce
  27.9 1.0 reshape.261
  28.9 11.8 %all-to-all-start = ((bf16[64,2,1088]{2,1,0:T(2,128)(2,1)}), bf16[64,2,1088]{2,1,0:T(2,128)(2,1)S(1)}, u32[]{:S(2)}, u32[]{:S(2)}) async-start(bf16[64,2,1088]{2,1,0:T(2,128)(2,1)} %reshape.261), calls=%async_computation | async-start | bytes 589824 | tf_op jit(solution)/shard_map/all_to_all | solution.py:50
  41.0 0.2 copy.67
  41.3 1.0 fusion.33
  42.4 11.5 %all-to-all-done = bf16[64,2,1088]{2,1,0:T(2,128)(2,1)S(1)} async-done(((bf16[64,2,1088]{2,1,0:T(2,128)(2,1)}), bf16[64,2,1088]{2,1,0:T(2,128)(2,1)S(1)}, u32[]{:S(2)}, u32[]{:S(2)}) %all-to-all-start) | async-done | bytes 278560 | tf_op jit(solution)/shard_map/all_to_all | solution.py:50
  53.9 0.3 reshape.262
  54.7 0.3 fusion.7
  55.2 1.6 fusion.16
  56.8 0.6 reshape.248
  57.4 0.7 pad_maximum_fusion
  58.2 263.0 %all-reduce.2.cloned.1.call-done = f32[544,128]{1,0:T(8,128)} async-done(((f32[544,128]{1,0:T(8,128)}), f32[544,128]{1,0:T(8,128)}) %all-reduce.2.cloned.1.call-update) | async-done | bytes 278544 | tf_op jit(solution)/shard_map/psum | solution.py:82
  321.1 1.0 slice.23
  322.1 0.6 reshape.250
  322.7 0.7 copy.71
  323.5 1.6 fusion.4
  325.3 0.3 broadcast_multiply_fusion
  325.5 0.4 mul.87
  325.9 0.6 fusion.40
  326.7 0.7 copy.75
  (53 shorter events, 2.5 us)
Async XLA Ops:
  7.2 15.1 %copy-start = (bf16[64,8,128]{2,1,0:T(8,128)(2,1)S(1)}, bf16[64,8,128]{2,1,0:T(8,128)(2,1)}, u32[]{:S(2)}) copy-start(bf16[64,8,128]{2,1,0:T(8,128)(2,1)} %param.9) | copy-start | bytes 393220
  7.2 15.7 %copy-start.2 = (s32[1,64,2]{1,2,0:T(2,128)S(1)}, s32[1,64,2]{1,2,0:T(2,128)}, u32[]{:S(2)}) copy-start(s32[1,64,2]{1,2,0:T(2,128)} %param.13) | copy-start | bytes 1540
  7.2 16.3 %copy-start.1 = (s32[64,8]{0,1:T(8,128)S(1)}, s32[64,8]{0,1:T(8,128)}, u32[]{:S(2)}) copy-start(s32[64,8]{0,1:T(8,128)} %param.11) | copy-start | bytes 6148
  9.1 19.8 %all-to-all-start.1 = ((bf16[8,4,16,512]{3,1,2,0:T(4,128)(2,1)}), bf16[8,4,16,512]{3,1,2,0:T(4,128)(2,1)S(1)}, u32[]{:S(2)}, u32[]{:S(2)}) async-start(bf16[8,4,16,512]{3,1,2,0:T(4,128)(2,1)} %broadcast_in_dim.33), calls=%async_computation.1 | async-start | bytes 1048576 | tf_op jit(solution)/shard_map/all_to_all | solution.py:55
  23.5 17.3 %copy-start.3 = (f32[64]{0:T(128)S(1)}, f32[64]{0:T(128)}, u32[]{:S(2)}) copy-start(f32[64]{0:T(128)} %param.14) | copy-start | bytes 772
  28.9 25.0 %all-to-all-start = ((bf16[64,2,1088]{2,1,0:T(2,128)(2,1)}), bf16[64,2,1088]{2,1,0:T(2,128)(2,1)S(1)}, u32[]{:S(2)}, u32[]{:S(2)}) async-start(bf16[64,2,1088]{2,1,0:T(2,128)(2,1)} %reshape.261), calls=%async_computation | async-start | bytes 589824 | tf_op jit(solution)/shard_map/all_to_all | solution.py:50
  40.7 280.4 %all-reduce.2.cloned.1.call-start = ((), (), s32[]{:S(2)}) async-start(), calls=%async_computation.2 | async-start | bytes 557056 | tf_op jit(solution)/shard_map/psum | solution.py:82
  321.1 2.3 slice-start
Sparse Core Ops, SparseCore 0:
  58.2 262.8 all-reduce.1

commit v8 on v6

--- a/solution.py
+++ b/solution.py
@@ -1,10 +1,19 @@
 import jax
 import jax.numpy as jnp
 from jax import lax
-from jax.sharding import PartitionSpec as P
+from jax.sharding import Mesh, PartitionSpec as P
 
 TILE = 128
 HI = lax.Precision.HIGHEST
+
+
+def cell_exchange(x):
+    rows = x.shape[0]
+    side = lax.axis_size("cz")
+    x = x.reshape((side, rows // side) + x.shape[1:])
+    x = lax.all_to_all(x, "cy", split_axis=1, concat_axis=1, tiled=True)
+    x = lax.all_to_all(x, "cz", split_axis=0, concat_axis=0, tiled=True)
+    return x.reshape((rows,) + x.shape[2:])
 
 
 def local(flux, foot, block_slot, block_time, block_count, request_tiles, obs_weight, prior):
@@ -42,7 +51,7 @@
     meta_send = meta_send.reshape(n_source, cap).astype(jnp.bfloat16)
     meta_pad = jnp.zeros((n_source, TILE - cap), jnp.bfloat16)
     send = jnp.concatenate([foot_send.reshape(n_source, cap * TILE), meta_send, meta_pad], axis=1)
-    recv = lax.all_to_all(send, "cell", split_axis=0, concat_axis=0, tiled=True)
+    recv = cell_exchange(send)
 
     my_group = lax.axis_index("tm")
     groups = lax.axis_size("tm")
@@ -60,9 +69,7 @@
     panel = lax.dynamic_slice(prior, (my_group * slices, 0), (slices, groups * slices))
     coupled = jnp.einsum("ts,skn->tkn", panel, flux_all, precision=HI)
     coupled, partial = lax.optimization_barrier((coupled, partial))
-    back = lax.all_to_all(
-        partial.reshape(n_source, cap * directions), "cell", split_axis=0, concat_axis=0, tiled=True
-    ).reshape(n_slot, directions)
+    back = cell_exchange(partial.reshape(n_source, cap * directions)).reshape(n_slot, directions)
 
     place_f = place.astype(f32)
     per_block = jnp.dot(place_f.T, back, precision=HI, preferred_element_type=f32)
@@ -72,9 +79,7 @@
     weighted = obs_weight[:, None] * images
     w_block = jnp.repeat(weighted, nb, axis=0)
     w_send = jnp.dot(place_f, w_block, precision=HI, preferred_element_type=f32)
-    w_recv = lax.all_to_all(
-        w_send.reshape(n_source, cap * directions), "cell", split_axis=0, concat_axis=0, tiled=True
-    ).reshape(n_slot, directions)
+    w_recv = cell_exchange(w_send.reshape(n_source, cap * directions)).reshape(n_slot, directions)
 
     hot_tt = meta_hot.reshape(n_slot, tiles, slices).transpose(0, 2, 1)
     w_meta = (hot_tt[:, :, None, :] * w_recv[:, None, :, None]).reshape(n_slot, n_meta * directions)
@@ -86,15 +91,19 @@
 
 
 def solution(mesh):
+    n_cell, n_tm = mesh.devices.shape
+    cz = int(round(n_cell ** 0.5))
+    grid = Mesh(mesh.devices.reshape(cz, n_cell // cz, n_tm), ("cz", "cy", "tm"))
+    cell = ("cz", "cy")
     in_specs = (
-        P("tm", None, "cell"),
-        P("cell", "tm", None),
-        P("cell", "tm"),
-        P("cell", "tm"),
-        P("cell", "tm"),
-        P("cell", None, None),
-        P("cell"),
+        P("tm", None, cell),
+        P(cell, "tm", None),
+        P(cell, "tm"),
+        P(cell, "tm"),
+        P(cell, "tm"),
+        P(cell, None, None),
+        P(cell),
         P(),
     )
-    out_specs = (P("cell", None), P("tm", None, "cell"))
-    return jax.shard_map(local, mesh=mesh, in_specs=in_specs, out_specs=out_specs, check_vma=False)
+    out_specs = (P(cell, None), P("tm", None, cell))
+    return jax.shard_map(local, mesh=grid, in_specs=in_specs, out_specs=out_specs, check_vma=False)

time: 102 us -> 130 us (1.27)
  waiting for transfers between devices: 41.8 us -> 55.6 us
  blocking collectives: 0 us -> 12 us
  local copies, waits for them, and re-layouts: 10.6 us -> 12.2 us
    all_to_all x0 -> x1, blocking collectives: none -> 12 us  [local(): lax.all_to_all(stack, 'tm', split_axis=0, concat_axis=0, tiled=True)]
    all_to_all x4 -> x6, waiting for transfers between devices: 38.2 us -> 46.9 us  [the longest x3 23.7 us: cell_exchange(): x = lax.all_to_all(x, 'cy', split_axis=1, concat_axis=1, tiled=True)]
    all_to_all x1, waiting for transfers between devices: 3.59 us -> 8.74 us  [local(): lax.all_to_all(copies, 'tm', split_axis=0, concat_axis=0, tiled=True)]
    all_to_all x1, starting transfers between devices: 10.3 us -> 7.86 us  [local(): lax.all_to_all(copies, 'tm', split_axis=0, concat_axis=0, tiled=True)]
    all_to_all x4 -> x6, starting transfers between devices: 28.8 us -> 31.1 us  [the longest x3 16.7 us: cell_exchange(): x = lax.all_to_all(x, 'cz', split_axis=0, concat_axis=0, tiled=True)]
    another operation x0 -> x5, local copies, waits for them, and re-layouts: none -> 1.98 us  [the longest x4 1.79 us: cell_exchange(): x = x.reshape((side, rows // side) + x.shape[1:])]
    unnamed x27 -> x18, local copies, waits for them, and re-layouts: 4.11 us -> 3.29 us
  transfers between devices with their start and end apart: 5 -> 7, of which waited for: 5 -> 7; matrix products, arithmetic and copies ran while one was open for 7% -> 2% of each run, Pallas kernels for 0% -> 0%
where the time goes in v8:
time: 130 us; the launch traced here: 128 us
  waiting for transfers between devices  55.6 us (43%)
  starting transfers between devices  38.9 us (30%)
  local copies, waits for them, and re-layouts  12.2 us (9%)
  blocking collectives  12 us (9%)
  matrix products  6.24 us (5%)
  other arithmetic  2.34 us (2%)
    all_to_all x3, waiting for transfers between devices, cell_exchange(): x = lax.all_to_all(x, 'cy', split_axis=1, concat_axis=1, tiled=True)  23.7 us
    all_to_all x3, waiting for transfers between devices, cell_exchange(): x = lax.all_to_all(x, 'cz', split_axis=0, concat_axis=0, tiled=True)  23.2 us
    all_to_all x3, starting transfers between devices, cell_exchange(): x = lax.all_to_all(x, 'cz', split_axis=0, concat_axis=0, tiled=True)  16.7 us
    all_to_all x3, starting transfers between devices, cell_exchange(): x = lax.all_to_all(x, 'cy', split_axis=1, concat_axis=1, tiled=True)  14.4 us
    all_to_all x1, blocking collectives, local(): lax.all_to_all(stack, 'tm', split_axis=0, concat_axis=0, tiled=True)  12 us
    all_to_all x1, waiting for transfers between devices, local(): lax.all_to_all(copies, 'tm', split_axis=0, concat_axis=0, tiled=True)  8.74 us
    all_to_all x1, starting transfers between devices, local(): lax.all_to_all(copies, 'tm', split_axis=0, concat_axis=0, tiled=True)  7.86 us
    unnamed x18, local copies, waits for them, and re-layouts  3.29 us
  transfers between devices with their start and end apart: 7, of which 7 were waited for; matrix products, arithmetic and copies ran while one was open for 2% of the time, Pallas kernels for 0%

profile of v8, /device:TPU:1, one launch (start us, length us, event | category | flops | bytes accessed | tf_op | source)
XLA Modules:
  0.0 128.4 jit_solution(2563969838534140600)
XLA Ops:
  0.7 0.8 iota_compare_fusion.11
  1.5 0.8 copy.115
  2.7 0.8 copy.123
  3.5 0.8 copy.122
  4.9 1.4 %fusion.5 = f32[1,64,16]{2,0,1:T(1,128)S(1)} fusion(bf16[512,1,1]{0,1,2:T(2,128)(2,1)S(1)} %reshape.252, s32[64,16]{1,0:T(8,128)S(1)} %multiply_add_fusion, s32[512]{0:T(512)S(1)} %add_select_fusion.2), kind=kOutput, calls=%fused_computation.6 | convolution fusion | flops 1572864 | bytes 11264 | tf_op jit(solution)/shard_map/dot_general | solution.py:50
  7.1 0.8 concatenate.10
  7.8 7.7 %all-to-all-start.1 = ((bf16[8,8,2176]{2,0,1:T(8,128)(2,1)}), bf16[8,8,2176]{2,0,1:T(8,128)(2,1)S(1)}, u32[]{:S(2)}, u32[]{:S(2)}) async-start(bf16[8,8,2176]{2,0,1:T(8,128)(2,1)} %concatenate.10), calls=%async_computation.1 | async-start | bytes 557056 | tf_op jit(solution)/shard_map/all_to_all | solution.py:14
  15.6 9.5 %all-to-all-done.1 = bf16[8,8,2176]{2,0,1:T(8,128)(2,1)S(1)} async-done(((bf16[8,8,2176]{2,0,1:T(8,128)(2,1)}), bf16[8,8,2176]{2,0,1:T(8,128)(2,1)S(1)}, u32[]{:S(2)}, u32[]{:S(2)}) %all-to-all-start.1) | async-done | bytes 278560 | tf_op jit(solution)/shard_map/all_to_all | solution.py:14
  25.1 0.9 broadcast_in_dim.29
  26.0 7.9 %all-to-all-start = ((bf16[8,4,16,512]{3,1,2,0:T(4,128)(2,1)}), bf16[8,4,16,512]{3,1,2,0:T(4,128)(2,1)S(1)}, u32[]{:S(2)}, u32[]{:S(2)}) async-start(bf16[8,4,16,512]{3,1,2,0:T(4,128)(2,1)} %broadcast_in_dim.29), calls=%async_computation | async-start | bytes 1048576 | tf_op jit(solution)/shard_map/all_to_all | solution.py:59
  33.9 0.7 copy.126
  34.6 8.7 %all-to-all-done = bf16[8,4,16,512]{3,1,2,0:T(4,128)(2,1)S(1)} async-done(((bf16[8,4,16,512]{3,1,2,0:T(4,128)(2,1)}), bf16[8,4,16,512]{3,1,2,0:T(4,128)(2,1)S(1)}, u32[]{:S(2)}, u32[]{:S(2)}) %all-to-all-start) | async-done | bytes 524320 | tf_op jit(solution)/shard_map/all_to_all | solution.py:59
  43.4 10.0 %all-to-all-start.2 = ((bf16[8,8,2176]{2,1,0:T(8,128)(2,1)}), bf16[8,8,2176]{2,1,0:T(8,128)(2,1)S(1)}, u32[]{:S(2)}, u32[]{:S(2)}) async-start(bf16[8,8,2176]{2,1,0:T(8,128)(2,1)} %copy.126), calls=%async_computation.2 | async-start | bytes 557056 | tf_op jit(solution)/shard_map/all_to_all | solution.py:15
  53.8 1.0 fusion.34
  54.8 9.0 %all-to-all-done.2 = bf16[8,8,2176]{2,1,0:T(8,128)(2,1)S(1)} async-done(((bf16[8,8,2176]{2,1,0:T(8,128)(2,1)}), bf16[8,8,2176]{2,1,0:T(8,128)(2,1)S(1)}, u32[]{:S(2)}, u32[]{:S(2)}) %all-to-all-start.2) | async-done | bytes 278560 | tf_op jit(solution)/shard_map/all_to_all | solution.py:15
  64.8 0.7 copy.129
  65.5 3.4 %all-to-all-start.3 = ((f32[8,8,256]{2,0,1:T(8,128)}), f32[8,8,256]{2,0,1:T(8,128)S(1)}, u32[]{:S(2)}, u32[]{:S(2)}) async-start(f32[8,8,256]{2,0,1:T(8,128)} %copy.129), calls=%async_computation.3 | async-start | bytes 131072 | tf_op jit(solution)/shard_map/all_to_all | solution.py:14
  69.0 7.1 %all-to-all-done.3 = f32[8,8,256]{2,0,1:T(8,128)S(1)} async-done(((f32[8,8,256]{2,0,1:T(8,128)}), f32[8,8,256]{2,0,1:T(8,128)S(1)}, u32[]{:S(2)}, u32[]{:S(2)}) %all-to-all-start.3) | async-done | bytes 65568 | tf_op jit(solution)/shard_map/all_to_all | solution.py:14
  76.1 0.7 copy.130
  76.8 3.4 %all-to-all-start.4 = ((f32[8,8,256]{2,1,0:T(8,128)}), f32[8,8,256]{2,1,0:T(8,128)S(1)}, u32[]{:S(2)}, u32[]{:S(2)}) async-start(f32[8,8,256]{2,1,0:T(8,128)} %copy.130), calls=%async_computation.4 | async-start | bytes 131072 | tf_op jit(solution)/shard_map/all_to_all | solution.py:15
  80.2 7.1 %all-to-all-done.4 = f32[8,8,256]{2,1,0:T(8,128)S(1)} async-done(((f32[8,8,256]{2,1,0:T(8,128)}), f32[8,8,256]{2,1,0:T(8,128)S(1)}, u32[]{:S(2)}, u32[]{:S(2)}) %all-to-all-start.4) | async-done | bytes 65568 | tf_op jit(solution)/shard_map/all_to_all | solution.py:15
  87.5 1.1 fusion.9
  88.8 12.0 %all_to_all.40 = f32[8,1,1024]{2,1,0:T(1,128)S(1)} all-to-all(f32[8,1,1024]{2,1,0:T(1,128)S(1)} %reshape.258), channel_id=1, replica_groups=mesh['cz'=8,'cy'=8,'tm'=8] {'tm'}, dimensions={0} | all-to-all | bytes 65536 | tf_op jit(solution)/shard_map/all_to_all | solution.py:78
  101.3 0.7 reduce
  102.3 1.0 fusion
  103.6 0.7 copy.135
  104.2 3.4 %all-to-all-start.6 = ((f32[8,8,256]{2,0,1:T(8,128)}), f32[8,8,256]{2,0,1:T(8,128)S(1)}, u32[]{:S(2)}, u32[]{:S(2)}) async-start(f32[8,8,256]{2,0,1:T(8,128)} %copy.135), calls=%async_computation.6 | async-start | bytes 131072 | tf_op jit(solution)/shard_map/all_to_all | solution.py:14
  107.7 7.0 %all-to-all-done.6 = f32[8,8,256]{2,0,1:T(8,128)S(1)} async-done(((f32[8,8,256]{2,0,1:T(8,128)}), f32[8,8,256]{2,0,1:T(8,128)S(1)}, u32[]{:S(2)}, u32[]{:S(2)}) %all-to-all-start.6) | async-done | bytes 65568 | tf_op jit(solution)/shard_map/all_to_all | solution.py:14
  114.7 0.7 copy.136
  115.4 3.4 %all-to-all-start.7 = ((f32[8,8,256]{2,1,0:T(8,128)}), f32[8,8,256]{2,1,0:T(8,128)S(1)}, u32[]{:S(2)}, u32[]{:S(2)}) async-start(f32[8,8,256]{2,1,0:T(8,128)} %copy.136), calls=%async_computation.7 | async-start | bytes 131072 | tf_op jit(solution)/shard_map/all_to_all | solution.py:15
  118.8 7.2 %all-to-all-done.7 = f32[8,8,256]{2,1,0:T(8,128)S(1)} async-done(((f32[8,8,256]{2,1,0:T(8,128)}), f32[8,8,256]{2,1,0:T(8,128)S(1)}, u32[]{:S(2)}, u32[]{:S(2)}) %all-to-all-start.7) | async-done | bytes 65568 | tf_op jit(solution)/shard_map/all_to_all | solution.py:15
  127.7 0.7 copy.139
  (64 shorter events, 6.7 us)
Async XLA Ops:
  0.6 5.7 %copy-start = (bf16[64,8,128]{2,1,0:T(8,128)(2,1)S(1)}, bf16[64,8,128]{2,1,0:T(8,128)(2,1)}, u32[]{:S(2)}) copy-start(bf16[64,8,128]{2,1,0:T(8,128)(2,1)} %param.9) | copy-start | bytes 393220
  6.8 8.7 %copy-start.1 = (bf16[4,16,512]{2,1,0:T(8,128)(2,1)S(1)}, bf16[4,16,512]{2,1,0:T(8,128)(2,1)}, u32[]{:S(2)}) copy-start(bf16[4,16,512]{2,1,0:T(8,128)(2,1)} %param.8) | copy-start | bytes 196612
  7.8 17.3 %all-to-all-start.1 = ((bf16[8,8,2176]{2,0,1:T(8,128)(2,1)}), bf16[8,8,2176]{2,0,1:T(8,128)(2,1)S(1)}, u32[]{:S(2)}, u32[]{:S(2)}) async-start(bf16[8,8,2176]{2,0,1:T(8,128)(2,1)} %concatenate.10), calls=%async_computation.1 | async-start | bytes 557056 | tf_op jit(solution)/shard_map/all_to_all | solution.py:14
  26.0 17.3 %all-to-all-start = ((bf16[8,4,16,512]{3,1,2,0:T(4,128)(2,1)}), bf16[8,4,16,512]{3,1,2,0:T(4,128)(2,1)S(1)}, u32[]{:S(2)}, u32[]{:S(2)}) async-start(bf16[8,4,16,512]{3,1,2,0:T(4,128)(2,1)} %broadcast_in_dim.29), calls=%async_computation | async-start | bytes 1048576 | tf_op jit(solution)/shard_map/all_to_all | solution.py:59
  43.4 20.5 %all-to-all-start.2 = ((bf16[8,8,2176]{2,1,0:T(8,128)(2,1)}), bf16[8,8,2176]{2,1,0:T(8,128)(2,1)S(1)}, u32[]{:S(2)}, u32[]{:S(2)}) async-start(bf16[8,8,2176]{2,1,0:T(8,128)(2,1)} %copy.126), calls=%async_computation.2 | async-start | bytes 557056 | tf_op jit(solution)/shard_map/all_to_all | solution.py:15
  64.4 15.7 %copy-start.3 = (s32[64,1]{0,1:T(1,128)S(1)}, s32[64,1]{0,1:T(1,128)}, u32[]{:S(2)}) copy-start(s32[64,1]{0,1:T(1,128)} %param.12) | copy-start | bytes 772
  65.5 10.6 %all-to-all-start.3 = ((f32[8,8,256]{2,0,1:T(8,128)}), f32[8,8,256]{2,0,1:T(8,128)S(1)}, u32[]{:S(2)}, u32[]{:S(2)}) async-start(f32[8,8,256]{2,0,1:T(8,128)} %copy.129), calls=%async_computation.3 | async-start | bytes 131072 | tf_op jit(solution)/shard_map/all_to_all | solution.py:14
  76.8 10.5 %all-to-all-start.4 = ((f32[8,8,256]{2,1,0:T(8,128)}), f32[8,8,256]{2,1,0:T(8,128)S(1)}, u32[]{:S(2)}, u32[]{:S(2)}) async-start(f32[8,8,256]{2,1,0:T(8,128)} %copy.130), calls=%async_computation.4 | async-start | bytes 131072 | tf_op jit(solution)/shard_map/all_to_all | solution.py:15
  80.2 22.0 %copy-start.4 = (f32[64]{0:T(128)S(1)}, f32[64]{0:T(128)}, u32[]{:S(2)}) copy-start(f32[64]{0:T(128)} %param.14) | copy-start | bytes 772
  102.2 5.5 %copy-start.2 = (f32[64,16]{0,1:T(8,128)}, f32[64,16]{0,1:T(8,128)S(1)}, u32[]{:S(2)}) copy-start(f32[64,16]{0,1:T(8,128)S(1)} %bitcast_reduce_fusion) | copy-start | bytes 12292
  104.2 10.5 %all-to-all-start.6 = ((f32[8,8,256]{2,0,1:T(8,128)}), f32[8,8,256]{2,0,1:T(8,128)S(1)}, u32[]{:S(2)}, u32[]{:S(2)}) async-start(f32[8,8,256]{2,0,1:T(8,128)} %copy.135), calls=%async_computation.6 | async-start | bytes 131072 | tf_op jit(solution)/shard_map/all_to_all | solution.py:14
  115.4 10.6 %all-to-all-start.7 = ((f32[8,8,256]{2,1,0:T(8,128)}), f32[8,8,256]{2,1,0:T(8,128)S(1)}, u32[]{:S(2)}, u32[]{:S(2)}) async-start(f32[8,8,256]{2,1,0:T(8,128)} %copy.136), calls=%async_computation.7 | async-start | bytes 131072 | tf_op jit(solution)/shard_map/all_to_all | solution.py:15

commit v9 on v6

--- a/solution.py
+++ b/solution.py
@@ -59,26 +59,39 @@
     partial = jnp.sum(every * meta_hot[:, :, None], axis=1)
     panel = lax.dynamic_slice(prior, (my_group * slices, 0), (slices, groups * slices))
     coupled = jnp.einsum("ts,skn->tkn", panel, flux_all, precision=HI)
-    coupled, partial = lax.optimization_barrier((coupled, partial))
+    place_f = place.astype(f32)
+    foot_w = foot_r.astype(f32)
+    keep = (coupled, meta_hot, foot_w, place_f)
+    partial, keep = lax.optimization_barrier((partial, keep))
     back = lax.all_to_all(
         partial.reshape(n_source, cap * directions), "cell", split_axis=0, concat_axis=0, tiled=True
     ).reshape(n_slot, directions)
+    back, keep = lax.optimization_barrier((back, keep))
+    coupled, meta_hot, foot_w, place_f = keep
 
-    place_f = place.astype(f32)
     per_block = jnp.dot(place_f.T, back, precision=HI, preferred_element_type=f32)
     partial_value = per_block.reshape(sounds, nb, directions).sum(axis=1)
     stack = jnp.broadcast_to(partial_value[None], (groups,) + partial_value.shape)
-    images = lax.all_to_all(stack, "tm", split_axis=0, concat_axis=0, tiled=True).sum(axis=0)
+    keep = (coupled, meta_hot, foot_w, place_f)
+    stack, keep = lax.optimization_barrier((stack, keep))
+    gathered = lax.all_to_all(stack, "tm", split_axis=0, concat_axis=0, tiled=True)
+    gathered, keep = lax.optimization_barrier((gathered, keep))
+    coupled, meta_hot, foot_w, place_f = keep
+    images = gathered.sum(axis=0)
     weighted = obs_weight[:, None] * images
     w_block = jnp.repeat(weighted, nb, axis=0)
     w_send = jnp.dot(place_f, w_block, precision=HI, preferred_element_type=f32)
+    hot_tt = meta_hot.reshape(n_slot, tiles, slices).transpose(0, 2, 1)
+    keep = (coupled, hot_tt, foot_w)
+    w_send, keep = lax.optimization_barrier((w_send, keep))
     w_recv = lax.all_to_all(
         w_send.reshape(n_source, cap * directions), "cell", split_axis=0, concat_axis=0, tiled=True
     ).reshape(n_slot, directions)
+    w_recv, keep = lax.optimization_barrier((w_recv, keep))
+    coupled, hot_tt, foot_w = keep
 
-    hot_tt = meta_hot.reshape(n_slot, tiles, slices).transpose(0, 2, 1)
     w_meta = (hot_tt[:, :, None, :] * w_recv[:, None, :, None]).reshape(n_slot, n_meta * directions)
-    adj = jnp.dot(w_meta.T, foot_r.astype(f32), precision=HI, preferred_element_type=f32)
+    adj = jnp.dot(w_meta.T, foot_w, precision=HI, preferred_element_type=f32)
     adjoint = adj.reshape(slices, directions, cell_count)
 
     hess = adjoint + coupled

time: 102 us -> 106 us (1.039)
  blocking collectives: 0 us -> 41.7 us
  waiting for transfers between devices: 41.8 us -> 12.9 us
  starting transfers between devices: 39.1 us -> 22.3 us
  matrix products: 6.25 us -> 10.7 us
  local copies, waits for them, and re-layouts: 10.6 us -> 13 us
    all_to_all x0 -> x3, blocking collectives: none -> 41.7 us  [the longest x1 16.7 us: local(): lax.all_to_all(partial.reshape(n_source, cap * directions), 'cell', split...]
    all_to_all x3 -> x0, waiting for transfers between devices: 26.7 us -> none  [the longest x1 11.1 us: local(): lax.all_to_all(w_send.reshape(n_source, cap * directions), 'cell', split_...]
    all_to_all x3 -> x0, starting transfers between devices: 17 us -> none  [the longest x1 6.56 us: local(): lax.all_to_all(stack, 'tm', split_axis=0, concat_axis=0, tiled=True)]
    dot_general x1, matrix products: 1.13 us -> 3.43 us  [local(): jnp.dot(place_f.T, back, precision=HI, preferred_element_type=f32)]
    unnamed x27 -> x23, local copies, waits for them, and re-layouts: 4.11 us -> 6.29 us
    all_to_all x1, waiting for transfers between devices: 3.59 us -> 2.27 us  [local(): lax.all_to_all(copies, 'tm', split_axis=0, concat_axis=0, tiled=True)]
  transfers between devices with their start and end apart: 5 -> 2, of which waited for: 5 -> 2; matrix products, arithmetic and copies ran while one was open for 7% -> 9% of each run, Pallas kernels for 0% -> 0%
where the time goes in v9:
time: 106 us; the launch traced here: 105 us
  blocking collectives  41.7 us (39%)
  starting transfers between devices  22.3 us (21%)
  local copies, waits for them, and re-layouts  13 us (12%)
  waiting for transfers between devices  12.9 us (12%)
  matrix products  10.7 us (10%)
  other arithmetic  3.59 us (3%)
    all_to_all x1, blocking collectives, local(): lax.all_to_all(partial.reshape(n_source, cap * directions), 'cell', split...  16.7 us
    all_to_all x1, blocking collectives, local(): lax.all_to_all(w_send.reshape(n_source, cap * directions), 'cell', split_...  14.9 us
    all_to_all x1, starting transfers between devices, local(): recv = lax.all_to_all(send, 'cell', split_axis=0, concat_axis=0, tiled=True)  12 us
    all_to_all x1, waiting for transfers between devices, local(): recv = lax.all_to_all(send, 'cell', split_axis=0, concat_axis=0, tiled=True)  10.6 us
    all_to_all x1, starting transfers between devices, local(): lax.all_to_all(copies, 'tm', split_axis=0, concat_axis=0, tiled=True)  10.3 us
    all_to_all x1, blocking collectives, local(): lax.all_to_all(stack, 'tm', split_axis=0, concat_axis=0, tiled=True)  10 us
    unnamed x23, local copies, waits for them, and re-layouts  6.29 us
    dot_general x1, matrix products, local(): jnp.dot(place_f.T, back, precision=HI, preferred_element_type=f32)  3.43 us
  transfers between devices with their start and end apart: 2, of which 2 were waited for; matrix products, arithmetic and copies ran while one was open for 9% of the time, Pallas kernels for 0%

profile of v9, /device:TPU:1, one launch (start us, length us, event | category | flops | bytes accessed | tf_op | source)
XLA Modules:
  0.0 105.2 jit_solution(5701162062131945306)
XLA Ops:
  0.7 1.0 copy.97
  1.6 0.9 broadcast_in_dim.31
  2.6 10.3 %all-to-all-start.1 = ((bf16[8,4,16,512]{3,1,2,0:T(4,128)(2,1)}), bf16[8,4,16,512]{3,1,2,0:T(4,128)(2,1)S(1)}, u32[]{:S(2)}, u32[]{:S(2)}) async-start(bf16[8,4,16,512]{3,1,2,0:T(4,128)(2,1)} %broadcast_in_dim.31), calls=%async_computation.1 | async-start | bytes 1048576 | tf_op jit(solution)/shard_map/all_to_all | solution.py:50
  12.8 0.7 iota_compare_fusion.9
  13.7 0.8 copy.92
  14.5 0.3 fusion.7
  14.9 0.5 fusion.5
  16.3 1.4 %fusion.2 = f32[1,64,16]{2,0,1:T(1,128)S(1)} fusion(bf16[512,1,1]{0,1,2:T(2,128)(2,1)S(1)} %reshape.229, s32[64,16]{1,0:T(8,128)S(1)} %multiply_add_fusion, s32[512]{0:T(512)S(1)} %add_select_fusion.1), kind=kOutput, calls=%fused_computation.3 | convolution fusion | flops 1572864 | bytes 11264 | tf_op jit(solution)/shard_map/dot_general | solution.py:41
  17.8 0.5 broadcast.120
  18.3 0.8 reduce.2
  19.1 1.0 reshape.237
  20.1 2.3 %all-to-all-done.1 = bf16[8,4,16,512]{3,1,2,0:T(4,128)(2,1)S(1)} async-done(((bf16[8,4,16,512]{3,1,2,0:T(4,128)(2,1)}), bf16[8,4,16,512]{3,1,2,0:T(4,128)(2,1)S(1)}, u32[]{:S(2)}, u32[]{:S(2)}) %all-to-all-start.1) | async-done | bytes 524320 | tf_op jit(solution)/shard_map/all_to_all | solution.py:50
  22.3 12.0 %all-to-all-start = ((bf16[64,2,1088]{2,1,0:T(2,128)(2,1)}), bf16[64,2,1088]{2,1,0:T(2,128)(2,1)}, u32[]{:S(2)}, u32[]{:S(2)}) async-start(bf16[64,2,1088]{2,1,0:T(2,128)(2,1)} %reshape.237), calls=%async_computation | async-start | bytes 589824 | tf_op jit(solution)/shard_map/all_to_all | solution.py:45
  34.4 0.6 copy.96
  35.1 0.3 fusion
  35.4 0.2 copy.98
  35.7 1.0 fusion.22
  36.8 10.6 %all-to-all-done = bf16[64,2,1088]{2,1,0:T(2,128)(2,1)} async-done(((bf16[64,2,1088]{2,1,0:T(2,128)(2,1)}), bf16[64,2,1088]{2,1,0:T(2,128)(2,1)}, u32[]{:S(2)}, u32[]{:S(2)}) %all-to-all-start) | async-done | bytes 278560 | tf_op jit(solution)/shard_map/all_to_all | solution.py:45
  47.4 2.4 %reshape.238 = bf16[64,1,2176]{2,1,0:T(2,128)(2,1)S(1)} reshape(bf16[64,2,1088]{2,1,0:T(2,128)(2,1)} %all-to-all-done) | data formatting | bytes 557056
  49.8 0.8 reshape.231
  50.9 1.3 %fusion.4 = f32[1024,16]{0,1:T(8,128)S(1)} fusion(bf16[1024,128,1]{1,0,2:T(8,128)(2,1)} %reshape.231, bf16[16,16,128]{2,1,0:T(8,128)(2,1)} %bitcast.53, f32[1024,16]{0,1:T(8,128)S(1)} %fusion.19), kind=kOutput, calls=%fused_computation.6 | convolution fusion | flops 67616768 | bytes 458752 | tf_op jit(solution)/shard_map/dot_general | solution.py:58
  52.6 16.7 %all_to_all.42 = f32[64,1,256]{2,1,0:T(1,128)S(1)} all-to-all(f32[64,1,256]{2,1,0:T(1,128)S(1)} %all_to_all.35), channel_id=1, replica_groups=mesh['cell'=64,'tm'=8] {'cell'}, dimensions={0} | all-to-all | bytes 131072 | tf_op jit(solution)/shard_map/all_to_all | solution.py:66
  69.7 3.4 %fusion.6 = f32[64,16]{1,0:T(8,128)S(1)} fusion(f32[1024,512]{1,0:T(8,128)S(1)} %fusion, f32[1024,16]{1,0:T(8,128)S(1)} %reshape.222), kind=kOutput, calls=%fused_computation.9 | convolution fusion | flops 100670464 | bytes 2166784 | tf_op jit(solution)/shard_map/dot_general | solution.py:72
  73.3 10.0 %all_to_all.43 = f32[8,1,1024]{2,1,0:T(1,128)S(1)} all-to-all(f32[8,1,1024]{2,1,0:T(1,128)S(1)} %reshape.239), channel_id=1, replica_groups=mesh['cell'=64,'tm'=8] {'tm'}, dimensions={0} | all-to-all | bytes 65536 | tf_op jit(solution)/shard_map/all_to_all | solution.py:77
  83.3 0.5 broadcast.121
  83.8 0.7 reduce.3
  84.9 1.9 %fusion.11 = f32[1024,16]{0,1:T(8,128)S(1)} fusion(f32[1024,512]{1,0:T(8,128)S(1)} %fusion, f32[64,16]{1,0:T(8,128)S(1)} %broadcast_multiply_fusion.1), kind=kOutput, calls=%fused_computation.18 | convolution fusion | flops 100663296 | bytes 2166784 | tf_op jit(solution)/shard_map/dot_general | solution.py:83
  87.2 14.9 %all_to_all.44 = f32[64,1,256]{2,1,0:T(1,128)S(1)} all-to-all(f32[64,1,256]{2,1,0:T(1,128)S(1)} %all_to_all.36), channel_id=1, replica_groups=mesh['cell'=64,'tm'=8] {'cell'}, dimensions={0} | all-to-all | bytes 131072 | tf_op jit(solution)/shard_map/all_to_all | solution.py:87
  102.7 0.3 broadcast_multiply_fusion
  103.0 0.4 mul.75
  103.3 1.0 fusion.27
  104.5 0.7 copy.110
  (58 shorter events, 4.0 us)
Async XLA Ops:
  0.6 14.2 %copy-start = (bf16[64,8,128]{2,1,0:T(8,128)(2,1)S(1)}, bf16[64,8,128]{2,1,0:T(8,128)(2,1)}, u32[]{:S(2)}) copy-start(bf16[64,8,128]{2,1,0:T(8,128)(2,1)} %param.9) | copy-start | bytes 393220
  0.6 14.8 %copy-start.4 = (s32[1,64,2]{1,2,0:T(2,128)S(1)}, s32[1,64,2]{1,2,0:T(2,128)}, u32[]{:S(2)}) copy-start(s32[1,64,2]{1,2,0:T(2,128)} %param.13) | copy-start | bytes 1540
  0.7 15.4 %copy-start.3 = (s32[64,8]{0,1:T(8,128)S(1)}, s32[64,8]{0,1:T(8,128)}, u32[]{:S(2)}) copy-start(s32[64,8]{0,1:T(8,128)} %param.11) | copy-start | bytes 6148
  2.6 19.8 %all-to-all-start.1 = ((bf16[8,4,16,512]{3,1,2,0:T(4,128)(2,1)}), bf16[8,4,16,512]{3,1,2,0:T(4,128)(2,1)S(1)}, u32[]{:S(2)}, u32[]{:S(2)}) async-start(bf16[8,4,16,512]{3,1,2,0:T(4,128)(2,1)} %broadcast_in_dim.31), calls=%async_computation.1 | async-start | bytes 1048576 | tf_op jit(solution)/shard_map/all_to_all | solution.py:50
  15.3 19.1 %copy-start.1 = (bf16[4,16,512]{2,1,0:T(8,128)(2,1)S(1)}, bf16[4,16,512]{2,1,0:T(8,128)(2,1)}, u32[]{:S(2)}) copy-start(bf16[4,16,512]{2,1,0:T(8,128)(2,1)} %param.8) | copy-start | bytes 196612
  22.3 25.1 %all-to-all-start = ((bf16[64,2,1088]{2,1,0:T(2,128)(2,1)}), bf16[64,2,1088]{2,1,0:T(2,128)(2,1)}, u32[]{:S(2)}, u32[]{:S(2)}) async-start(bf16[64,2,1088]{2,1,0:T(2,128)(2,1)} %reshape.237), calls=%async_computation | async-start | bytes 589824 | tf_op jit(solution)/shard_map/all_to_all | solution.py:45
  69.3 15.5 %copy-start.5 = (f32[64]{0:T(128)S(1)}, f32[64]{0:T(128)}, u32[]{:S(2)}) copy-start(f32[64]{0:T(128)} %param.14) | copy-start | bytes 772
  84.6 17.9 %copy-start.2 = (f32[64,16]{0,1:T(8,128)}, f32[64,16]{0,1:T(8,128)S(1)}, u32[]{:S(2)}) copy-start(f32[64,16]{0,1:T(8,128)S(1)} %reduce_sum.49) | copy-start | bytes 12292

commit v10 on v6

--- a/solution.py
+++ b/solution.py
@@ -65,20 +65,27 @@
     ).reshape(n_slot, directions)
 
     place_f = place.astype(f32)
-    per_block = jnp.dot(place_f.T, back, precision=HI, preferred_element_type=f32)
-    partial_value = per_block.reshape(sounds, nb, directions).sum(axis=1)
+    of_sound = (row[:, None] // nb == jnp.arange(sounds, dtype=jnp.int32)[None, :]).astype(f32)
+    gather_sound = jnp.dot(of_sound.T, place_f.T, precision=HI, preferred_element_type=f32)
+    slot_weight = jnp.dot(place_f, of_sound * obs_weight[None, :], precision=HI, preferred_element_type=f32)
+    slot_weight = jnp.tile(slot_weight, (1, groups))
+    partial_value = jnp.dot(gather_sound, back, precision=HI, preferred_element_type=f32)
     stack = jnp.broadcast_to(partial_value[None], (groups,) + partial_value.shape)
-    images = lax.all_to_all(stack, "tm", split_axis=0, concat_axis=0, tiled=True).sum(axis=0)
-    weighted = obs_weight[:, None] * images
-    w_block = jnp.repeat(weighted, nb, axis=0)
-    w_send = jnp.dot(place_f, w_block, precision=HI, preferred_element_type=f32)
+    gathered = lax.all_to_all(stack, "tm", split_axis=0, concat_axis=0, tiled=True)
+    images = gathered.sum(axis=0)
+    gathered = gathered.reshape(groups * sounds, directions)
+    w_send = jnp.dot(slot_weight, gathered, precision=HI, preferred_element_type=f32)
     w_recv = lax.all_to_all(
         w_send.reshape(n_source, cap * directions), "cell", split_axis=0, concat_axis=0, tiled=True
     ).reshape(n_slot, directions)
 
-    hot_tt = meta_hot.reshape(n_slot, tiles, slices).transpose(0, 2, 1)
-    w_meta = (hot_tt[:, :, None, :] * w_recv[:, None, :, None]).reshape(n_slot, n_meta * directions)
-    adj = jnp.dot(w_meta.T, foot_r.astype(f32), precision=HI, preferred_element_type=f32)
+    tile_r = meta_r // slices
+    time_r = meta_r % slices
+    hot_time = (time_r[:, None] == jnp.arange(slices, dtype=jnp.int32)[None, :]).astype(f32)
+    hot_tile = (tile_r[:, None] == jnp.arange(tiles, dtype=jnp.int32)[None, :]).astype(f32)
+    foot_tiles = (hot_tile[:, :, None] * foot_r.astype(f32)[:, None, :]).reshape(n_slot, cell_count)
+    w_time = (hot_time[:, :, None] * w_recv[:, None, :]).reshape(n_slot, slices * directions)
+    adj = jnp.dot(w_time.T, foot_tiles, precision=HI, preferred_element_type=f32)
     adjoint = adj.reshape(slices, directions, cell_count)
 
     hess = adjoint + coupled

time: 102 us -> 110 us (1.078)
  matrix products: 6.25 us -> 17.5 us
  waiting for transfers between devices: 41.8 us -> 31.7 us
  other arithmetic: 2.72 us -> 7.64 us
  local copies, waits for them, and re-layouts: 10.6 us -> 12.6 us
    dot_general x3 -> x5, matrix products: 2.78 us -> 14 us  [the longest x1 7.62 us: local(): jnp.dot(slot_weight, gathered, precision=HI, preferred_element_type=f32)]
    all_to_all x1, waiting for transfers between devices: 4.61 us -> 0.89 us  [local(): lax.all_to_all(stack, 'tm', split_axis=0, concat_axis=0, tiled=True)]
    mul x2 -> x1, other arithmetic: 0.26 us -> 3.84 us  [local(): hot_tile[:, :, None] * foot_r.astype(f32)[:, None, :]]
    all_to_all x1, waiting for transfers between devices: 11.1 us -> 8.61 us  [local(): lax.all_to_all(w_send.reshape(n_source, cap * directions), 'cell', split_...]
    all_to_all x1, waiting for transfers between devices: 11.6 us -> 9.16 us  [local(): recv = lax.all_to_all(send, 'cell', split_axis=0, concat_axis=0, tiled=True)]
    mul x4 -> x3, local copies, waits for them, and re-layouts: 0.8 us -> 2.26 us  [the longest x1 1.91 us: local(): hot_tile[:, :, None] * foot_r.astype(f32)[:, None, :]]
    all_to_all x1, waiting for transfers between devices: 3.59 us -> 2.24 us  [local(): lax.all_to_all(copies, 'tm', split_axis=0, concat_axis=0, tiled=True)]
    unnamed x27 -> x21, local copies, waits for them, and re-layouts: 4.11 us -> 4.79 us
  transfers between devices with their start and end apart: 5 -> 5, of which waited for: 5 -> 5; matrix products, arithmetic and copies ran while one was open for 7% -> 16% of each run, Pallas kernels for 0% -> 0%
where the time goes in v10:
time: 110 us
  starting transfers between devices  39.1 us (36%)
  waiting for transfers between devices  31.7 us (29%)
  matrix products  17.5 us (16%)
  local copies, waits for them, and re-layouts  12.6 us (11%)
  other arithmetic  7.64 us (7%)
    all_to_all x1, starting transfers between devices, local(): recv = lax.all_to_all(send, 'cell', split_axis=0, concat_axis=0, tiled=True)  11.8 us
    all_to_all x1, waiting for transfers between devices, local(): lax.all_to_all(partial.reshape(n_source, cap * directions), 'cell', split...  10.8 us
    all_to_all x1, starting transfers between devices, local(): lax.all_to_all(copies, 'tm', split_axis=0, concat_axis=0, tiled=True)  10.3 us
    all_to_all x1, waiting for transfers between devices, local(): recv = lax.all_to_all(send, 'cell', split_axis=0, concat_axis=0, tiled=True)  9.16 us
    all_to_all x1, waiting for transfers between devices, local(): lax.all_to_all(w_send.reshape(n_source, cap * directions), 'cell', split_...  8.61 us
    dot_general x1, matrix products, local(): jnp.dot(slot_weight, gathered, precision=HI, preferred_element_type=f32)  7.62 us
    all_to_all x1, starting transfers between devices, local(): lax.all_to_all(stack, 'tm', split_axis=0, concat_axis=0, tiled=True)  6.56 us
    all_to_all x1, starting transfers between devices, local(): lax.all_to_all(partial.reshape(n_source, cap * directions), 'cell', split...  5.83 us
  transfers between devices with their start and end apart: 5, of which 5 were waited for; matrix products, arithmetic and copies ran while one was open for 16% of the time, Pallas kernels for 0%

profile of v10, /device:TPU:1, one launch (start us, length us, event | category | flops | bytes accessed | tf_op | source)
XLA Modules:
  0.0 109.6 jit_solution(6050342503007916532)
XLA Ops:
  0.7 0.9 copy.59
  1.6 0.9 broadcast_in_dim.25
  2.5 10.3 %all-to-all-start = ((bf16[8,4,16,512]{3,1,2,0:T(4,128)(2,1)}), bf16[8,4,16,512]{3,1,2,0:T(4,128)(2,1)S(1)}, u32[]{:S(2)}, u32[]{:S(2)}) async-start(bf16[8,4,16,512]{3,1,2,0:T(4,128)(2,1)} %broadcast_in_dim.25), calls=%async_computation | async-start | bytes 1048576 | tf_op jit(solution)/shard_map/all_to_all | solution.py:50
  12.8 0.7 iota_compare_fusion.14
  13.6 0.8 copy.58
  16.2 1.4 %fusion.3 = f32[1,64,16]{2,0,1:T(1,128)S(1)} fusion(bf16[512,1,1]{0,1,2:T(2,128)(2,1)S(1)} %reshape.345, s32[64,16]{1,0:T(8,128)S(1)} %multiply_add_fusion, s32[512]{0:T(512)S(1)} %add_select_fusion.4), kind=kOutput, calls=%fused_computation.4 | convolution fusion | flops 1572864 | bytes 11264 | tf_op jit(solution)/shard_map/dot_general | solution.py:41
  17.8 0.5 broadcast.251
  18.3 0.8 reduce.2
  19.0 1.0 reshape.355
  20.1 2.2 %all-to-all-done = bf16[8,4,16,512]{3,1,2,0:T(4,128)(2,1)S(1)} async-done(((bf16[8,4,16,512]{3,1,2,0:T(4,128)(2,1)}), bf16[8,4,16,512]{3,1,2,0:T(4,128)(2,1)S(1)}, u32[]{:S(2)}, u32[]{:S(2)}) %all-to-all-start) | async-done | bytes 524320 | tf_op jit(solution)/shard_map/all_to_all | solution.py:50
  22.3 11.8 %all-to-all-start.1 = ((bf16[64,2,1088]{2,1,0:T(2,128)(2,1)}), bf16[64,2,1088]{2,1,0:T(2,128)(2,1)S(1)}, u32[]{:S(2)}, u32[]{:S(2)}) async-start(bf16[64,2,1088]{2,1,0:T(2,128)(2,1)} %reshape.355), calls=%async_computation.1 | async-start | bytes 589824 | tf_op jit(solution)/shard_map/all_to_all | solution.py:45
  34.1 0.6 fusion.2
  34.8 1.9 %fusion = f32[1024,64]{0,1:T(8,128)} fusion(s32[512]{0:T(512)S(1)} %add_select_fusion.4, f32[64]{0:T(128)S(1)} %copy-done.4, s32[512]{0:T(512)S(1)} %add_select_fusion.3), kind=kOutput, calls=%fused_computation.1 | convolution fusion | flops 403243008 | bytes 266496 | tf_op jit(solution)/shard_map/dot_general | solution.py:70
  37.1 1.0 fusion.40
  38.1 9.2 %all-to-all-done.1 = bf16[64,2,1088]{2,1,0:T(2,128)(2,1)S(1)} async-done(((bf16[64,2,1088]{2,1,0:T(2,128)(2,1)}), bf16[64,2,1088]{2,1,0:T(2,128)(2,1)S(1)}, u32[]{:S(2)}, u32[]{:S(2)}) %all-to-all-start.1) | async-done | bytes 278560 | tf_op jit(solution)/shard_map/all_to_all | solution.py:45
  48.5 0.9 all_to_all.35
  49.4 5.8 %all-to-all-start.2 = ((f32[64,1,256]{2,1,0:T(1,128)}), f32[64,1,256]{2,1,0:T(1,128)S(1)}, u32[]{:S(2)}, u32[]{:S(2)}) async-start(f32[64,1,256]{2,1,0:T(1,128)} %all_to_all.35), calls=%async_computation.2 | async-start | bytes 131072 | tf_op jit(solution)/shard_map/all_to_all | solution.py:63
  55.5 10.8 %all-to-all-done.2 = f32[64,1,256]{2,1,0:T(1,128)S(1)} async-done(((f32[64,1,256]{2,1,0:T(1,128)}), f32[64,1,256]{2,1,0:T(1,128)S(1)}, u32[]{:S(2)}, u32[]{:S(2)}) %all-to-all-start.2) | async-done | bytes 65568 | tf_op jit(solution)/shard_map/all_to_all | solution.py:63
  66.7 0.9 fusion.48
  67.6 0.7 reshape.357
  68.4 6.6 %all-to-all-start.3 = ((f32[8,1,1024]{2,1,0:T(1,128)}), f32[8,1,1024]{2,1,0:T(1,128)S(1)}, u32[]{:S(2)}, u32[]{:S(2)}) async-start(f32[8,1,1024]{2,1,0:T(1,128)} %reshape.357), calls=%async_computation.3 | async-start | bytes 65536 | tf_op jit(solution)/shard_map/all_to_all | solution.py:74
  74.9 3.8 %broadcast_multiply_fusion = f32[1024,4,128]{2,1,0:T(4,128)S(1)} fusion(f32[1024,128]{1,0:T(8,128)S(1)} %convert_element_type.88, f32[1024,4]{1,0:T(8,128)S(1)} %fusion.14), kind=kLoop, calls=%fused_computation.12 | loop fusion | flops 524288 | bytes 2637824 | tf_op jit(solution)/shard_map/mul | solution.py:86
  78.8 0.9 all-to-all-done.3
  80.2 0.7 reduce.3
  81.0 7.6 %convolution_bitcast_fusion = f32[1024,16]{1,0:T(8,128)S(1)} fusion(f32[1024,64]{0,1:T(8,128)} %fusion, f32[8,16,64]{2,1,0:T(8,128)S(1)} %reshape.358), kind=kOutput, calls=%fused_computation.8 | convolution fusion | flops 100663296 | bytes 360448 | tf_op jit(solution)/shard_map/dot_general | solution.py:77
  88.6 0.9 all_to_all.36
  89.5 4.6 %all-to-all-start.4 = ((f32[64,1,256]{2,1,0:T(1,128)}), f32[64,1,256]{2,1,0:T(1,128)S(1)}, u32[]{:S(2)}, u32[]{:S(2)}) async-start(f32[64,1,256]{2,1,0:T(1,128)} %all_to_all.36), calls=%async_computation.4 | async-start | bytes 131072 | tf_op jit(solution)/shard_map/all_to_all | solution.py:78
  94.1 1.9 %reshape.349 = f32[1024,512,1]{1,0,2:T(8,128)} reshape(f32[1024,4,128]{2,1,0:T(4,128)S(1)} %broadcast_multiply_fusion) | data formatting | bytes 4194304 | tf_op jit(solution)/shard_map/mul | solution.py:86
  96.0 0.6 bitcast_reduce_fusion
  96.6 8.6 %all-to-all-done.4 = f32[64,1,256]{2,1,0:T(1,128)S(1)} async-done(((f32[64,1,256]{2,1,0:T(1,128)}), f32[64,1,256]{2,1,0:T(1,128)S(1)}, u32[]{:S(2)}, u32[]{:S(2)}) %all-to-all-start.4) | async-done | bytes 65568 | tf_op jit(solution)/shard_map/all_to_all | solution.py:78
  105.7 3.0 %fusion.15 = f32[4,16,512]{2,1,0:T(8,128)S(1)} fusion(f32[1024,512,1]{1,0,2:T(8,128)} %reshape.349, f32[1024,16]{0,1:T(8,128)S(1)} %copy.69, f32[1024,4]{0,1:T(4,128)S(1)} %fusion.34), kind=kOutput, calls=%fused_computation.23 | convolution fusion | flops 402718720 | bytes 2310144 | tf_op jit(solution)/shard_map/dot_general | solution.py:88
  108.9 0.7 copy.71
  (57 shorter events, 5.4 us)
Async XLA Ops:
  0.6 14.9 %copy-start = (bf16[64,8,128]{2,1,0:T(8,128)(2,1)S(1)}, bf16[64,8,128]{2,1,0:T(8,128)(2,1)}, u32[]{:S(2)}) copy-start(bf16[64,8,128]{2,1,0:T(8,128)(2,1)} %param.9) | copy-start | bytes 393220
  0.6 14.2 %copy-start.3 = (s32[1,64,2]{1,2,0:T(2,128)S(1)}, s32[1,64,2]{1,2,0:T(2,128)}, u32[]{:S(2)}) copy-start(s32[1,64,2]{1,2,0:T(2,128)} %param.13) | copy-start | bytes 1540
  0.7 14.8 %copy-start.2 = (s32[64,8]{0,1:T(8,128)S(1)}, s32[64,8]{0,1:T(8,128)}, u32[]{:S(2)}) copy-start(s32[64,8]{0,1:T(8,128)} %param.11) | copy-start | bytes 6148
  2.5 19.8 %all-to-all-start = ((bf16[8,4,16,512]{3,1,2,0:T(4,128)(2,1)}), bf16[8,4,16,512]{3,1,2,0:T(4,128)(2,1)S(1)}, u32[]{:S(2)}, u32[]{:S(2)}) async-start(bf16[8,4,16,512]{3,1,2,0:T(4,128)(2,1)} %broadcast_in_dim.25), calls=%async_computation | async-start | bytes 1048576 | tf_op jit(solution)/shard_map/all_to_all | solution.py:50
  16.1 18.6 %copy-start.1 = (bf16[4,16,512]{2,1,0:T(8,128)(2,1)S(1)}, bf16[4,16,512]{2,1,0:T(8,128)(2,1)}, u32[]{:S(2)}) copy-start(bf16[4,16,512]{2,1,0:T(8,128)(2,1)} %param.8) | copy-start | bytes 196612
  16.2 18.5 %copy-start.4 = (f32[64]{0:T(128)S(1)}, f32[64]{0:T(128)}, u32[]{:S(2)}) copy-start(f32[64]{0:T(128)} %param.14) | copy-start | bytes 772
  22.3 25.0 %all-to-all-start.1 = ((bf16[64,2,1088]{2,1,0:T(2,128)(2,1)}), bf16[64,2,1088]{2,1,0:T(2,128)(2,1)S(1)}, u32[]{:S(2)}, u32[]{:S(2)}) async-start(bf16[64,2,1088]{2,1,0:T(2,128)(2,1)} %reshape.355), calls=%async_computation.1 | async-start | bytes 589824 | tf_op jit(solution)/shard_map/all_to_all | solution.py:45
  49.4 16.9 %all-to-all-start.2 = ((f32[64,1,256]{2,1,0:T(1,128)}), f32[64,1,256]{2,1,0:T(1,128)S(1)}, u32[]{:S(2)}, u32[]{:S(2)}) async-start(f32[64,1,256]{2,1,0:T(1,128)} %all_to_all.35), calls=%async_computation.2 | async-start | bytes 131072 | tf_op jit(solution)/shard_map/all_to_all | solution.py:63
  68.4 11.3 %all-to-all-start.3 = ((f32[8,1,1024]{2,1,0:T(1,128)}), f32[8,1,1024]{2,1,0:T(1,128)S(1)}, u32[]{:S(2)}, u32[]{:S(2)}) async-start(f32[8,1,1024]{2,1,0:T(1,128)} %reshape.357), calls=%async_computation.3 | async-start | bytes 65536 | tf_op jit(solution)/shard_map/all_to_all | solution.py:74
  89.5 15.8 %all-to-all-start.4 = ((f32[64,1,256]{2,1,0:T(1,128)}), f32[64,1,256]{2,1,0:T(1,128)S(1)}, u32[]{:S(2)}, u32[]{:S(2)}) async-start(f32[64,1,256]{2,1,0:T(1,128)} %all_to_all.36), calls=%async_computation.4 | async-start | bytes 131072 | tf_op jit(solution)/shard_map/all_to_all | solution.py:78

commit v11 on v6

--- a/solution.py
+++ b/solution.py
@@ -40,7 +40,7 @@
     foot_send = jnp.dot(place_b, foot_flat, preferred_element_type=f32).astype(jnp.bfloat16)
     meta_send = jnp.dot(place_b, meta.astype(jnp.bfloat16)[:, None], preferred_element_type=f32)
     meta_send = meta_send.reshape(n_source, cap).astype(jnp.bfloat16)
-    meta_pad = jnp.zeros((n_source, TILE - cap), jnp.bfloat16)
+    meta_pad = jnp.zeros((n_source, 2 * TILE - cap), jnp.bfloat16)
     send = jnp.concatenate([foot_send.reshape(n_source, cap * TILE), meta_send, meta_pad], axis=1)
     recv = lax.all_to_all(send, "cell", split_axis=0, concat_axis=0, tiled=True)
 

time: 102 us -> 102 us (level)
  no operation moved by 1% of the time
where the time goes in v11:
time: 102 us; the launch traced here: 101 us
  waiting for transfers between devices  42 us (41%)
  starting transfers between devices  39.1 us (38%)
  local copies, waits for them, and re-layouts  10.3 us (10%)
  matrix products  6.24 us (6%)
  other arithmetic  2.76 us (3%)
  between operations  1.06 us (1%)
    all_to_all x1, starting transfers between devices, local(): recv = lax.all_to_all(send, 'cell', split_axis=0, concat_axis=0, tiled=True)  11.8 us
    all_to_all x1, waiting for transfers between devices, local(): recv = lax.all_to_all(send, 'cell', split_axis=0, concat_axis=0, tiled=True)  11.6 us
    all_to_all x1, waiting for transfers between devices, local(): lax.all_to_all(w_send.reshape(n_source, cap * directions), 'cell', split_...  11.1 us
    all_to_all x1, waiting for transfers between devices, local(): lax.all_to_all(partial.reshape(n_source, cap * directions), 'cell', split...  11 us
    all_to_all x1, starting transfers between devices, local(): lax.all_to_all(copies, 'tm', split_axis=0, concat_axis=0, tiled=True)  10.3 us
    all_to_all x1, starting transfers between devices, local(): lax.all_to_all(stack, 'tm', split_axis=0, concat_axis=0, tiled=True)  6.56 us
    all_to_all x1, starting transfers between devices, local(): lax.all_to_all(partial.reshape(n_source, cap * directions), 'cell', split...  5.83 us
    all_to_all x1, starting transfers between devices, local(): lax.all_to_all(w_send.reshape(n_source, cap * directions), 'cell', split_...  4.62 us
  transfers between devices with their start and end apart: 5, of which 5 were waited for; matrix products, arithmetic and copies ran while one was open for 7% of the time, Pallas kernels for 0%

profile of v11, /device:TPU:1, one launch (start us, length us, event | category | flops | bytes accessed | tf_op | source)
XLA Modules:
  0.0 101.5 jit_solution(11010675997488941009)
XLA Ops:
  0.7 0.9 copy.109
  1.6 0.9 broadcast_in_dim.29
  2.5 10.3 %all-to-all-start = ((bf16[8,4,16,512]{3,1,2,0:T(4,128)(2,1)}), bf16[8,4,16,512]{3,1,2,0:T(4,128)(2,1)S(1)}, u32[]{:S(2)}, u32[]{:S(2)}) async-start(bf16[8,4,16,512]{3,1,2,0:T(4,128)(2,1)} %broadcast_in_dim.29), calls=%async_computation | async-start | bytes 1048576 | tf_op jit(solution)/shard_map/all_to_all | solution.py:50
  13.2 0.3 fusion.12
  14.3 1.4 %fusion.5 = f32[1,64,16]{2,0,1:T(1,128)S(1)} fusion(bf16[512,1,1]{0,1,2:T(2,128)(2,1)S(1)} %reshape.262, s32[64,16]{1,0:T(8,128)S(1)} %multiply_add_fusion, s32[512]{0:T(512)S(1)} %add_select_fusion.2), kind=kOutput, calls=%fused_computation.6 | convolution fusion | flops 1572864 | bytes 11264 | tf_op jit(solution)/shard_map/dot_general | solution.py:41
  15.7 0.5 fusion.8
  16.5 0.5 broadcast.162
  17.0 0.8 reduce.2
  17.8 0.8 reshape.270
  18.5 3.8 %all-to-all-done = bf16[8,4,16,512]{3,1,2,0:T(4,128)(2,1)S(1)} async-done(((bf16[8,4,16,512]{3,1,2,0:T(4,128)(2,1)}), bf16[8,4,16,512]{3,1,2,0:T(4,128)(2,1)S(1)}, u32[]{:S(2)}, u32[]{:S(2)}) %all-to-all-start) | async-done | bytes 524320 | tf_op jit(solution)/shard_map/all_to_all | solution.py:50
  22.3 11.8 %all-to-all-start.1 = ((bf16[64,2,1152]{2,1,0:T(2,128)(2,1)}), bf16[64,2,1152]{2,1,0:T(2,128)(2,1)S(1)}, u32[]{:S(2)}, u32[]{:S(2)}) async-start(bf16[64,2,1152]{2,1,0:T(2,128)(2,1)} %reshape.270), calls=%async_computation.1 | async-start | bytes 589824 | tf_op jit(solution)/shard_map/all_to_all | solution.py:45
  34.7 1.0 fusion.34
  35.7 11.6 %all-to-all-done.1 = bf16[64,2,1152]{2,1,0:T(2,128)(2,1)S(1)} async-done(((bf16[64,2,1152]{2,1,0:T(2,128)(2,1)}), bf16[64,2,1152]{2,1,0:T(2,128)(2,1)S(1)}, u32[]{:S(2)}, u32[]{:S(2)}) %all-to-all-start.1) | async-done | bytes 294944 | tf_op jit(solution)/shard_map/all_to_all | solution.py:45
  47.3 0.2 reshape.271
  47.8 0.3 fusion.7
  48.3 0.9 all_to_all.35
  49.2 5.8 %all-to-all-start.2 = ((f32[64,1,256]{2,1,0:T(1,128)}), f32[64,1,256]{2,1,0:T(1,128)S(1)}, u32[]{:S(2)}, u32[]{:S(2)}) async-start(f32[64,1,256]{2,1,0:T(1,128)} %all_to_all.35), calls=%async_computation.2 | async-start | bytes 131072 | tf_op jit(solution)/shard_map/all_to_all | solution.py:63
  55.1 11.0 %all-to-all-done.2 = f32[64,1,256]{2,1,0:T(1,128)S(1)} async-done(((f32[64,1,256]{2,1,0:T(1,128)}), f32[64,1,256]{2,1,0:T(1,128)S(1)}, u32[]{:S(2)}, u32[]{:S(2)}) %all-to-all-start.2) | async-done | bytes 65568 | tf_op jit(solution)/shard_map/all_to_all | solution.py:63
  66.5 1.1 %fusion.9 = f32[64,16]{1,0:T(8,128)S(1)} fusion(s32[64,8]{1,0:T(8,128)S(1)} %fusion.31, f32[1024,16]{1,0:T(8,128)S(1)} %reshape.257), kind=kOutput, calls=%fused_computation.11 | convolution fusion | flops 101194752 | bytes 71680 | tf_op jit(solution)/shard_map/dot_general | solution.py:68
  67.7 0.7 reshape.272
  68.4 6.6 %all-to-all-start.3 = ((f32[8,1,1024]{2,1,0:T(1,128)}), f32[8,1,1024]{2,1,0:T(1,128)S(1)}, u32[]{:S(2)}, u32[]{:S(2)}) async-start(f32[8,1,1024]{2,1,0:T(1,128)} %reshape.272), calls=%async_computation.3 | async-start | bytes 65536 | tf_op jit(solution)/shard_map/all_to_all | solution.py:71
  75.1 4.6 %all-to-all-done.3 = f32[8,1,1024]{2,1,0:T(1,128)S(1)} async-done(((f32[8,1,1024]{2,1,0:T(1,128)}), f32[8,1,1024]{2,1,0:T(1,128)S(1)}, u32[]{:S(2)}, u32[]{:S(2)}) %all-to-all-start.3) | async-done | bytes 32800 | tf_op jit(solution)/shard_map/all_to_all | solution.py:71
  79.7 0.5 broadcast.163
  80.2 0.7 reduce.3
  81.2 1.0 %fusion = f32[1024,16]{1,0:T(8,128)S(1)} fusion(s32[512]{0:T(512)S(1)} %add_select_fusion.2, f32[64,16]{1,0:T(8,128)S(1)} %copy.119), kind=kOutput, calls=%fused_computation.1 | convolution fusion | flops 101187584 | bytes 71680 | tf_op jit(solution)/shard_map/dot_general | solution.py:74
  82.2 0.9 all_to_all.36
  83.1 4.6 %all-to-all-start.4 = ((f32[64,1,256]{2,1,0:T(1,128)}), f32[64,1,256]{2,1,0:T(1,128)S(1)}, u32[]{:S(2)}, u32[]{:S(2)}) async-start(f32[64,1,256]{2,1,0:T(1,128)} %all_to_all.36), calls=%async_computation.4 | async-start | bytes 131072 | tf_op jit(solution)/shard_map/all_to_all | solution.py:75
  87.8 11.1 %all-to-all-done.4 = f32[64,1,256]{2,1,0:T(1,128)S(1)} async-done(((f32[64,1,256]{2,1,0:T(1,128)}), f32[64,1,256]{2,1,0:T(1,128)S(1)}, u32[]{:S(2)}, u32[]{:S(2)}) %all-to-all-start.4) | async-done | bytes 65568 | tf_op jit(solution)/shard_map/all_to_all | solution.py:75
  99.4 0.3 broadcast_multiply_fusion
  99.6 0.4 mul.91
  100.0 0.6 fusion.39
  100.8 0.7 copy.124
  (65 shorter events, 3.9 us)
Async XLA Ops:
  0.6 15.1 %copy-start = (bf16[64,8,128]{2,1,0:T(8,128)(2,1)S(1)}, bf16[64,8,128]{2,1,0:T(8,128)(2,1)}, u32[]{:S(2)}) copy-start(bf16[64,8,128]{2,1,0:T(8,128)(2,1)} %param.9) | copy-start | bytes 393220
  0.6 12.2 %copy-start.5 = (s32[64,1]{0,1:T(1,128)S(1)}, s32[64,1]{0,1:T(1,128)}, u32[]{:S(2)}) copy-start(s32[64,1]{0,1:T(1,128)} %param.12) | copy-start | bytes 772
  0.7 12.4 %copy-start.3 = (s32[64,8]{0,1:T(8,128)S(1)}, s32[64,8]{0,1:T(8,128)}, u32[]{:S(2)}) copy-start(s32[64,8]{0,1:T(8,128)} %param.10) | copy-start | bytes 6148
  1.6 11.9 %copy-start.4 = (s32[64,8]{0,1:T(8,128)S(1)}, s32[64,8]{0,1:T(8,128)}, u32[]{:S(2)}) copy-start(s32[64,8]{0,1:T(8,128)} %param.11) | copy-start | bytes 6148
  1.6 12.0 %copy-start.6 = (s32[1,64,2]{1,2,0:T(2,128)S(1)}, s32[1,64,2]{1,2,0:T(2,128)}, u32[]{:S(2)}) copy-start(s32[1,64,2]{1,2,0:T(2,128)} %param.13) | copy-start | bytes 1540
  2.5 19.8 %all-to-all-start = ((bf16[8,4,16,512]{3,1,2,0:T(4,128)(2,1)}), bf16[8,4,16,512]{3,1,2,0:T(4,128)(2,1)S(1)}, u32[]{:S(2)}, u32[]{:S(2)}) async-start(bf16[8,4,16,512]{3,1,2,0:T(4,128)(2,1)} %broadcast_in_dim.29), calls=%async_computation | async-start | bytes 1048576 | tf_op jit(solution)/shard_map/all_to_all | solution.py:50
  16.3 17.8 %copy-start.1 = (bf16[4,16,512]{2,1,0:T(8,128)(2,1)S(1)}, bf16[4,16,512]{2,1,0:T(8,128)(2,1)}, u32[]{:S(2)}) copy-start(bf16[4,16,512]{2,1,0:T(8,128)(2,1)} %param.8) | copy-start | bytes 196612
  22.3 25.0 %all-to-all-start.1 = ((bf16[64,2,1152]{2,1,0:T(2,128)(2,1)}), bf16[64,2,1152]{2,1,0:T(2,128)(2,1)S(1)}, u32[]{:S(2)}, u32[]{:S(2)}) async-start(bf16[64,2,1152]{2,1,0:T(2,128)(2,1)} %reshape.270), calls=%async_computation.1 | async-start | bytes 589824 | tf_op jit(solution)/shard_map/all_to_all | solution.py:45
  49.2 16.9 %all-to-all-start.2 = ((f32[64,1,256]{2,1,0:T(1,128)}), f32[64,1,256]{2,1,0:T(1,128)S(1)}, u32[]{:S(2)}, u32[]{:S(2)}) async-start(f32[64,1,256]{2,1,0:T(1,128)} %all_to_all.35), calls=%async_computation.2 | async-start | bytes 131072 | tf_op jit(solution)/shard_map/all_to_all | solution.py:63
  66.5 14.6 %copy-start.7 = (f32[64]{0:T(128)S(1)}, f32[64]{0:T(128)}, u32[]{:S(2)}) copy-start(f32[64]{0:T(128)} %param.14) | copy-start | bytes 772
  68.4 11.3 %all-to-all-start.3 = ((f32[8,1,1024]{2,1,0:T(1,128)}), f32[8,1,1024]{2,1,0:T(1,128)S(1)}, u32[]{:S(2)}, u32[]{:S(2)}) async-start(f32[8,1,1024]{2,1,0:T(1,128)} %reshape.272), calls=%async_computation.3 | async-start | bytes 65536 | tf_op jit(solution)/shard_map/all_to_all | solution.py:71
  81.1 18.1 %copy-start.2 = (f32[64,16]{0,1:T(8,128)}, f32[64,16]{0,1:T(8,128)S(1)}, u32[]{:S(2)}) copy-start(f32[64,16]{0,1:T(8,128)S(1)} %bitcast_reduce_fusion) | copy-start | bytes 12292
  83.1 15.8 %all-to-all-start.4 = ((f32[64,1,256]{2,1,0:T(1,128)}), f32[64,1,256]{2,1,0:T(1,128)S(1)}, u32[]{:S(2)}, u32[]{:S(2)}) async-start(f32[64,1,256]{2,1,0:T(1,128)} %all_to_all.36), calls=%async_computation.4 | async-start | bytes 131072 | tf_op jit(solution)/shard_map/all_to_all | solution.py:75

commit v12 on v6

--- a/solution.py
+++ b/solution.py
@@ -46,9 +46,7 @@
 
     my_group = lax.axis_index("tm")
     groups = lax.axis_size("tm")
-    copies = jnp.broadcast_to(flux[None], (groups,) + flux.shape)
-    flux_all = lax.all_to_all(copies, "tm", split_axis=0, concat_axis=0, tiled=True)
-    flux_all = flux_all.reshape(groups * slices, directions, cell_count).astype(f32)
+    flux_all = lax.all_gather(flux, "tm", axis=0, tiled=True).astype(f32)
 
     foot_r = recv[:, : cap * TILE].reshape(n_slot, TILE)
     meta_r = recv[:, cap * TILE : cap * TILE + cap].reshape(n_slot).astype(jnp.int32)

time: 102 us -> 102 us (level)
  waiting for transfers between devices: 41.8 us -> 26.6 us
  blocking collectives: 0 us -> 14.3 us
    all_gather x0 -> x1, blocking collectives: none -> 14.3 us  [local(): flux_all = lax.all_gather(flux, 'tm', axis=0, tiled=True).astype(f32)]
    all_to_all x1, waiting for transfers between devices: 11.6 us -> 0.01 us  [local(): recv = lax.all_to_all(send, 'cell', split_axis=0, concat_axis=0, tiled=True)]
    all_to_all x1 -> x0, starting transfers between devices: 10.3 us -> none  [local(): lax.all_to_all(copies, 'tm', split_axis=0, concat_axis=0, tiled=True)]
    all_to_all x1, starting transfers between devices: 5.83 us -> 12.4 us  [local(): lax.all_to_all(partial.reshape(n_source, cap * directions), 'cell', split...]
    all_to_all x1, starting transfers between devices: 11.8 us -> 17.1 us  [local(): recv = lax.all_to_all(send, 'cell', split_axis=0, concat_axis=0, tiled=True)]
    all_to_all x1 -> x0, waiting for transfers between devices: 3.59 us -> none  [local(): lax.all_to_all(copies, 'tm', split_axis=0, concat_axis=0, tiled=True)]
    all_to_all x1, starting transfers between devices: 6.56 us -> 5.27 us  [local(): lax.all_to_all(stack, 'tm', split_axis=0, concat_axis=0, tiled=True)]
    unnamed x27 -> x20, local copies, waits for them, and re-layouts: 4.11 us -> 5.23 us
  transfers between devices with their start and end apart: 5 -> 4, of which waited for: 5 -> 3; matrix products, arithmetic and copies ran while one was open for 7% -> 2% of each run, Pallas kernels for 0% -> 0%
where the time goes in v12:
time: 102 us
  starting transfers between devices  39.4 us (39%)
  waiting for transfers between devices  26.6 us (26%)
  blocking collectives  14.3 us (14%)
  local copies, waits for them, and re-layouts  10.4 us (10%)
  matrix products  6.46 us (6%)
  other arithmetic  3.41 us (3%)
  between operations  1.02 us (1%)
    all_to_all x1, starting transfers between devices, local(): recv = lax.all_to_all(send, 'cell', split_axis=0, concat_axis=0, tiled=True)  17.1 us
    all_gather x1, blocking collectives, local(): flux_all = lax.all_gather(flux, 'tm', axis=0, tiled=True).astype(f32)  14.3 us
    all_to_all x1, starting transfers between devices, local(): lax.all_to_all(partial.reshape(n_source, cap * directions), 'cell', split...  12.4 us
    all_to_all x1, waiting for transfers between devices, local(): lax.all_to_all(w_send.reshape(n_source, cap * directions), 'cell', split_...  11.1 us
    all_to_all x1, waiting for transfers between devices, local(): lax.all_to_all(partial.reshape(n_source, cap * directions), 'cell', split...  11 us
    all_to_all x1, starting transfers between devices, local(): lax.all_to_all(stack, 'tm', split_axis=0, concat_axis=0, tiled=True)  5.27 us
    unnamed x20, local copies, waits for them, and re-layouts  5.23 us
    all_to_all x1, starting transfers between devices, local(): lax.all_to_all(w_send.reshape(n_source, cap * directions), 'cell', split_...  4.62 us
  transfers between devices with their start and end apart: 4, of which 3 were waited for; matrix products, arithmetic and copies ran while one was open for 2% of the time, Pallas kernels for 0%

profile of v12, /device:TPU:1, one launch (start us, length us, event | category | flops | bytes accessed | tf_op | source)
XLA Modules:
  0.0 101.6 jit_solution(7927136757142136921)
XLA Ops:
  0.7 0.8 iota_compare_fusion.11
  1.5 0.8 copy.101
  2.4 0.3 fusion.12
  2.7 0.8 copy.108
  3.5 0.8 copy.107
  4.9 1.4 %fusion.5 = f32[1,64,16]{2,0,1:T(1,128)S(1)} fusion(bf16[512,1,1]{0,1,2:T(2,128)(2,1)S(1)} %reshape.257, s32[64,16]{1,0:T(8,128)S(1)} %multiply_add_fusion, s32[512]{0:T(512)S(1)} %add_select_fusion.2), kind=kOutput, calls=%fused_computation.6 | convolution fusion | flops 1572864 | bytes 11264 | tf_op jit(solution)/shard_map/dot_general | solution.py:41
  6.3 0.5 fusion.8
  7.0 0.5 broadcast.161
  7.5 0.8 reduce.2
  8.3 1.0 reshape.265
  9.3 17.1 %all-to-all-start = ((bf16[64,2,1088]{2,1,0:T(2,128)(2,1)}), bf16[64,2,1088]{2,1,0:T(2,128)(2,1)S(1)}, u32[]{:S(2)}, u32[]{:S(2)}) async-start(bf16[64,2,1088]{2,1,0:T(2,128)(2,1)} %reshape.265), calls=%async_computation | async-start | bytes 589824 | tf_op jit(solution)/shard_map/all_to_all | solution.py:45
  26.6 14.3 %all_gather.3 = bf16[32,16,512]{2,1,0:T(8,128)(2,1)S(1)} all-gather(bf16[4,16,512]{2,1,0:T(8,128)(2,1)S(1)} %copy-done.1), channel_id=1, replica_groups=mesh['cell'=64,'tm'=8] {'tm'}, dimensions={0}, use_global_device_ids=true | all-gather | bytes 589824 | tf_op jit(solution)/shard_map/all_gather | solution.py:49
  40.8 1.2 %fusion.19 = f32[4,16,512]{2,0,1:T(4,128)S(1)} fusion(bf16[32,16,512]{2,1,0:T(8,128)(2,1)S(1)} %all_gather.3, f32[32,32]{1,0:T(8,128)} %param.15, s32[]{:T(128)S(6)} %select_n.37), kind=kOutput, calls=%fused_computation.21 | convolution fusion | flops 12582912 | bytes 657412 | tf_op jit(solution)/shard_map/ts,skn->tkn/dot_general | solution.py:59
  42.1 0.3 reshape.266
  42.7 0.3 fusion.7
  43.2 0.9 all_to_all.31
  44.1 12.4 %all-to-all-start.1 = ((f32[64,1,256]{2,1,0:T(1,128)}), f32[64,1,256]{2,1,0:T(1,128)S(1)}, u32[]{:S(2)}, u32[]{:S(2)}) async-start(f32[64,1,256]{2,1,0:T(1,128)} %all_to_all.31), calls=%async_computation.1 | async-start | bytes 131072 | tf_op jit(solution)/shard_map/all_to_all | solution.py:61
  56.6 11.0 %all-to-all-done.1 = f32[64,1,256]{2,1,0:T(1,128)S(1)} async-done(((f32[64,1,256]{2,1,0:T(1,128)}), f32[64,1,256]{2,1,0:T(1,128)S(1)}, u32[]{:S(2)}, u32[]{:S(2)}) %all-to-all-start.1) | async-done | bytes 65568 | tf_op jit(solution)/shard_map/all_to_all | solution.py:61
  68.0 1.1 %fusion.9 = f32[64,16]{1,0:T(8,128)S(1)} fusion(s32[64,8]{1,0:T(8,128)S(1)} %fusion.33, f32[1024,16]{1,0:T(8,128)S(1)} %reshape.252), kind=kOutput, calls=%fused_computation.11 | convolution fusion | flops 101194752 | bytes 71680 | tf_op jit(solution)/shard_map/dot_general | solution.py:66
  69.2 0.7 reshape.267
  69.9 5.3 %all-to-all-start.2 = ((f32[8,1,1024]{2,1,0:T(1,128)}), f32[8,1,1024]{2,1,0:T(1,128)S(1)}, u32[]{:S(2)}, u32[]{:S(2)}) async-start(f32[8,1,1024]{2,1,0:T(1,128)} %reshape.267), calls=%async_computation.2 | async-start | bytes 65536 | tf_op jit(solution)/shard_map/all_to_all | solution.py:69
  75.3 4.6 %all-to-all-done.2 = f32[8,1,1024]{2,1,0:T(1,128)S(1)} async-done(((f32[8,1,1024]{2,1,0:T(1,128)}), f32[8,1,1024]{2,1,0:T(1,128)S(1)}, u32[]{:S(2)}, u32[]{:S(2)}) %all-to-all-start.2) | async-done | bytes 32800 | tf_op jit(solution)/shard_map/all_to_all | solution.py:69
  79.9 0.5 broadcast.162
  80.4 0.7 reduce.3
  81.4 1.0 %fusion = f32[1024,16]{1,0:T(8,128)S(1)} fusion(s32[512]{0:T(512)S(1)} %add_select_fusion.2, f32[64,16]{1,0:T(8,128)S(1)} %copy.115), kind=kOutput, calls=%fused_computation.1 | convolution fusion | flops 101187584 | bytes 71680 | tf_op jit(solution)/shard_map/dot_general | solution.py:72
  82.4 0.9 all_to_all.32
  83.3 4.6 %all-to-all-start.3 = ((f32[64,1,256]{2,1,0:T(1,128)}), f32[64,1,256]{2,1,0:T(1,128)S(1)}, u32[]{:S(2)}, u32[]{:S(2)}) async-start(f32[64,1,256]{2,1,0:T(1,128)} %all_to_all.32), calls=%async_computation.3 | async-start | bytes 131072 | tf_op jit(solution)/shard_map/all_to_all | solution.py:73
  88.0 11.1 %all-to-all-done.3 = f32[64,1,256]{2,1,0:T(1,128)S(1)} async-done(((f32[64,1,256]{2,1,0:T(1,128)}), f32[64,1,256]{2,1,0:T(1,128)S(1)}, u32[]{:S(2)}, u32[]{:S(2)}) %all-to-all-start.3) | async-done | bytes 65568 | tf_op jit(solution)/shard_map/all_to_all | solution.py:73
  99.5 0.3 broadcast_multiply_fusion
  99.8 0.4 mul.91
  100.2 0.6 fusion.40
  100.9 0.7 copy.120
  (54 shorter events, 3.1 us)
Async XLA Ops:
  0.6 5.6 %copy-start = (bf16[64,8,128]{2,1,0:T(8,128)(2,1)S(1)}, bf16[64,8,128]{2,1,0:T(8,128)(2,1)}, u32[]{:S(2)}) copy-start(bf16[64,8,128]{2,1,0:T(8,128)(2,1)} %param.9) | copy-start | bytes 393220
  6.9 19.6 %copy-start.1 = (bf16[4,16,512]{2,1,0:T(8,128)(2,1)S(1)}, bf16[4,16,512]{2,1,0:T(8,128)(2,1)}, u32[]{:S(2)}) copy-start(bf16[4,16,512]{2,1,0:T(8,128)(2,1)} %param.8) | copy-start | bytes 196612
  9.3 32.8 %all-to-all-start = ((bf16[64,2,1088]{2,1,0:T(2,128)(2,1)}), bf16[64,2,1088]{2,1,0:T(2,128)(2,1)S(1)}, u32[]{:S(2)}, u32[]{:S(2)}) async-start(bf16[64,2,1088]{2,1,0:T(2,128)(2,1)} %reshape.265), calls=%async_computation | async-start | bytes 589824 | tf_op jit(solution)/shard_map/all_to_all | solution.py:45
  42.7 13.8 %copy-start.3 = (s32[64,1]{0,1:T(1,128)S(1)}, s32[64,1]{0,1:T(1,128)}, u32[]{:S(2)}) copy-start(s32[64,1]{0,1:T(1,128)} %param.12) | copy-start | bytes 772
  44.1 23.5 %all-to-all-start.1 = ((f32[64,1,256]{2,1,0:T(1,128)}), f32[64,1,256]{2,1,0:T(1,128)S(1)}, u32[]{:S(2)}, u32[]{:S(2)}) async-start(f32[64,1,256]{2,1,0:T(1,128)} %all_to_all.31), calls=%async_computation.1 | async-start | bytes 131072 | tf_op jit(solution)/shard_map/all_to_all | solution.py:61
  68.0 13.3 %copy-start.4 = (f32[64]{0:T(128)S(1)}, f32[64]{0:T(128)}, u32[]{:S(2)}) copy-start(f32[64]{0:T(128)} %param.14) | copy-start | bytes 772
  69.9 10.0 %all-to-all-start.2 = ((f32[8,1,1024]{2,1,0:T(1,128)}), f32[8,1,1024]{2,1,0:T(1,128)S(1)}, u32[]{:S(2)}, u32[]{:S(2)}) async-start(f32[8,1,1024]{2,1,0:T(1,128)} %reshape.267), calls=%async_computation.2 | async-start | bytes 65536 | tf_op jit(solution)/shard_map/all_to_all | solution.py:69
  81.2 18.1 %copy-start.2 = (f32[64,16]{0,1:T(8,128)}, f32[64,16]{0,1:T(8,128)S(1)}, u32[]{:S(2)}) copy-start(f32[64,16]{0,1:T(8,128)S(1)} %bitcast_reduce_fusion) | copy-start | bytes 12292
  83.3 15.8 %all-to-all-start.3 = ((f32[64,1,256]{2,1,0:T(1,128)}), f32[64,1,256]{2,1,0:T(1,128)S(1)}, u32[]{:S(2)}, u32[]{:S(2)}) async-start(f32[64,1,256]{2,1,0:T(1,128)} %all_to_all.32), calls=%async_computation.3 | async-start | bytes 131072 | tf_op jit(solution)/shard_map/all_to_all | solution.py:73

commit v13 on v12

--- a/solution.py
+++ b/solution.py
@@ -46,7 +46,6 @@
 
     my_group = lax.axis_index("tm")
     groups = lax.axis_size("tm")
-    flux_all = lax.all_gather(flux, "tm", axis=0, tiled=True).astype(f32)
 
     foot_r = recv[:, : cap * TILE].reshape(n_slot, TILE)
     meta_r = recv[:, cap * TILE : cap * TILE + cap].reshape(n_slot).astype(jnp.int32)
@@ -55,9 +54,7 @@
     panels = panels.reshape(TILE, n_meta * directions)
     every = jnp.dot(foot_r, panels, preferred_element_type=f32).reshape(n_slot, n_meta, directions)
     partial = jnp.sum(every * meta_hot[:, :, None], axis=1)
-    panel = lax.dynamic_slice(prior, (my_group * slices, 0), (slices, groups * slices))
-    coupled = jnp.einsum("ts,skn->tkn", panel, flux_all, precision=HI)
-    coupled, partial = lax.optimization_barrier((coupled, partial))
+    flux_late, partial = lax.optimization_barrier((flux, partial))
     back = lax.all_to_all(
         partial.reshape(n_source, cap * directions), "cell", split_axis=0, concat_axis=0, tiled=True
     ).reshape(n_slot, directions)
@@ -70,6 +67,10 @@
     weighted = obs_weight[:, None] * images
     w_block = jnp.repeat(weighted, nb, axis=0)
     w_send = jnp.dot(place_f, w_block, precision=HI, preferred_element_type=f32)
+    flux_all = lax.all_gather(flux_late, "tm", axis=0, tiled=True).astype(f32)
+    panel = lax.dynamic_slice(prior, (my_group * slices, 0), (slices, groups * slices))
+    coupled = jnp.einsum("ts,skn->tkn", panel, flux_all, precision=HI)
+    coupled, w_send = lax.optimization_barrier((coupled, w_send))
     w_recv = lax.all_to_all(
         w_send.reshape(n_source, cap * directions), "cell", split_axis=0, concat_axis=0, tiled=True
     ).reshape(n_slot, directions)

time: 102 us -> 104 us (1.020)
  blocking collectives: 14.3 us -> 15.4 us
    all_to_all x1, waiting for transfers between devices: 0.01 us -> 12.9 us  [local(): recv = lax.all_to_all(send, 'cell', split_axis=0, concat_axis=0, tiled=True)]
    all_to_all x1, waiting for transfers between devices: 11 us -> 0.01 us  [local(): lax.all_to_all(partial.reshape(n_source, cap * directions), 'cell', split...]
    all_to_all x1, starting transfers between devices: 4.62 us -> 12.4 us  [local(): lax.all_to_all(w_send.reshape(n_source, cap * directions), 'cell', split_...]
    all_to_all x1, starting transfers between devices: 12.4 us -> 5.81 us  [local(): lax.all_to_all(partial.reshape(n_source, cap * directions), 'cell', split...]
    all_to_all x1, starting transfers between devices: 5.27 us -> 3.84 us  [local(): lax.all_to_all(stack, 'tm', split_axis=0, concat_axis=0, tiled=True)]
    all_to_all x1, waiting for transfers between devices: 4.59 us -> 3.35 us  [local(): lax.all_to_all(stack, 'tm', split_axis=0, concat_axis=0, tiled=True)]
    all_gather x1, blocking collectives: 14.3 us -> 15.4 us  [local(): flux_all = lax.all_gather(flux_late, 'tm', axis=0, tiled=True).astype(f32)]
where the time goes in v13:
time: 104 us; the launch traced here: 103 us
  starting transfers between devices  39.2 us (38%)
  waiting for transfers between devices  27.3 us (26%)
  blocking collectives  15.4 us (15%)
  local copies, waits for them, and re-layouts  10.6 us (10%)
  matrix products  6.45 us (6%)
  other arithmetic  3.41 us (3%)
    all_to_all x1, starting transfers between devices, local(): recv = lax.all_to_all(send, 'cell', split_axis=0, concat_axis=0, tiled=True)  17.1 us
    all_gather x1, blocking collectives, local(): flux_all = lax.all_gather(flux_late, 'tm', axis=0, tiled=True).astype(f32)  15.4 us
    all_to_all x1, waiting for transfers between devices, local(): recv = lax.all_to_all(send, 'cell', split_axis=0, concat_axis=0, tiled=True)  12.9 us
    all_to_all x1, starting transfers between devices, local(): lax.all_to_all(w_send.reshape(n_source, cap * directions), 'cell', split_...  12.4 us
    all_to_all x1, waiting for transfers between devices, local(): lax.all_to_all(w_send.reshape(n_source, cap * directions), 'cell', split_...  11 us
    all_to_all x1, starting transfers between devices, local(): lax.all_to_all(partial.reshape(n_source, cap * directions), 'cell', split...  5.81 us
    unnamed x20, local copies, waits for them, and re-layouts  5.21 us
    all_to_all x1, starting transfers between devices, local(): lax.all_to_all(stack, 'tm', split_axis=0, concat_axis=0, tiled=True)  3.84 us
  transfers between devices with their start and end apart: 4, of which 3 were waited for; matrix products, arithmetic and copies ran while one was open for 2% of the time, Pallas kernels for 0%

profile of v13, /device:TPU:1, one launch (start us, length us, event | category | flops | bytes accessed | tf_op | source)
XLA Modules:
  0.0 103.4 jit_solution(14152894368537540464)
XLA Ops:
  0.7 0.8 iota_compare_fusion.11
  1.5 0.8 copy.101
  2.4 0.3 fusion.12
  2.7 0.8 copy.107
  3.5 0.8 copy.106
  4.9 1.4 %fusion.5 = f32[1,64,16]{2,0,1:T(1,128)S(1)} fusion(bf16[512,1,1]{0,1,2:T(2,128)(2,1)S(1)} %reshape.256, s32[64,16]{1,0:T(8,128)S(1)} %multiply_add_fusion, s32[512]{0:T(512)S(1)} %add_select_fusion.2), kind=kOutput, calls=%fused_computation.6 | convolution fusion | flops 1572864 | bytes 11264 | tf_op jit(solution)/shard_map/dot_general | solution.py:41
  6.3 0.5 fusion.8
  7.0 0.5 broadcast.161
  7.5 0.8 reduce.2
  8.3 1.0 reshape.265
  9.3 17.1 %all-to-all-start = ((bf16[64,2,1088]{2,1,0:T(2,128)(2,1)}), bf16[64,2,1088]{2,1,0:T(2,128)(2,1)S(1)}, u32[]{:S(2)}, u32[]{:S(2)}) async-start(bf16[64,2,1088]{2,1,0:T(2,128)(2,1)} %reshape.265), calls=%async_computation | async-start | bytes 589824 | tf_op jit(solution)/shard_map/all_to_all | solution.py:45
  26.7 12.9 %all-to-all-done = bf16[64,2,1088]{2,1,0:T(2,128)(2,1)S(1)} async-done(((bf16[64,2,1088]{2,1,0:T(2,128)(2,1)}), bf16[64,2,1088]{2,1,0:T(2,128)(2,1)S(1)}, u32[]{:S(2)}, u32[]{:S(2)}) %all-to-all-start) | async-done | bytes 278560 | tf_op jit(solution)/shard_map/all_to_all | solution.py:45
  39.6 0.3 reshape.266
  40.3 0.3 fusion.7
  40.8 0.9 all_to_all.31
  41.6 5.8 %all-to-all-start.1 = ((f32[64,1,256]{2,1,0:T(1,128)}), f32[64,1,256]{2,1,0:T(1,128)S(1)}, u32[]{:S(2)}, u32[]{:S(2)}) async-start(f32[64,1,256]{2,1,0:T(1,128)} %all_to_all.31), calls=%async_computation.1 | async-start | bytes 131072 | tf_op jit(solution)/shard_map/all_to_all | solution.py:58
  47.5 15.4 %all_gather.3 = bf16[32,16,512]{2,1,0:T(8,128)(2,1)S(1)} all-gather(bf16[4,16,512]{2,1,0:T(8,128)(2,1)S(1)} %copy-done.1), channel_id=1, replica_groups=mesh['cell'=64,'tm'=8] {'tm'}, dimensions={0}, use_global_device_ids=true | all-gather | bytes 589824 | tf_op jit(solution)/shard_map/all_gather | solution.py:70
  63.2 1.1 %fusion.9 = f32[64,16]{1,0:T(8,128)S(1)} fusion(s32[64,8]{1,0:T(8,128)S(1)} %fusion.33, f32[1024,16]{1,0:T(8,128)S(1)} %reshape.252), kind=kOutput, calls=%fused_computation.11 | convolution fusion | flops 101194752 | bytes 71680 | tf_op jit(solution)/shard_map/dot_general | solution.py:63
  64.4 0.7 reshape.267
  65.1 3.8 %all-to-all-start.2 = ((f32[8,1,1024]{2,1,0:T(1,128)}), f32[8,1,1024]{2,1,0:T(1,128)S(1)}, u32[]{:S(2)}, u32[]{:S(2)}) async-start(f32[8,1,1024]{2,1,0:T(1,128)} %reshape.267), calls=%async_computation.2 | async-start | bytes 65536 | tf_op jit(solution)/shard_map/all_to_all | solution.py:66
  69.0 1.2 %fusion.19 = f32[4,16,512]{2,0,1:T(4,128)S(1)} fusion(bf16[32,16,512]{2,1,0:T(8,128)(2,1)S(1)} %all_gather.3, f32[32,32]{1,0:T(8,128)} %param.15, s32[]{:T(128)S(6)} %select_n.39), kind=kOutput, calls=%fused_computation.21 | convolution fusion | flops 12582912 | bytes 657412 | tf_op jit(solution)/shard_map/ts,skn->tkn/dot_general | solution.py:72
  70.3 3.3 %all-to-all-done.2 = f32[8,1,1024]{2,1,0:T(1,128)S(1)} async-done(((f32[8,1,1024]{2,1,0:T(1,128)}), f32[8,1,1024]{2,1,0:T(1,128)S(1)}, u32[]{:S(2)}, u32[]{:S(2)}) %all-to-all-start.2) | async-done | bytes 32800 | tf_op jit(solution)/shard_map/all_to_all | solution.py:66
  73.7 0.5 broadcast.162
  74.2 0.7 reduce.3
  75.1 1.0 fusion
  76.4 0.9 all_to_all.32
  77.2 12.4 %all-to-all-start.3 = ((f32[64,1,256]{2,1,0:T(1,128)}), f32[64,1,256]{2,1,0:T(1,128)S(1)}, u32[]{:S(2)}, u32[]{:S(2)}) async-start(f32[64,1,256]{2,1,0:T(1,128)} %all_to_all.32), calls=%async_computation.3 | async-start | bytes 131072 | tf_op jit(solution)/shard_map/all_to_all | solution.py:74
  89.7 11.0 %all-to-all-done.3 = f32[64,1,256]{2,1,0:T(1,128)S(1)} async-done(((f32[64,1,256]{2,1,0:T(1,128)}), f32[64,1,256]{2,1,0:T(1,128)S(1)}, u32[]{:S(2)}, u32[]{:S(2)}) %all-to-all-start.3) | async-done | bytes 65568 | tf_op jit(solution)/shard_map/all_to_all | solution.py:74
  101.3 0.3 broadcast_multiply_fusion
  101.5 0.4 mul.91
  101.9 0.6 fusion.40
  102.7 0.7 copy.120
  (55 shorter events, 3.4 us)
Async XLA Ops:
  0.6 5.6 %copy-start = (bf16[64,8,128]{2,1,0:T(8,128)(2,1)S(1)}, bf16[64,8,128]{2,1,0:T(8,128)(2,1)}, u32[]{:S(2)}) copy-start(bf16[64,8,128]{2,1,0:T(8,128)(2,1)} %param.9) | copy-start | bytes 393220
  6.9 19.7 %copy-start.1 = (bf16[4,16,512]{2,1,0:T(8,128)(2,1)S(1)}, bf16[4,16,512]{2,1,0:T(8,128)(2,1)}, u32[]{:S(2)}) copy-start(bf16[4,16,512]{2,1,0:T(8,128)(2,1)} %param.8) | copy-start | bytes 196612
  7.0 19.6 %copy-start.3 = (s32[64,1]{0,1:T(1,128)S(1)}, s32[64,1]{0,1:T(1,128)}, u32[]{:S(2)}) copy-start(s32[64,1]{0,1:T(1,128)} %param.12) | copy-start | bytes 772
  9.3 30.4 %all-to-all-start = ((bf16[64,2,1088]{2,1,0:T(2,128)(2,1)}), bf16[64,2,1088]{2,1,0:T(2,128)(2,1)S(1)}, u32[]{:S(2)}, u32[]{:S(2)}) async-start(bf16[64,2,1088]{2,1,0:T(2,128)(2,1)} %reshape.265), calls=%async_computation | async-start | bytes 589824 | tf_op jit(solution)/shard_map/all_to_all | solution.py:45
  41.6 21.2 %all-to-all-start.1 = ((f32[64,1,256]{2,1,0:T(1,128)}), f32[64,1,256]{2,1,0:T(1,128)S(1)}, u32[]{:S(2)}, u32[]{:S(2)}) async-start(f32[64,1,256]{2,1,0:T(1,128)} %all_to_all.31), calls=%async_computation.1 | async-start | bytes 131072 | tf_op jit(solution)/shard_map/all_to_all | solution.py:58
  64.3 10.7 %copy-start.4 = (f32[64]{0:T(128)S(1)}, f32[64]{0:T(128)}, u32[]{:S(2)}) copy-start(f32[64]{0:T(128)} %param.14) | copy-start | bytes 772
  65.1 8.6 %all-to-all-start.2 = ((f32[8,1,1024]{2,1,0:T(1,128)}), f32[8,1,1024]{2,1,0:T(1,128)S(1)}, u32[]{:S(2)}, u32[]{:S(2)}) async-start(f32[8,1,1024]{2,1,0:T(1,128)} %reshape.267), calls=%async_computation.2 | async-start | bytes 65536 | tf_op jit(solution)/shard_map/all_to_all | solution.py:66
  75.0 25.9 %copy-start.2 = (f32[64,16]{0,1:T(8,128)}, f32[64,16]{0,1:T(8,128)S(1)}, u32[]{:S(2)}) copy-start(f32[64,16]{0,1:T(8,128)S(1)} %bitcast_reduce_fusion) | copy-start | bytes 12292
  77.2 23.5 %all-to-all-start.3 = ((f32[64,1,256]{2,1,0:T(1,128)}), f32[64,1,256]{2,1,0:T(1,128)S(1)}, u32[]{:S(2)}, u32[]{:S(2)}) async-start(f32[64,1,256]{2,1,0:T(1,128)} %all_to_all.32), calls=%async_computation.3 | async-start | bytes 131072 | tf_op jit(solution)/shard_map/all_to_all | solution.py:74

commit v14 on v13

--- a/solution.py
+++ b/solution.py
@@ -54,7 +54,8 @@
     panels = panels.reshape(TILE, n_meta * directions)
     every = jnp.dot(foot_r, panels, preferred_element_type=f32).reshape(n_slot, n_meta, directions)
     partial = jnp.sum(every * meta_hot[:, :, None], axis=1)
-    flux_late, partial = lax.optimization_barrier((flux, partial))
+    half = directions // 2
+    flux_a, partial = lax.optimization_barrier((flux[:, :half], partial))
     back = lax.all_to_all(
         partial.reshape(n_source, cap * directions), "cell", split_axis=0, concat_axis=0, tiled=True
     ).reshape(n_slot, directions)
@@ -67,10 +68,10 @@
     weighted = obs_weight[:, None] * images
     w_block = jnp.repeat(weighted, nb, axis=0)
     w_send = jnp.dot(place_f, w_block, precision=HI, preferred_element_type=f32)
-    flux_all = lax.all_gather(flux_late, "tm", axis=0, tiled=True).astype(f32)
     panel = lax.dynamic_slice(prior, (my_group * slices, 0), (slices, groups * slices))
-    coupled = jnp.einsum("ts,skn->tkn", panel, flux_all, precision=HI)
-    coupled, w_send = lax.optimization_barrier((coupled, w_send))
+    gathered_a = lax.all_gather(flux_a, "tm", axis=0, tiled=True).astype(f32)
+    coupled_a = jnp.einsum("ts,skn->tkn", panel, gathered_a, precision=HI)
+    coupled_a, flux_b, w_send = lax.optimization_barrier((coupled_a, flux[:, half:], w_send))
     w_recv = lax.all_to_all(
         w_send.reshape(n_source, cap * directions), "cell", split_axis=0, concat_axis=0, tiled=True
     ).reshape(n_slot, directions)
@@ -80,7 +81,9 @@
     adj = jnp.dot(w_meta.T, foot_r.astype(f32), precision=HI, preferred_element_type=f32)
     adjoint = adj.reshape(slices, directions, cell_count)
 
-    hess = adjoint + coupled
+    gathered_b = lax.all_gather(flux_b, "tm", axis=0, tiled=True).astype(f32)
+    coupled_b = jnp.einsum("ts,skn->tkn", panel, gathered_b, precision=HI)
+    hess = adjoint + jnp.concatenate([coupled_a, coupled_b], axis=1)
     return (images, hess)
 
 

time: 104 us -> 108 us (1.038)
  blocking collectives: 15.4 us -> 28.9 us
  waiting for transfers between devices: 27.3 us -> 17.4 us
    all_gather x1 -> x2, blocking collectives: 15.4 us -> 28.9 us  [the longest x1 15.1 us: local(): gathered_a = lax.all_gather(flux_a, 'tm', axis=0, tiled=True).astype(f32)]
    all_to_all x1, waiting for transfers between devices: 11 us -> 0.01 us  [local(): lax.all_to_all(w_send.reshape(n_source, cap * directions), 'cell', split_...]
    all_to_all x1, waiting for transfers between devices: 3.35 us -> 4.51 us  [local(): lax.all_to_all(stack, 'tm', split_axis=0, concat_axis=0, tiled=True)]
  transfers between devices with their start and end apart: 4 -> 4, of which waited for: 3 -> 2; matrix products, arithmetic and copies ran while one was open for 2% -> 2% of each run, Pallas kernels for 0% -> 0%
where the time goes in v14:
time: 108 us
  starting transfers between devices  39.2 us (36%)
  blocking collectives  28.9 us (27%)
  waiting for transfers between devices  17.4 us (16%)
  local copies, waits for them, and re-layouts  10.7 us (10%)
  matrix products  7.12 us (7%)
  other arithmetic  3.39 us (3%)
    all_to_all x1, starting transfers between devices, local(): recv = lax.all_to_all(send, 'cell', split_axis=0, concat_axis=0, tiled=True)  17.1 us
    all_gather x1, blocking collectives, local(): gathered_a = lax.all_gather(flux_a, 'tm', axis=0, tiled=True).astype(f32)  15.1 us
    all_gather x1, blocking collectives, local(): gathered_b = lax.all_gather(flux_b, 'tm', axis=0, tiled=True).astype(f32)  13.9 us
    all_to_all x1, waiting for transfers between devices, local(): recv = lax.all_to_all(send, 'cell', split_axis=0, concat_axis=0, tiled=True)  12.9 us
    all_to_all x1, starting transfers between devices, local(): lax.all_to_all(w_send.reshape(n_source, cap * directions), 'cell', split_...  12.4 us
    all_to_all x1, starting transfers between devices, local(): lax.all_to_all(partial.reshape(n_source, cap * directions), 'cell', split...  5.81 us
    unnamed x20, local copies, waits for them, and re-layouts  5.25 us
    all_to_all x1, waiting for transfers between devices, local(): lax.all_to_all(stack, 'tm', split_axis=0, concat_axis=0, tiled=True)  4.51 us
  transfers between devices with their start and end apart: 4, of which 2 were waited for; matrix products, arithmetic and copies ran while one was open for 2% of the time, Pallas kernels for 0%

profile of v14, /device:TPU:1, one launch (start us, length us, event | category | flops | bytes accessed | tf_op | source)
XLA Modules:
  0.0 107.8 jit_solution(12235967815041244382)
XLA Ops:
  0.7 0.8 copy.107
  1.6 0.7 iota_compare_fusion.11
  2.4 0.3 fusion.12
  2.7 0.8 copy.112
  4.0 0.8 copy.113
  4.9 1.4 %fusion.5 = f32[1,64,16]{2,0,1:T(1,128)S(1)} fusion(bf16[512,1,1]{0,1,2:T(2,128)(2,1)S(1)} %reshape.256, s32[64,16]{1,0:T(8,128)S(1)} %multiply_add_fusion, s32[512]{0:T(512)S(1)} %add_select_fusion.2), kind=kOutput, calls=%fused_computation.6 | convolution fusion | flops 1572864 | bytes 11264 | tf_op jit(solution)/shard_map/dot_general | solution.py:41
  6.3 0.5 fusion.8
  7.0 0.5 broadcast.161
  7.5 0.8 reduce.2
  8.3 1.0 reshape.265
  9.3 17.1 %all-to-all-start = ((bf16[64,2,1088]{2,1,0:T(2,128)(2,1)}), bf16[64,2,1088]{2,1,0:T(2,128)(2,1)S(1)}, u32[]{:S(2)}, u32[]{:S(2)}) async-start(bf16[64,2,1088]{2,1,0:T(2,128)(2,1)} %reshape.265), calls=%async_computation | async-start | bytes 589824 | tf_op jit(solution)/shard_map/all_to_all | solution.py:45
  26.7 12.9 %all-to-all-done = bf16[64,2,1088]{2,1,0:T(2,128)(2,1)S(1)} async-done(((bf16[64,2,1088]{2,1,0:T(2,128)(2,1)}), bf16[64,2,1088]{2,1,0:T(2,128)(2,1)S(1)}, u32[]{:S(2)}, u32[]{:S(2)}) %all-to-all-start) | async-done | bytes 278560 | tf_op jit(solution)/shard_map/all_to_all | solution.py:45
  39.6 0.3 reshape.266
  40.3 0.3 fusion.7
  40.8 0.9 all_to_all.31
  41.6 5.8 %all-to-all-start.1 = ((f32[64,1,256]{2,1,0:T(1,128)}), f32[64,1,256]{2,1,0:T(1,128)S(1)}, u32[]{:S(2)}, u32[]{:S(2)}) async-start(f32[64,1,256]{2,1,0:T(1,128)} %all_to_all.31), calls=%async_computation.1 | async-start | bytes 131072 | tf_op jit(solution)/shard_map/all_to_all | solution.py:59
  47.5 15.1 %all_gather.6 = bf16[32,8,512]{2,1,0:T(8,128)(2,1)S(1)} all-gather(bf16[4,8,512]{2,1,0:T(8,128)(2,1)S(1)} %get-tuple-element.8), channel_id=1, replica_groups=mesh['cell'=64,'tm'=8] {'tm'}, dimensions={0}, use_global_device_ids=true | all-gather | bytes 294912 | tf_op jit(solution)/shard_map/all_gather | solution.py:72
  62.5 1.0 fusion.22
  63.9 1.1 %fusion.9 = f32[64,16]{1,0:T(8,128)S(1)} fusion(s32[64,8]{1,0:T(8,128)S(1)} %fusion.35, f32[1024,16]{1,0:T(8,128)S(1)} %reshape.252), kind=kOutput, calls=%fused_computation.11 | convolution fusion | flops 101194752 | bytes 71680 | tf_op jit(solution)/shard_map/dot_general | solution.py:64
  65.1 0.7 reshape.267
  65.8 3.8 %all-to-all-start.2 = ((f32[8,1,1024]{2,1,0:T(1,128)}), f32[8,1,1024]{2,1,0:T(1,128)S(1)}, u32[]{:S(2)}, u32[]{:S(2)}) async-start(f32[8,1,1024]{2,1,0:T(1,128)} %reshape.267), calls=%async_computation.2 | async-start | bytes 65536 | tf_op jit(solution)/shard_map/all_to_all | solution.py:67
  69.9 4.5 %all-to-all-done.2 = f32[8,1,1024]{2,1,0:T(1,128)S(1)} async-done(((f32[8,1,1024]{2,1,0:T(1,128)}), f32[8,1,1024]{2,1,0:T(1,128)S(1)}, u32[]{:S(2)}, u32[]{:S(2)}) %all-to-all-start.2) | async-done | bytes 32800 | tf_op jit(solution)/shard_map/all_to_all | solution.py:67
  74.4 0.5 broadcast.162
  74.9 0.7 reduce.3
  75.8 1.0 fusion
  77.1 0.9 all_to_all.32
  77.9 12.4 %all-to-all-start.3 = ((f32[64,1,256]{2,1,0:T(1,128)}), f32[64,1,256]{2,1,0:T(1,128)S(1)}, u32[]{:S(2)}, u32[]{:S(2)}) async-start(f32[64,1,256]{2,1,0:T(1,128)} %all_to_all.32), calls=%async_computation.3 | async-start | bytes 131072 | tf_op jit(solution)/shard_map/all_to_all | solution.py:75
  90.4 13.9 %all_gather.7 = bf16[32,8,512]{2,1,0:T(8,128)(2,1)S(1)} all-gather(bf16[4,8,512]{2,1,0:T(8,128)(2,1)S(1)} %get-tuple-element.11), channel_id=1, replica_groups=mesh['cell'=64,'tm'=8] {'tm'}, dimensions={0}, use_global_device_ids=true | all-gather | bytes 294912 | tf_op jit(solution)/shard_map/all_gather | solution.py:84
  104.2 1.0 fusion.20
  106.0 0.4 mul.91
  106.4 0.6 fusion.46
  107.1 0.7 copy.127
  (58 shorter events, 3.6 us)
Async XLA Ops:
  0.6 5.6 %copy-start = (bf16[64,8,128]{2,1,0:T(8,128)(2,1)S(1)}, bf16[64,8,128]{2,1,0:T(8,128)(2,1)}, u32[]{:S(2)}) copy-start(bf16[64,8,128]{2,1,0:T(8,128)(2,1)} %param.9) | copy-start | bytes 393220
  6.9 19.6 %copy-start.1 = (bf16[4,16,512]{2,1,0:T(8,128)(2,1)S(1)}, bf16[4,16,512]{2,1,0:T(8,128)(2,1)}, u32[]{:S(2)}) copy-start(bf16[4,16,512]{2,1,0:T(8,128)(2,1)} %param.8) | copy-start | bytes 196612
  7.5 19.1 %copy-start.3 = (s32[64,1]{0,1:T(1,128)S(1)}, s32[64,1]{0,1:T(1,128)}, u32[]{:S(2)}) copy-start(s32[64,1]{0,1:T(1,128)} %param.12) | copy-start | bytes 772
  9.3 30.4 %all-to-all-start = ((bf16[64,2,1088]{2,1,0:T(2,128)(2,1)}), bf16[64,2,1088]{2,1,0:T(2,128)(2,1)S(1)}, u32[]{:S(2)}, u32[]{:S(2)}) async-start(bf16[64,2,1088]{2,1,0:T(2,128)(2,1)} %reshape.265), calls=%async_computation | async-start | bytes 589824 | tf_op jit(solution)/shard_map/all_to_all | solution.py:45
  41.6 21.9 %all-to-all-start.1 = ((f32[64,1,256]{2,1,0:T(1,128)}), f32[64,1,256]{2,1,0:T(1,128)S(1)}, u32[]{:S(2)}, u32[]{:S(2)}) async-start(f32[64,1,256]{2,1,0:T(1,128)} %all_to_all.31), calls=%async_computation.1 | async-start | bytes 131072 | tf_op jit(solution)/shard_map/all_to_all | solution.py:59
  63.9 11.8 %copy-start.4 = (f32[64]{0:T(128)S(1)}, f32[64]{0:T(128)}, u32[]{:S(2)}) copy-start(f32[64]{0:T(128)} %param.14) | copy-start | bytes 772
  65.8 8.6 %all-to-all-start.2 = ((f32[8,1,1024]{2,1,0:T(1,128)}), f32[8,1,1024]{2,1,0:T(1,128)S(1)}, u32[]{:S(2)}, u32[]{:S(2)}) async-start(f32[8,1,1024]{2,1,0:T(1,128)} %reshape.267), calls=%async_computation.2 | async-start | bytes 65536 | tf_op jit(solution)/shard_map/all_to_all | solution.py:67
  75.7 28.5 %copy-start.2 = (f32[64,16]{0,1:T(8,128)}, f32[64,16]{0,1:T(8,128)S(1)}, u32[]{:S(2)}) copy-start(f32[64,16]{0,1:T(8,128)S(1)} %bitcast_reduce_fusion) | copy-start | bytes 12292
  77.9 27.3 %all-to-all-start.3 = ((f32[64,1,256]{2,1,0:T(1,128)}), f32[64,1,256]{2,1,0:T(1,128)S(1)}, u32[]{:S(2)}, u32[]{:S(2)}) async-start(f32[64,1,256]{2,1,0:T(1,128)} %all_to_all.32), calls=%async_computation.3 | async-start | bytes 131072 | tf_op jit(solution)/shard_map/all_to_all | solution.py:75

commit v15 on v13

--- a/solution.py
+++ b/solution.py
@@ -46,7 +46,6 @@
 
     my_group = lax.axis_index("tm")
     groups = lax.axis_size("tm")
-
     foot_r = recv[:, : cap * TILE].reshape(n_slot, TILE)
     meta_r = recv[:, cap * TILE : cap * TILE + cap].reshape(n_slot).astype(jnp.int32)
     meta_hot = (meta_r[:, None] == jnp.arange(n_meta, dtype=jnp.int32)[None, :]).astype(f32)
@@ -54,7 +53,6 @@
     panels = panels.reshape(TILE, n_meta * directions)
     every = jnp.dot(foot_r, panels, preferred_element_type=f32).reshape(n_slot, n_meta, directions)
     partial = jnp.sum(every * meta_hot[:, :, None], axis=1)
-    flux_late, partial = lax.optimization_barrier((flux, partial))
     back = lax.all_to_all(
         partial.reshape(n_source, cap * directions), "cell", split_axis=0, concat_axis=0, tiled=True
     ).reshape(n_slot, directions)
@@ -62,15 +60,26 @@
     place_f = place.astype(f32)
     per_block = jnp.dot(place_f.T, back, precision=HI, preferred_element_type=f32)
     partial_value = per_block.reshape(sounds, nb, directions).sum(axis=1)
-    stack = jnp.broadcast_to(partial_value[None], (groups,) + partial_value.shape)
-    images = lax.all_to_all(stack, "tm", split_axis=0, concat_axis=0, tiled=True).sum(axis=0)
+    bf = jnp.bfloat16
+    hi = lax.reduce_precision(partial_value, exponent_bits=8, mantissa_bits=7)
+    rest = partial_value - hi
+    mid = lax.reduce_precision(rest, exponent_bits=8, mantissa_bits=7)
+    lo = rest - mid
+    pieces = jnp.stack([hi, mid, lo]).astype(bf).reshape(-1, TILE)
+    flux_rows = flux.reshape(-1, TILE)
+    payload = jnp.concatenate([flux_rows, pieces], axis=0)
+    copies = jnp.broadcast_to(payload[None], (groups,) + payload.shape)
+    arrived = lax.all_to_all(copies, "tm", split_axis=0, concat_axis=0, tiled=True)
+    n_rows = flux_rows.shape[0]
+    flux_all = arrived[:, :n_rows].reshape(groups * slices, directions, cell_count).astype(f32)
+    parts = arrived[:, n_rows:].reshape(groups, 3, sounds, directions).astype(f32)
+    values = (parts[:, 0] + parts[:, 1]) + parts[:, 2]
+    images = values.sum(axis=0)
     weighted = obs_weight[:, None] * images
     w_block = jnp.repeat(weighted, nb, axis=0)
     w_send = jnp.dot(place_f, w_block, precision=HI, preferred_element_type=f32)
-    flux_all = lax.all_gather(flux_late, "tm", axis=0, tiled=True).astype(f32)
     panel = lax.dynamic_slice(prior, (my_group * slices, 0), (slices, groups * slices))
     coupled = jnp.einsum("ts,skn->tkn", panel, flux_all, precision=HI)
-    coupled, w_send = lax.optimization_barrier((coupled, w_send))
     w_recv = lax.all_to_all(
         w_send.reshape(n_source, cap * directions), "cell", split_axis=0, concat_axis=0, tiled=True
     ).reshape(n_slot, directions)

time: 104 us -> 99.6 us (0.958)
  waiting for transfers between devices: 27.3 us -> 43.6 us
  blocking collectives: 15.4 us -> 0 us
  starting transfers between devices: 39.2 us -> 35.2 us
    all_gather x1 -> x0, blocking collectives: 15.4 us -> none  [local(): flux_all = lax.all_gather(flux_late, 'tm', axis=0, tiled=True).astype(f32)]
    all_to_all x1, waiting for transfers between devices: 0.01 us -> 11 us  [local(): lax.all_to_all(partial.reshape(n_source, cap * directions), 'cell', split...]
    all_to_all x1, starting transfers between devices: 12.4 us -> 4.8 us  [local(): lax.all_to_all(w_send.reshape(n_source, cap * directions), 'cell', split_...]
    all_to_all x1, waiting for transfers between devices: 3.35 us -> 9.86 us  [local(): lax.all_to_all(copies, 'tm', split_axis=0, concat_axis=0, tiled=True)]
    all_to_all x1, starting transfers between devices: 3.84 us -> 7.5 us  [local(): lax.all_to_all(copies, 'tm', split_axis=0, concat_axis=0, tiled=True)]
    unnamed x20, local copies, waits for them, and re-layouts: 5.21 us -> 3.75 us
    all_to_all x1, waiting for transfers between devices: 11 us -> 9.78 us  [local(): lax.all_to_all(w_send.reshape(n_source, cap * directions), 'cell', split_...]
  transfers between devices with their start and end apart: 4 -> 4, of which waited for: 3 -> 4; matrix products, arithmetic and copies ran while one was open for 2% -> 1% of each run, Pallas kernels for 0% -> 0%
where the time goes in v15:
time: 99.6 us; the launch traced here: 99.2 us
  waiting for transfers between devices  43.6 us (44%)
  starting transfers between devices  35.2 us (35%)
  local copies, waits for them, and re-layouts  10.1 us (10%)
  matrix products  6.48 us (7%)
  other arithmetic  2.69 us (3%)
  between operations  1.04 us (1%)
    all_to_all x1, starting transfers between devices, local(): recv = lax.all_to_all(send, 'cell', split_axis=0, concat_axis=0, tiled=True)  17.1 us
    all_to_all x1, waiting for transfers between devices, local(): recv = lax.all_to_all(send, 'cell', split_axis=0, concat_axis=0, tiled=True)  13 us
    all_to_all x1, waiting for transfers between devices, local(): lax.all_to_all(partial.reshape(n_source, cap * directions), 'cell', split...  11 us
    all_to_all x1, waiting for transfers between devices, local(): lax.all_to_all(copies, 'tm', split_axis=0, concat_axis=0, tiled=True)  9.86 us
    all_to_all x1, waiting for transfers between devices, local(): lax.all_to_all(w_send.reshape(n_source, cap * directions), 'cell', split_...  9.78 us
    all_to_all x1, starting transfers between devices, local(): lax.all_to_all(copies, 'tm', split_axis=0, concat_axis=0, tiled=True)  7.5 us
    all_to_all x1, starting transfers between devices, local(): lax.all_to_all(partial.reshape(n_source, cap * directions), 'cell', split...  5.81 us
    all_to_all x1, starting transfers between devices, local(): lax.all_to_all(w_send.reshape(n_source, cap * directions), 'cell', split_...  4.8 us
  transfers between devices with their start and end apart: 4, of which 4 were waited for; matrix products, arithmetic and copies ran while one was open for 1% of the time, Pallas kernels for 0%

profile of v15, /device:TPU:1, one launch (start us, length us, event | category | flops | bytes accessed | tf_op | source)
XLA Modules:
  0.0 99.2 jit_solution(3953022418747259753)
XLA Ops:
  0.7 0.8 copy.125
  1.6 0.7 iota_compare_fusion.11
  2.4 0.3 fusion.12
  2.7 0.5 fusion.8
  3.6 0.2 select_reduce_fusion
  4.1 1.4 %fusion.5 = f32[1,64,16]{2,0,1:T(1,128)S(1)} fusion(bf16[512,1,1]{0,1,2:T(2,128)(2,1)S(1)} %reshape.297, s32[64,16]{1,0:T(8,128)S(1)} %multiply_add_fusion, s32[512]{0:T(512)S(1)} %add_select_fusion.2), kind=kOutput, calls=%fused_computation.6 | convolution fusion | flops 1572864 | bytes 11264 | tf_op jit(solution)/shard_map/dot_general | solution.py:41
  5.7 0.5 broadcast.161
  6.2 0.8 reduce.3
  6.9 1.0 %reshape.306 = bf16[64,2,1088]{2,1,0:T(2,128)(2,1)} reshape(bf16[64,2176]{1,0:T(8,128)(2,1)S(1)} %reduce.3) | data formatting | bytes 557056
  7.9 17.1 %all-to-all-start = ((bf16[64,2,1088]{2,1,0:T(2,128)(2,1)}), bf16[64,2,1088]{2,1,0:T(2,128)(2,1)S(1)}, u32[]{:S(2)}, u32[]{:S(2)}) async-start(bf16[64,2,1088]{2,1,0:T(2,128)(2,1)} %reshape.306), calls=%async_computation | async-start | bytes 589824 | tf_op jit(solution)/shard_map/all_to_all | solution.py:45
  25.3 13.0 %all-to-all-done = bf16[64,2,1088]{2,1,0:T(2,128)(2,1)S(1)} async-done(((bf16[64,2,1088]{2,1,0:T(2,128)(2,1)}), bf16[64,2,1088]{2,1,0:T(2,128)(2,1)S(1)}, u32[]{:S(2)}, u32[]{:S(2)}) %all-to-all-start) | async-done | bytes 278560 | tf_op jit(solution)/shard_map/all_to_all | solution.py:45
  38.3 0.3 reshape.307
  38.9 0.3 fusion.7
  39.5 0.9 all_to_all.31
  40.3 5.8 %all-to-all-start.1 = ((f32[64,1,256]{2,1,0:T(1,128)}), f32[64,1,256]{2,1,0:T(1,128)S(1)}, u32[]{:S(2)}, u32[]{:S(2)}) async-start(f32[64,1,256]{2,1,0:T(1,128)} %all_to_all.31), calls=%async_computation.1 | async-start | bytes 131072 | tf_op jit(solution)/shard_map/all_to_all | solution.py:56
  46.2 11.0 %all-to-all-done.1 = f32[64,1,256]{2,1,0:T(1,128)S(1)} async-done(((f32[64,1,256]{2,1,0:T(1,128)}), f32[64,1,256]{2,1,0:T(1,128)S(1)}, u32[]{:S(2)}, u32[]{:S(2)}) %all-to-all-start.1) | async-done | bytes 65568 | tf_op jit(solution)/shard_map/all_to_all | solution.py:56
  57.6 1.1 %fusion.9 = f32[64,16]{1,0:T(8,128)S(1)} fusion(s32[64,8]{1,0:T(8,128)S(1)} %fusion.33, f32[1024,16]{1,0:T(8,128)S(1)} %reshape.291), kind=kOutput, calls=%fused_computation.11 | convolution fusion | flops 101194752 | bytes 71680 | tf_op jit(solution)/shard_map/dot_general | solution.py:61
  59.0 0.9 broadcast_in_dim.52
  59.9 7.5 %all-to-all-start.2 = ((bf16[8,280,128]{2,1,0:T(8,128)(2,1)}), bf16[8,280,128]{2,1,0:T(8,128)(2,1)S(1)}, u32[]{:S(2)}, u32[]{:S(2)}) async-start(bf16[8,280,128]{2,1,0:T(8,128)(2,1)} %broadcast_in_dim.52), calls=%async_computation.2 | async-start | bytes 1146880 | tf_op jit(solution)/shard_map/all_to_all | solution.py:72
  67.5 9.9 %all-to-all-done.2 = bf16[8,280,128]{2,1,0:T(8,128)(2,1)S(1)} async-done(((bf16[8,280,128]{2,1,0:T(8,128)(2,1)}), bf16[8,280,128]{2,1,0:T(8,128)(2,1)S(1)}, u32[]{:S(2)}, u32[]{:S(2)}) %all-to-all-start.2) | async-done | bytes 573472 | tf_op jit(solution)/shard_map/all_to_all | solution.py:72
  77.4 0.2 reshape.296
  77.8 1.0 %fusion = f32[1024,16]{1,0:T(8,128)S(1)} fusion(s32[512]{0:T(512)S(1)} %add_select_fusion.2, f32[64,16]{1,0:T(8,128)S(1)} %broadcast_multiply_fusion.1), kind=kOutput, calls=%fused_computation.1 | convolution fusion | flops 101187584 | bytes 71680 | tf_op jit(solution)/shard_map/dot_general | solution.py:80
  78.9 0.9 all_to_all.32
  79.7 4.8 %all-to-all-start.3 = ((f32[64,1,256]{2,1,0:T(1,128)}), f32[64,1,256]{2,1,0:T(1,128)S(1)}, u32[]{:S(2)}, u32[]{:S(2)}) async-start(f32[64,1,256]{2,1,0:T(1,128)} %all_to_all.32), calls=%async_computation.3 | async-start | bytes 131072 | tf_op jit(solution)/shard_map/all_to_all | solution.py:83
  84.6 0.7 copy.144
  85.3 0.3 reshape.294
  85.6 9.8 %all-to-all-done.3 = f32[64,1,256]{2,1,0:T(1,128)S(1)} async-done(((f32[64,1,256]{2,1,0:T(1,128)}), f32[64,1,256]{2,1,0:T(1,128)S(1)}, u32[]{:S(2)}, u32[]{:S(2)}) %all-to-all-start.3) | async-done | bytes 65568 | tf_op jit(solution)/shard_map/all_to_all | solution.py:83
  95.9 0.3 broadcast_multiply_fusion
  96.2 0.4 mul.90
  96.6 0.6 fusion.41
  97.2 1.3 %convolution_add_fusion = f32[4,16,512]{2,0,1:T(4,128)S(1)} fusion(bf16[32,16,512]{2,1,0:T(8,128)(2,1)S(1)} %reshape.294, f32[4,16,512]{2,1,0:T(8,128)S(1)} %reshape.293, f32[32,32]{1,0:T(8,128)} %param.15, s32[]{:T(128)S(6)} %select_n.39), kind=kOutput, calls=%fused_computation.12 | convolution fusion | flops 12615680 | bytes 788484 | tf_op jit(solution)/shard_map/ts,skn->tkn/dot_general | solution.py:82
  98.5 0.7 copy.145
  (60 shorter events, 3.3 us)
Async XLA Ops:
  0.6 2.1 %copy-start = (bf16[64,8,128]{2,1,0:T(8,128)(2,1)S(1)}, bf16[64,8,128]{2,1,0:T(8,128)(2,1)}, u32[]{:S(2)}) copy-start(bf16[64,8,128]{2,1,0:T(8,128)(2,1)} %param.9) | copy-start | bytes 393220
  1.5 1.9 %copy-start.4 = (s32[1,64,2]{1,2,0:T(2,128)S(1)}, s32[1,64,2]{1,2,0:T(2,128)}, u32[]{:S(2)}) copy-start(s32[1,64,2]{1,2,0:T(2,128)} %param.13) | copy-start | bytes 1540
  2.4 1.5 %copy-start.2 = (s32[64,8]{0,1:T(8,128)S(1)}, s32[64,8]{0,1:T(8,128)}, u32[]{:S(2)}) copy-start(s32[64,8]{0,1:T(8,128)} %param.11) | copy-start | bytes 6148
  5.5 19.5 %copy-start.1 = (bf16[4,16,512]{2,1,0:T(8,128)(2,1)S(1)}, bf16[4,16,512]{2,1,0:T(8,128)(2,1)}, u32[]{:S(2)}) copy-start(bf16[4,16,512]{2,1,0:T(8,128)(2,1)} %param.8) | copy-start | bytes 196612
  7.9 30.4 %all-to-all-start = ((bf16[64,2,1088]{2,1,0:T(2,128)(2,1)}), bf16[64,2,1088]{2,1,0:T(2,128)(2,1)S(1)}, u32[]{:S(2)}, u32[]{:S(2)}) async-start(bf16[64,2,1088]{2,1,0:T(2,128)(2,1)} %reshape.306), calls=%async_computation | async-start | bytes 589824 | tf_op jit(solution)/shard_map/all_to_all | solution.py:45
  38.9 7.2 %copy-start.3 = (s32[64,1]{0,1:T(1,128)S(1)}, s32[64,1]{0,1:T(1,128)}, u32[]{:S(2)}) copy-start(s32[64,1]{0,1:T(1,128)} %param.12) | copy-start | bytes 772
  40.3 16.9 %all-to-all-start.1 = ((f32[64,1,256]{2,1,0:T(1,128)}), f32[64,1,256]{2,1,0:T(1,128)S(1)}, u32[]{:S(2)}, u32[]{:S(2)}) async-start(f32[64,1,256]{2,1,0:T(1,128)} %all_to_all.31), calls=%async_computation.1 | async-start | bytes 131072 | tf_op jit(solution)/shard_map/all_to_all | solution.py:56
  59.9 17.5 %all-to-all-start.2 = ((bf16[8,280,128]{2,1,0:T(8,128)(2,1)}), bf16[8,280,128]{2,1,0:T(8,128)(2,1)S(1)}, u32[]{:S(2)}, u32[]{:S(2)}) async-start(bf16[8,280,128]{2,1,0:T(8,128)(2,1)} %broadcast_in_dim.52), calls=%async_computation.2 | async-start | bytes 1146880 | tf_op jit(solution)/shard_map/all_to_all | solution.py:72
  67.5 10.2 %copy-start.5 = (f32[64]{0:T(128)S(1)}, f32[64]{0:T(128)}, u32[]{:S(2)}) copy-start(f32[64]{0:T(128)} %param.14) | copy-start | bytes 772
  79.7 15.7 %all-to-all-start.3 = ((f32[64,1,256]{2,1,0:T(1,128)}), f32[64,1,256]{2,1,0:T(1,128)S(1)}, u32[]{:S(2)}, u32[]{:S(2)}) async-start(f32[64,1,256]{2,1,0:T(1,128)} %all_to_all.32), calls=%async_computation.3 | async-start | bytes 131072 | tf_op jit(solution)/shard_map/all_to_all | solution.py:83

commit v16 on v15

--- a/solution.py
+++ b/solution.py
@@ -83,6 +83,7 @@
     w_recv = lax.all_to_all(
         w_send.reshape(n_source, cap * directions), "cell", split_axis=0, concat_axis=0, tiled=True
     ).reshape(n_slot, directions)
+    coupled, w_recv = lax.optimization_barrier((coupled, w_recv))
 
     hot_tt = meta_hot.reshape(n_slot, tiles, slices).transpose(0, 2, 1)
     w_meta = (hot_tt[:, :, None, :] * w_recv[:, None, :, None]).reshape(n_slot, n_meta * directions)

time: 99.6 us -> 101 us (1.014)
  local copies, waits for them, and re-layouts: 10.1 us -> 11.4 us
    unnamed x20 -> x16, local copies, waits for them, and re-layouts: 3.75 us -> 5.06 us
  transfers between devices with their start and end apart: 4 -> 4, of which waited for: 4 -> 4; matrix products, arithmetic and copies ran while one was open for 1% -> 2% of each run, Pallas kernels for 0% -> 0%
where the time goes in v16:
time: 101 us; the launch traced here: 100 us
  waiting for transfers between devices  43.6 us (43%)
  starting transfers between devices  35.1 us (35%)
  local copies, waits for them, and re-layouts  11.4 us (11%)
  matrix products  6.47 us (6%)
  other arithmetic  2.83 us (3%)
  between operations  1.03 us (1%)
    all_to_all x1, starting transfers between devices, local(): recv = lax.all_to_all(send, 'cell', split_axis=0, concat_axis=0, tiled=True)  17.1 us
    all_to_all x1, waiting for transfers between devices, local(): recv = lax.all_to_all(send, 'cell', split_axis=0, concat_axis=0, tiled=True)  13 us
    all_to_all x1, waiting for transfers between devices, local(): lax.all_to_all(partial.reshape(n_source, cap * directions), 'cell', split...  11 us
    all_to_all x1, waiting for transfers between devices, local(): lax.all_to_all(w_send.reshape(n_source, cap * directions), 'cell', split_...  9.83 us
    all_to_all x1, waiting for transfers between devices, local(): lax.all_to_all(copies, 'tm', split_axis=0, concat_axis=0, tiled=True)  9.79 us
    all_to_all x1, starting transfers between devices, local(): lax.all_to_all(copies, 'tm', split_axis=0, concat_axis=0, tiled=True)  7.51 us
    all_to_all x1, starting transfers between devices, local(): lax.all_to_all(partial.reshape(n_source, cap * directions), 'cell', split...  5.82 us
    unnamed x16, local copies, waits for them, and re-layouts  5.06 us
  transfers between devices with their start and end apart: 4, of which 4 were waited for; matrix products, arithmetic and copies ran while one was open for 2% of the time, Pallas kernels for 0%

profile of v16, /device:TPU:1, one launch (start us, length us, event | category | flops | bytes accessed | tf_op | source)
XLA Modules:
  0.0 100.4 jit_solution(13230110924038471361)
XLA Ops:
  0.7 0.8 iota_compare_fusion.11
  1.5 0.8 copy.124
  2.4 0.3 fusion.12
  2.7 0.8 copy.130
  3.5 0.8 copy.129
  4.9 1.4 %fusion.5 = f32[1,64,16]{2,0,1:T(1,128)S(1)} fusion(bf16[512,1,1]{0,1,2:T(2,128)(2,1)S(1)} %reshape.301, s32[64,16]{1,0:T(8,128)S(1)} %multiply_add_fusion, s32[512]{0:T(512)S(1)} %add_select_fusion.2), kind=kOutput, calls=%fused_computation.6 | convolution fusion | flops 1572864 | bytes 11264 | tf_op jit(solution)/shard_map/dot_general | solution.py:41
  6.3 0.5 fusion.8
  7.0 0.5 broadcast.162
  7.5 0.8 reduce.3
  8.3 1.0 reshape.310
  9.3 17.1 %all-to-all-start = ((bf16[64,2,1088]{2,1,0:T(2,128)(2,1)}), bf16[64,2,1088]{2,1,0:T(2,128)(2,1)S(1)}, u32[]{:S(2)}, u32[]{:S(2)}) async-start(bf16[64,2,1088]{2,1,0:T(2,128)(2,1)} %reshape.310), calls=%async_computation | async-start | bytes 589824 | tf_op jit(solution)/shard_map/all_to_all | solution.py:45
  26.6 13.0 %all-to-all-done = bf16[64,2,1088]{2,1,0:T(2,128)(2,1)S(1)} async-done(((bf16[64,2,1088]{2,1,0:T(2,128)(2,1)}), bf16[64,2,1088]{2,1,0:T(2,128)(2,1)S(1)}, u32[]{:S(2)}, u32[]{:S(2)}) %all-to-all-start) | async-done | bytes 278560 | tf_op jit(solution)/shard_map/all_to_all | solution.py:45
  39.6 0.3 reshape.311
  40.3 0.3 fusion.7
  40.8 0.9 all_to_all.31
  41.6 5.8 %all-to-all-start.1 = ((f32[64,1,256]{2,1,0:T(1,128)}), f32[64,1,256]{2,1,0:T(1,128)S(1)}, u32[]{:S(2)}, u32[]{:S(2)}) async-start(f32[64,1,256]{2,1,0:T(1,128)} %all_to_all.31), calls=%async_computation.1 | async-start | bytes 131072 | tf_op jit(solution)/shard_map/all_to_all | solution.py:56
  47.5 11.0 %all-to-all-done.1 = f32[64,1,256]{2,1,0:T(1,128)S(1)} async-done(((f32[64,1,256]{2,1,0:T(1,128)}), f32[64,1,256]{2,1,0:T(1,128)S(1)}, u32[]{:S(2)}, u32[]{:S(2)}) %all-to-all-start.1) | async-done | bytes 65568 | tf_op jit(solution)/shard_map/all_to_all | solution.py:56
  58.9 1.1 %fusion.9 = f32[64,16]{1,0:T(8,128)S(1)} fusion(s32[64,8]{1,0:T(8,128)S(1)} %fusion.34, f32[1024,16]{1,0:T(8,128)S(1)} %reshape.294), kind=kOutput, calls=%fused_computation.11 | convolution fusion | flops 101194752 | bytes 71680 | tf_op jit(solution)/shard_map/dot_general | solution.py:61
  60.4 0.9 broadcast_in_dim.53
  61.2 7.5 %all-to-all-start.2 = ((bf16[8,280,128]{2,1,0:T(8,128)(2,1)}), bf16[8,280,128]{2,1,0:T(8,128)(2,1)S(1)}, u32[]{:S(2)}, u32[]{:S(2)}) async-start(bf16[8,280,128]{2,1,0:T(8,128)(2,1)} %broadcast_in_dim.53), calls=%async_computation.2 | async-start | bytes 1146880 | tf_op jit(solution)/shard_map/all_to_all | solution.py:72
  69.0 9.8 %all-to-all-done.2 = bf16[8,280,128]{2,1,0:T(8,128)(2,1)S(1)} async-done(((bf16[8,280,128]{2,1,0:T(8,128)(2,1)}), bf16[8,280,128]{2,1,0:T(8,128)(2,1)S(1)}, u32[]{:S(2)}, u32[]{:S(2)}) %all-to-all-start.2) | async-done | bytes 573472 | tf_op jit(solution)/shard_map/all_to_all | solution.py:72
  78.8 0.3 reshape.295
  79.5 0.7 copy.143
  80.2 1.0 %fusion = f32[1024,16]{1,0:T(8,128)S(1)} fusion(s32[512]{0:T(512)S(1)} %add_select_fusion.2, f32[64,16]{1,0:T(8,128)S(1)} %broadcast_multiply_fusion.1), kind=kOutput, calls=%fused_computation.1 | convolution fusion | flops 101187584 | bytes 71680 | tf_op jit(solution)/shard_map/dot_general | solution.py:80
  81.2 0.9 all_to_all.32
  82.1 4.6 %all-to-all-start.3 = ((f32[64,1,256]{2,1,0:T(1,128)}), f32[64,1,256]{2,1,0:T(1,128)S(1)}, u32[]{:S(2)}, u32[]{:S(2)}) async-start(f32[64,1,256]{2,1,0:T(1,128)} %all_to_all.32), calls=%async_computation.3 | async-start | bytes 131072 | tf_op jit(solution)/shard_map/all_to_all | solution.py:83
  86.7 1.2 %fusion.19 = f32[4,16,512]{2,0,1:T(4,128)S(1)} fusion(bf16[32,16,512]{2,1,0:T(8,128)(2,1)S(1)} %reshape.295, f32[32,32]{1,0:T(8,128)} %param.15, s32[]{:T(128)S(6)} %select_n.39), kind=kOutput, calls=%fused_computation.21 | convolution fusion | flops 12582912 | bytes 657412 | tf_op jit(solution)/shard_map/ts,skn->tkn/dot_general | solution.py:82
  88.0 9.8 %all-to-all-done.3 = f32[64,1,256]{2,1,0:T(1,128)S(1)} async-done(((f32[64,1,256]{2,1,0:T(1,128)}), f32[64,1,256]{2,1,0:T(1,128)S(1)}, u32[]{:S(2)}, u32[]{:S(2)}) %all-to-all-start.3) | async-done | bytes 65568 | tf_op jit(solution)/shard_map/all_to_all | solution.py:83
  98.3 0.3 broadcast_multiply_fusion
  98.6 0.4 mul.88
  99.0 0.6 fusion.42
  99.7 0.7 copy.144
  (57 shorter events, 3.7 us)
Async XLA Ops:
  0.6 5.6 %copy-start = (bf16[64,8,128]{2,1,0:T(8,128)(2,1)S(1)}, bf16[64,8,128]{2,1,0:T(8,128)(2,1)}, u32[]{:S(2)}) copy-start(bf16[64,8,128]{2,1,0:T(8,128)(2,1)} %param.9) | copy-start | bytes 393220
  6.9 19.5 %copy-start.1 = (bf16[4,16,512]{2,1,0:T(8,128)(2,1)S(1)}, bf16[4,16,512]{2,1,0:T(8,128)(2,1)}, u32[]{:S(2)}) copy-start(bf16[4,16,512]{2,1,0:T(8,128)(2,1)} %param.8) | copy-start | bytes 196612
  9.3 30.4 %all-to-all-start = ((bf16[64,2,1088]{2,1,0:T(2,128)(2,1)}), bf16[64,2,1088]{2,1,0:T(2,128)(2,1)S(1)}, u32[]{:S(2)}, u32[]{:S(2)}) async-start(bf16[64,2,1088]{2,1,0:T(2,128)(2,1)} %reshape.310), calls=%async_computation | async-start | bytes 589824 | tf_op jit(solution)/shard_map/all_to_all | solution.py:45
  40.3 7.2 %copy-start.2 = (s32[64,1]{0,1:T(1,128)S(1)}, s32[64,1]{0,1:T(1,128)}, u32[]{:S(2)}) copy-start(s32[64,1]{0,1:T(1,128)} %param.12) | copy-start | bytes 772
  41.6 16.9 %all-to-all-start.1 = ((f32[64,1,256]{2,1,0:T(1,128)}), f32[64,1,256]{2,1,0:T(1,128)S(1)}, u32[]{:S(2)}, u32[]{:S(2)}) async-start(f32[64,1,256]{2,1,0:T(1,128)} %all_to_all.31), calls=%async_computation.1 | async-start | bytes 131072 | tf_op jit(solution)/shard_map/all_to_all | solution.py:56
  61.2 17.5 %all-to-all-start.2 = ((bf16[8,280,128]{2,1,0:T(8,128)(2,1)}), bf16[8,280,128]{2,1,0:T(8,128)(2,1)S(1)}, u32[]{:S(2)}, u32[]{:S(2)}) async-start(bf16[8,280,128]{2,1,0:T(8,128)(2,1)} %broadcast_in_dim.53), calls=%async_computation.2 | async-start | bytes 1146880 | tf_op jit(solution)/shard_map/all_to_all | solution.py:72
  79.1 1.0 %copy-start.3 = (f32[64]{0:T(128)S(1)}, f32[64]{0:T(128)}, u32[]{:S(2)}) copy-start(f32[64]{0:T(128)} %param.14) | copy-start | bytes 772
  82.1 15.7 %all-to-all-start.3 = ((f32[64,1,256]{2,1,0:T(1,128)}), f32[64,1,256]{2,1,0:T(1,128)S(1)}, u32[]{:S(2)}, u32[]{:S(2)}) async-start(f32[64,1,256]{2,1,0:T(1,128)} %all_to_all.32), calls=%async_computation.3 | async-start | bytes 131072 | tf_op jit(solution)/shard_map/all_to_all | solution.py:83

commit v17 on v15

--- a/solution.py
+++ b/solution.py
@@ -38,7 +38,7 @@
     place_b = place.astype(jnp.bfloat16)
     foot_flat = foot.reshape(n_blocks, TILE)
     foot_send = jnp.dot(place_b, foot_flat, preferred_element_type=f32).astype(jnp.bfloat16)
-    meta_send = jnp.dot(place_b, meta.astype(jnp.bfloat16)[:, None], preferred_element_type=f32)
+    meta_send = jnp.sum(jnp.where(place, meta[None, :], 0), axis=1)
     meta_send = meta_send.reshape(n_source, cap).astype(jnp.bfloat16)
     meta_pad = jnp.zeros((n_source, TILE - cap), jnp.bfloat16)
     send = jnp.concatenate([foot_send.reshape(n_source, cap * TILE), meta_send, meta_pad], axis=1)

time: 99.6 us -> 99.8 us (level)
  matrix products: 6.48 us -> 5.09 us
  local copies, waits for them, and re-layouts: 10.1 us -> 11.4 us
    dot_general x1 -> x0, matrix products: 1.4 us -> none  [local(): jnp.dot(place_b, meta.astype(jnp.bfloat16)[:, None], preferred_element_ty...]
    unnamed x20 -> x16, local copies, waits for them, and re-layouts: 3.75 us -> 5.1 us
where the time goes in v17:
time: 99.8 us; the launch traced here: 99.4 us
  waiting for transfers between devices  43.6 us (44%)
  starting transfers between devices  35.3 us (35%)
  local copies, waits for them, and re-layouts  11.4 us (11%)
  matrix products  5.09 us (5%)
  other arithmetic  2.96 us (3%)
  between operations  1 us (1%)
    all_to_all x1, starting transfers between devices, local(): recv = lax.all_to_all(send, 'cell', split_axis=0, concat_axis=0, tiled=True)  17.1 us
    all_to_all x1, waiting for transfers between devices, local(): recv = lax.all_to_all(send, 'cell', split_axis=0, concat_axis=0, tiled=True)  13 us
    all_to_all x1, waiting for transfers between devices, local(): lax.all_to_all(partial.reshape(n_source, cap * directions), 'cell', split...  11 us
    all_to_all x1, waiting for transfers between devices, local(): lax.all_to_all(copies, 'tm', split_axis=0, concat_axis=0, tiled=True)  9.86 us
    all_to_all x1, waiting for transfers between devices, local(): lax.all_to_all(w_send.reshape(n_source, cap * directions), 'cell', split_...  9.78 us
    all_to_all x1, starting transfers between devices, local(): lax.all_to_all(copies, 'tm', split_axis=0, concat_axis=0, tiled=True)  7.51 us
    all_to_all x1, starting transfers between devices, local(): lax.all_to_all(partial.reshape(n_source, cap * directions), 'cell', split...  5.82 us
    unnamed x16, local copies, waits for them, and re-layouts  5.1 us
  transfers between devices with their start and end apart: 4, of which 4 were waited for; matrix products, arithmetic and copies ran while one was open for 1% of the time, Pallas kernels for 0%

profile of v17, /device:TPU:1, one launch (start us, length us, event | category | flops | bytes accessed | tf_op | source)
XLA Modules:
  0.0 99.4 jit_solution(3036497580534703347)
XLA Ops:
  0.6 0.8 copy.125
  1.6 0.7 iota_compare_fusion.11
  2.4 0.8 copy.131
  3.3 0.8 copy.130
  4.4 0.3 fusion.10
  4.7 0.5 fusion.6
  5.3 0.3 select_reduce_fusion
  5.8 0.5 broadcast.142
  6.3 0.8 reduce.3
  7.1 1.0 %reshape.287 = bf16[64,2,1088]{2,1,0:T(2,128)(2,1)} reshape(bf16[64,2176]{1,0:T(8,128)(2,1)S(1)} %reduce.3) | data formatting | bytes 557056
  8.1 17.1 %all-to-all-start = ((bf16[64,2,1088]{2,1,0:T(2,128)(2,1)}), bf16[64,2,1088]{2,1,0:T(2,128)(2,1)S(1)}, u32[]{:S(2)}, u32[]{:S(2)}) async-start(bf16[64,2,1088]{2,1,0:T(2,128)(2,1)} %reshape.287), calls=%async_computation | async-start | bytes 589824 | tf_op jit(solution)/shard_map/all_to_all | solution.py:45
  25.4 13.0 %all-to-all-done = bf16[64,2,1088]{2,1,0:T(2,128)(2,1)S(1)} async-done(((bf16[64,2,1088]{2,1,0:T(2,128)(2,1)}), bf16[64,2,1088]{2,1,0:T(2,128)(2,1)S(1)}, u32[]{:S(2)}, u32[]{:S(2)}) %all-to-all-start) | async-done | bytes 278560 | tf_op jit(solution)/shard_map/all_to_all | solution.py:45
  38.4 0.3 reshape.288
  39.1 0.3 fusion.5
  39.6 0.9 all_to_all.31
  40.5 5.8 %all-to-all-start.1 = ((f32[64,1,256]{2,1,0:T(1,128)}), f32[64,1,256]{2,1,0:T(1,128)S(1)}, u32[]{:S(2)}, u32[]{:S(2)}) async-start(f32[64,1,256]{2,1,0:T(1,128)} %all_to_all.31), calls=%async_computation.1 | async-start | bytes 131072 | tf_op jit(solution)/shard_map/all_to_all | solution.py:56
  46.4 11.0 %all-to-all-done.1 = f32[64,1,256]{2,1,0:T(1,128)S(1)} async-done(((f32[64,1,256]{2,1,0:T(1,128)}), f32[64,1,256]{2,1,0:T(1,128)S(1)}, u32[]{:S(2)}, u32[]{:S(2)}) %all-to-all-start.1) | async-done | bytes 65568 | tf_op jit(solution)/shard_map/all_to_all | solution.py:56
  57.7 1.1 %fusion.7 = f32[64,16]{1,0:T(8,128)S(1)} fusion(s32[64,8]{1,0:T(8,128)S(1)} %fusion.29, f32[1024,16]{1,0:T(8,128)S(1)} %reshape.275), kind=kOutput, calls=%fused_computation.10 | convolution fusion | flops 101194752 | bytes 71680 | tf_op jit(solution)/shard_map/dot_general | solution.py:61
  59.2 0.9 broadcast_in_dim.66
  60.1 7.5 %all-to-all-start.2 = ((bf16[8,280,128]{2,1,0:T(8,128)(2,1)}), bf16[8,280,128]{2,1,0:T(8,128)(2,1)S(1)}, u32[]{:S(2)}, u32[]{:S(2)}) async-start(bf16[8,280,128]{2,1,0:T(8,128)(2,1)} %broadcast_in_dim.66), calls=%async_computation.2 | async-start | bytes 1146880 | tf_op jit(solution)/shard_map/all_to_all | solution.py:72
  67.7 9.9 %all-to-all-done.2 = bf16[8,280,128]{2,1,0:T(8,128)(2,1)S(1)} async-done(((bf16[8,280,128]{2,1,0:T(8,128)(2,1)}), bf16[8,280,128]{2,1,0:T(8,128)(2,1)S(1)}, u32[]{:S(2)}, u32[]{:S(2)}) %all-to-all-start.2) | async-done | bytes 573472 | tf_op jit(solution)/shard_map/all_to_all | solution.py:72
  78.0 1.0 %fusion = f32[1024,16]{1,0:T(8,128)S(1)} fusion(s32[512]{0:T(512)S(1)} %get-tuple-element.22, f32[64,16]{1,0:T(8,128)S(1)} %broadcast_multiply_fusion.1), kind=kOutput, calls=%fused_computation.2 | convolution fusion | flops 101187584 | bytes 71680 | tf_op jit(solution)/shard_map/dot_general | solution.py:80
  79.0 0.9 all_to_all.32
  79.9 4.8 %all-to-all-start.3 = ((f32[64,1,256]{2,1,0:T(1,128)}), f32[64,1,256]{2,1,0:T(1,128)S(1)}, u32[]{:S(2)}, u32[]{:S(2)}) async-start(f32[64,1,256]{2,1,0:T(1,128)} %all_to_all.32), calls=%async_computation.3 | async-start | bytes 131072 | tf_op jit(solution)/shard_map/all_to_all | solution.py:83
  84.8 0.7 copy.144
  85.5 0.3 reshape.278
  85.8 9.8 %all-to-all-done.3 = f32[64,1,256]{2,1,0:T(1,128)S(1)} async-done(((f32[64,1,256]{2,1,0:T(1,128)}), f32[64,1,256]{2,1,0:T(1,128)S(1)}, u32[]{:S(2)}, u32[]{:S(2)}) %all-to-all-start.3) | async-done | bytes 65568 | tf_op jit(solution)/shard_map/all_to_all | solution.py:83
  96.1 0.3 broadcast_multiply_fusion
  96.4 0.4 mul.87
  96.7 0.6 fusion.37
  97.4 1.3 %convolution_add_fusion = f32[4,16,512]{2,0,1:T(4,128)S(1)} fusion(bf16[32,16,512]{2,1,0:T(8,128)(2,1)S(1)} %reshape.278, f32[4,16,512]{2,1,0:T(8,128)S(1)} %reshape.277, f32[32,32]{1,0:T(8,128)} %param.15, s32[]{:T(128)S(6)} %select_n.44), kind=kOutput, calls=%fused_computation.11 | convolution fusion | flops 12615680 | bytes 788484 | tf_op jit(solution)/shard_map/ts,skn->tkn/dot_general | solution.py:82
  98.7 0.7 copy.145
  (53 shorter events, 3.5 us)
Async XLA Ops:
  0.6 4.1 %copy-start = (bf16[64,8,128]{2,1,0:T(8,128)(2,1)S(1)}, bf16[64,8,128]{2,1,0:T(8,128)(2,1)}, u32[]{:S(2)}) copy-start(bf16[64,8,128]{2,1,0:T(8,128)(2,1)} %param.9) | copy-start | bytes 393220
  5.7 19.5 %copy-start.1 = (bf16[4,16,512]{2,1,0:T(8,128)(2,1)S(1)}, bf16[4,16,512]{2,1,0:T(8,128)(2,1)}, u32[]{:S(2)}) copy-start(bf16[4,16,512]{2,1,0:T(8,128)(2,1)} %param.8) | copy-start | bytes 196612
  8.1 30.4 %all-to-all-start = ((bf16[64,2,1088]{2,1,0:T(2,128)(2,1)}), bf16[64,2,1088]{2,1,0:T(2,128)(2,1)S(1)}, u32[]{:S(2)}, u32[]{:S(2)}) async-start(bf16[64,2,1088]{2,1,0:T(2,128)(2,1)} %reshape.287), calls=%async_computation | async-start | bytes 589824 | tf_op jit(solution)/shard_map/all_to_all | solution.py:45
  39.1 7.2 %copy-start.2 = (s32[64,1]{0,1:T(1,128)S(1)}, s32[64,1]{0,1:T(1,128)}, u32[]{:S(2)}) copy-start(s32[64,1]{0,1:T(1,128)} %param.12) | copy-start | bytes 772
  40.5 16.9 %all-to-all-start.1 = ((f32[64,1,256]{2,1,0:T(1,128)}), f32[64,1,256]{2,1,0:T(1,128)S(1)}, u32[]{:S(2)}, u32[]{:S(2)}) async-start(f32[64,1,256]{2,1,0:T(1,128)} %all_to_all.31), calls=%async_computation.1 | async-start | bytes 131072 | tf_op jit(solution)/shard_map/all_to_all | solution.py:56
  60.1 17.5 %all-to-all-start.2 = ((bf16[8,280,128]{2,1,0:T(8,128)(2,1)}), bf16[8,280,128]{2,1,0:T(8,128)(2,1)S(1)}, u32[]{:S(2)}, u32[]{:S(2)}) async-start(bf16[8,280,128]{2,1,0:T(8,128)(2,1)} %broadcast_in_dim.66), calls=%async_computation.2 | async-start | bytes 1146880 | tf_op jit(solution)/shard_map/all_to_all | solution.py:72
  67.7 10.2 %copy-start.3 = (f32[64]{0:T(128)S(1)}, f32[64]{0:T(128)}, u32[]{:S(2)}) copy-start(f32[64]{0:T(128)} %param.14) | copy-start | bytes 772
  79.9 15.7 %all-to-all-start.3 = ((f32[64,1,256]{2,1,0:T(1,128)}), f32[64,1,256]{2,1,0:T(1,128)S(1)}, u32[]{:S(2)}, u32[]{:S(2)}) async-start(f32[64,1,256]{2,1,0:T(1,128)} %all_to_all.32), calls=%async_computation.3 | async-start | bytes 131072 | tf_op jit(solution)/shard_map/all_to_all | solution.py:83

commit v18 on v17

--- a/solution.py
+++ b/solution.py
@@ -42,7 +42,9 @@
     meta_send = meta_send.reshape(n_source, cap).astype(jnp.bfloat16)
     meta_pad = jnp.zeros((n_source, TILE - cap), jnp.bfloat16)
     send = jnp.concatenate([foot_send.reshape(n_source, cap * TILE), meta_send, meta_pad], axis=1)
+    send = send.reshape(n_source, 2, (cap + 1) * TILE // 2)
     recv = lax.all_to_all(send, "cell", split_axis=0, concat_axis=0, tiled=True)
+    recv = recv.reshape(n_source, (cap + 1) * TILE)
 
     my_group = lax.axis_index("tm")
     groups = lax.axis_size("tm")

time: 99.8 us -> 98.4 us (0.986)
    unnamed x16 -> x13, local copies, waits for them, and re-layouts: 5.1 us -> 3.75 us
    reshape x0 -> x2, local copies, waits for them, and re-layouts: none -> 1.21 us  [the longest x1 1 us: local(): send = send.reshape(n_source, 2, (cap + 1) * TILE // 2)]
  transfers between devices with their start and end apart: 4 -> 4, of which waited for: 4 -> 4; matrix products, arithmetic and copies ran while one was open for 1% -> 2% of each run, Pallas kernels for 0% -> 0%
where the time goes in v18:
time: 98.4 us; the launch traced here: 97.9 us
  waiting for transfers between devices  43.6 us (44%)
  starting transfers between devices  35.3 us (36%)
  local copies, waits for them, and re-layouts  10.8 us (11%)
  matrix products  5.09 us (5%)
  other arithmetic  2.2 us (2%)
  between operations  0.99 us (1%)
    all_to_all x1, starting transfers between devices, local(): recv = lax.all_to_all(send, 'cell', split_axis=0, concat_axis=0, tiled=True)  17.1 us
    all_to_all x1, waiting for transfers between devices, local(): recv = lax.all_to_all(send, 'cell', split_axis=0, concat_axis=0, tiled=True)  13 us
    all_to_all x1, waiting for transfers between devices, local(): lax.all_to_all(partial.reshape(n_source, cap * directions), 'cell', split...  11 us
    all_to_all x1, waiting for transfers between devices, local(): lax.all_to_all(copies, 'tm', split_axis=0, concat_axis=0, tiled=True)  9.86 us
    all_to_all x1, waiting for transfers between devices, local(): lax.all_to_all(w_send.reshape(n_source, cap * directions), 'cell', split_...  9.78 us
    all_to_all x1, starting transfers between devices, local(): lax.all_to_all(copies, 'tm', split_axis=0, concat_axis=0, tiled=True)  7.51 us
    all_to_all x1, starting transfers between devices, local(): lax.all_to_all(partial.reshape(n_source, cap * directions), 'cell', split...  5.82 us
    all_to_all x1, starting transfers between devices, local(): lax.all_to_all(w_send.reshape(n_source, cap * directions), 'cell', split_...  4.8 us
  transfers between devices with their start and end apart: 4, of which 4 were waited for; matrix products, arithmetic and copies ran while one was open for 2% of the time, Pallas kernels for 0%

profile of v18, /device:TPU:1, one launch (start us, length us, event | category | flops | bytes accessed | tf_op | source)
XLA Modules:
  0.0 97.9 jit_solution(9237375172328397157)
XLA Ops:
  0.6 0.8 copy.103
  1.6 0.7 iota_compare_fusion.11
  2.4 0.8 copy.109
  3.3 0.8 copy.108
  4.2 0.2 select_reduce_fusion.1
  4.4 0.3 fusion.10
  4.7 0.5 fusion.6
  5.3 0.3 select_reduce_fusion
  5.8 1.0 %reshape.276 = bf16[64,2,1088]{2,1,0:T(2,128)(2,1)} reshape(bf16[64,2176]{1,0:T(8,128)(2,1)S(1)} %concatenate.6) | data formatting | bytes 557056 | tf_op jit(solution)/shard_map/reshape | solution.py:45
  6.8 17.1 %all-to-all-start = ((bf16[64,2,1088]{2,1,0:T(2,128)(2,1)}), bf16[64,2,1088]{2,1,0:T(2,128)(2,1)S(1)}, u32[]{:S(2)}, u32[]{:S(2)}) async-start(bf16[64,2,1088]{2,1,0:T(2,128)(2,1)} %reshape.276), calls=%async_computation | async-start | bytes 589824 | tf_op jit(solution)/shard_map/all_to_all | solution.py:46
  24.2 13.0 %all-to-all-done = bf16[64,2,1088]{2,1,0:T(2,128)(2,1)S(1)} async-done(((bf16[64,2,1088]{2,1,0:T(2,128)(2,1)}), bf16[64,2,1088]{2,1,0:T(2,128)(2,1)S(1)}, u32[]{:S(2)}, u32[]{:S(2)}) %all-to-all-start) | async-done | bytes 278560 | tf_op jit(solution)/shard_map/all_to_all | solution.py:46
  37.2 0.2 reshape.277
  37.7 0.3 fusion.5
  38.2 0.9 all_to_all.24
  39.0 5.8 %all-to-all-start.1 = ((f32[64,1,256]{2,1,0:T(1,128)}), f32[64,1,256]{2,1,0:T(1,128)S(1)}, u32[]{:S(2)}, u32[]{:S(2)}) async-start(f32[64,1,256]{2,1,0:T(1,128)} %all_to_all.24), calls=%async_computation.1 | async-start | bytes 131072 | tf_op jit(solution)/shard_map/all_to_all | solution.py:58
  45.0 11.0 %all-to-all-done.1 = f32[64,1,256]{2,1,0:T(1,128)S(1)} async-done(((f32[64,1,256]{2,1,0:T(1,128)}), f32[64,1,256]{2,1,0:T(1,128)S(1)}, u32[]{:S(2)}, u32[]{:S(2)}) %all-to-all-start.1) | async-done | bytes 65568 | tf_op jit(solution)/shard_map/all_to_all | solution.py:58
  56.3 1.1 %fusion.7 = f32[64,16]{1,0:T(8,128)S(1)} fusion(s32[64,8]{1,0:T(8,128)S(1)} %fusion.29, f32[1024,16]{1,0:T(8,128)S(1)} %reshape.281), kind=kOutput, calls=%fused_computation.10 | convolution fusion | flops 101194752 | bytes 71680 | tf_op jit(solution)/shard_map/dot_general | solution.py:63
  57.8 0.9 broadcast_in_dim.66
  58.6 7.5 %all-to-all-start.2 = ((bf16[8,280,128]{2,1,0:T(8,128)(2,1)}), bf16[8,280,128]{2,1,0:T(8,128)(2,1)S(1)}, u32[]{:S(2)}, u32[]{:S(2)}) async-start(bf16[8,280,128]{2,1,0:T(8,128)(2,1)} %broadcast_in_dim.66), calls=%async_computation.2 | async-start | bytes 1146880 | tf_op jit(solution)/shard_map/all_to_all | solution.py:74
  66.3 9.9 %all-to-all-done.2 = bf16[8,280,128]{2,1,0:T(8,128)(2,1)S(1)} async-done(((bf16[8,280,128]{2,1,0:T(8,128)(2,1)}), bf16[8,280,128]{2,1,0:T(8,128)(2,1)S(1)}, u32[]{:S(2)}, u32[]{:S(2)}) %all-to-all-start.2) | async-done | bytes 573472 | tf_op jit(solution)/shard_map/all_to_all | solution.py:74
  76.2 0.2 reshape.286
  76.6 1.0 %fusion = f32[1024,16]{1,0:T(8,128)S(1)} fusion(s32[512]{0:T(512)S(1)} %get-tuple-element.20, f32[64,16]{1,0:T(8,128)S(1)} %broadcast_multiply_fusion.1), kind=kOutput, calls=%fused_computation.2 | convolution fusion | flops 101187584 | bytes 71680 | tf_op jit(solution)/shard_map/dot_general | solution.py:82
  77.6 0.9 all_to_all.25
  78.5 4.8 %all-to-all-start.3 = ((f32[64,1,256]{2,1,0:T(1,128)}), f32[64,1,256]{2,1,0:T(1,128)S(1)}, u32[]{:S(2)}, u32[]{:S(2)}) async-start(f32[64,1,256]{2,1,0:T(1,128)} %all_to_all.25), calls=%async_computation.3 | async-start | bytes 131072 | tf_op jit(solution)/shard_map/all_to_all | solution.py:85
  83.4 0.7 copy.121
  84.1 0.3 reshape.284
  84.4 9.8 %all-to-all-done.3 = f32[64,1,256]{2,1,0:T(1,128)S(1)} async-done(((f32[64,1,256]{2,1,0:T(1,128)}), f32[64,1,256]{2,1,0:T(1,128)S(1)}, u32[]{:S(2)}, u32[]{:S(2)}) %all-to-all-start.3) | async-done | bytes 65568 | tf_op jit(solution)/shard_map/all_to_all | solution.py:85
  94.7 0.3 broadcast_multiply_fusion
  95.0 0.4 mul.87
  95.3 0.6 fusion.37
  96.0 1.3 %convolution_add_fusion = f32[4,16,512]{2,0,1:T(4,128)S(1)} fusion(bf16[32,16,512]{2,1,0:T(8,128)(2,1)S(1)} %reshape.284, f32[4,16,512]{2,1,0:T(8,128)S(1)} %reshape.283, f32[32,32]{1,0:T(8,128)} %param.15, s32[]{:T(128)S(6)} %select_n.44), kind=kOutput, calls=%fused_computation.11 | convolution fusion | flops 12615680 | bytes 788484 | tf_op jit(solution)/shard_map/ts,skn->tkn/dot_general | solution.py:84
  97.2 0.7 copy.122
  (50 shorter events, 3.0 us)
Async XLA Ops:
  0.6 4.1 %copy-start = (bf16[64,8,128]{2,1,0:T(8,128)(2,1)S(1)}, bf16[64,8,128]{2,1,0:T(8,128)(2,1)}, u32[]{:S(2)}) copy-start(bf16[64,8,128]{2,1,0:T(8,128)(2,1)} %param.9) | copy-start | bytes 393220
  5.2 18.8 %copy-start.1 = (bf16[4,16,512]{2,1,0:T(8,128)(2,1)S(1)}, bf16[4,16,512]{2,1,0:T(8,128)(2,1)}, u32[]{:S(2)}) copy-start(bf16[4,16,512]{2,1,0:T(8,128)(2,1)} %param.8) | copy-start | bytes 196612
  6.8 30.4 %all-to-all-start = ((bf16[64,2,1088]{2,1,0:T(2,128)(2,1)}), bf16[64,2,1088]{2,1,0:T(2,128)(2,1)S(1)}, u32[]{:S(2)}, u32[]{:S(2)}) async-start(bf16[64,2,1088]{2,1,0:T(2,128)(2,1)} %reshape.276), calls=%async_computation | async-start | bytes 589824 | tf_op jit(solution)/shard_map/all_to_all | solution.py:46
  37.7 7.2 %copy-start.2 = (s32[64,1]{0,1:T(1,128)S(1)}, s32[64,1]{0,1:T(1,128)}, u32[]{:S(2)}) copy-start(s32[64,1]{0,1:T(1,128)} %param.12) | copy-start | bytes 772
  39.0 16.9 %all-to-all-start.1 = ((f32[64,1,256]{2,1,0:T(1,128)}), f32[64,1,256]{2,1,0:T(1,128)S(1)}, u32[]{:S(2)}, u32[]{:S(2)}) async-start(f32[64,1,256]{2,1,0:T(1,128)} %all_to_all.24), calls=%async_computation.1 | async-start | bytes 131072 | tf_op jit(solution)/shard_map/all_to_all | solution.py:58
  58.6 17.5 %all-to-all-start.2 = ((bf16[8,280,128]{2,1,0:T(8,128)(2,1)}), bf16[8,280,128]{2,1,0:T(8,128)(2,1)S(1)}, u32[]{:S(2)}, u32[]{:S(2)}) async-start(bf16[8,280,128]{2,1,0:T(8,128)(2,1)} %broadcast_in_dim.66), calls=%async_computation.2 | async-start | bytes 1146880 | tf_op jit(solution)/shard_map/all_to_all | solution.py:74
  66.3 10.2 %copy-start.3 = (f32[64]{0:T(128)S(1)}, f32[64]{0:T(128)}, u32[]{:S(2)}) copy-start(f32[64]{0:T(128)} %param.14) | copy-start | bytes 772
  78.5 15.7 %all-to-all-start.3 = ((f32[64,1,256]{2,1,0:T(1,128)}), f32[64,1,256]{2,1,0:T(1,128)S(1)}, u32[]{:S(2)}, u32[]{:S(2)}) async-start(f32[64,1,256]{2,1,0:T(1,128)} %all_to_all.25), calls=%async_computation.3 | async-start | bytes 131072 | tf_op jit(solution)/shard_map/all_to_all | solution.py:85

commit v19 on v18

--- a/solution.py
+++ b/solution.py
@@ -56,7 +56,7 @@
     every = jnp.dot(foot_r, panels, preferred_element_type=f32).reshape(n_slot, n_meta, directions)
     partial = jnp.sum(every * meta_hot[:, :, None], axis=1)
     back = lax.all_to_all(
-        partial.reshape(n_source, cap * directions), "cell", split_axis=0, concat_axis=0, tiled=True
+        partial.reshape(n_source, 2, cap * directions // 2), "cell", split_axis=0, concat_axis=0, tiled=True
     ).reshape(n_slot, directions)
 
     place_f = place.astype(f32)
@@ -83,7 +83,7 @@
     panel = lax.dynamic_slice(prior, (my_group * slices, 0), (slices, groups * slices))
     coupled = jnp.einsum("ts,skn->tkn", panel, flux_all, precision=HI)
     w_recv = lax.all_to_all(
-        w_send.reshape(n_source, cap * directions), "cell", split_axis=0, concat_axis=0, tiled=True
+        w_send.reshape(n_source, 2, cap * directions // 2), "cell", split_axis=0, concat_axis=0, tiled=True
     ).reshape(n_slot, directions)
 
     hot_tt = meta_hot.reshape(n_slot, tiles, slices).transpose(0, 2, 1)

time: 98.4 us -> 98.1 us (level)
    reshape x1 -> x3, local copies, waits for them, and re-layouts: 0.19 us -> 1.94 us  [the longest x1 0.87 us: local(): partial.reshape(n_source, 2, cap * directions // 2)]
    all_to_all x2 -> x0, local copies, waits for them, and re-layouts: 1.72 us -> none  [the longest x1 0.86 us: local(): lax.all_to_all(partial.reshape(n_source, cap * directions), 'cell', split...]
where the time goes in v19:
time: 98.1 us; the launch traced here: 97.7 us
  waiting for transfers between devices  43.8 us (45%)
  starting transfers between devices  35.1 us (36%)
  local copies, waits for them, and re-layouts  10.8 us (11%)
  matrix products  5.08 us (5%)
  other arithmetic  1.89 us (2%)
    all_to_all x1, starting transfers between devices, local(): recv = lax.all_to_all(send, 'cell', split_axis=0, concat_axis=0, tiled=True)  17.1 us
    all_to_all x1, waiting for transfers between devices, local(): recv = lax.all_to_all(send, 'cell', split_axis=0, concat_axis=0, tiled=True)  13 us
    all_to_all x1, waiting for transfers between devices, local(): lax.all_to_all(partial.reshape(n_source, 2, cap * directions // 2), 'cell...  11 us
    all_to_all x1, waiting for transfers between devices, local(): lax.all_to_all(w_send.reshape(n_source, 2, cap * directions // 2), 'cell'...  9.96 us
    all_to_all x1, waiting for transfers between devices, local(): lax.all_to_all(copies, 'tm', split_axis=0, concat_axis=0, tiled=True)  9.86 us
    all_to_all x1, starting transfers between devices, local(): lax.all_to_all(copies, 'tm', split_axis=0, concat_axis=0, tiled=True)  7.51 us
    all_to_all x1, starting transfers between devices, local(): lax.all_to_all(partial.reshape(n_source, 2, cap * directions // 2), 'cell...  5.83 us
    all_to_all x1, starting transfers between devices, local(): lax.all_to_all(w_send.reshape(n_source, 2, cap * directions // 2), 'cell'...  4.62 us
  transfers between devices with their start and end apart: 4, of which 4 were waited for; matrix products, arithmetic and copies ran while one was open for 2% of the time, Pallas kernels for 0%

profile of v19, /device:TPU:1, one launch (start us, length us, event | category | flops | bytes accessed | tf_op | source)
XLA Modules:
  0.0 97.7 jit_solution(8346387575251576499)
XLA Ops:
  0.6 0.8 copy.97
  1.6 0.7 iota_compare_fusion.11
  2.4 0.8 copy.103
  3.3 0.8 copy.102
  4.2 0.2 select_reduce_fusion.1
  4.4 0.3 fusion.10
  4.7 0.5 fusion.6
  5.3 0.3 select_reduce_fusion
  5.8 1.0 %reshape.272 = bf16[64,2,1088]{2,1,0:T(2,128)(2,1)} reshape(bf16[64,2176]{1,0:T(8,128)(2,1)S(1)} %concatenate.6) | data formatting | bytes 557056 | tf_op jit(solution)/shard_map/reshape | solution.py:45
  6.8 17.1 %all-to-all-start = ((bf16[64,2,1088]{2,1,0:T(2,128)(2,1)}), bf16[64,2,1088]{2,1,0:T(2,128)(2,1)S(1)}, u32[]{:S(2)}, u32[]{:S(2)}) async-start(bf16[64,2,1088]{2,1,0:T(2,128)(2,1)} %reshape.272), calls=%async_computation | async-start | bytes 589824 | tf_op jit(solution)/shard_map/all_to_all | solution.py:46
  24.2 13.0 %all-to-all-done = bf16[64,2,1088]{2,1,0:T(2,128)(2,1)S(1)} async-done(((bf16[64,2,1088]{2,1,0:T(2,128)(2,1)}), bf16[64,2,1088]{2,1,0:T(2,128)(2,1)S(1)}, u32[]{:S(2)}, u32[]{:S(2)}) %all-to-all-start) | async-done | bytes 278560 | tf_op jit(solution)/shard_map/all_to_all | solution.py:46
  37.7 0.3 fusion.5
  38.2 0.9 reshape.277
  39.0 5.8 %all-to-all-start.1 = ((f32[64,2,128]{2,1,0:T(2,128)}), f32[64,2,128]{2,1,0:T(2,128)S(1)}, u32[]{:S(2)}, u32[]{:S(2)}) async-start(f32[64,2,128]{2,1,0:T(2,128)} %reshape.277), calls=%async_computation.1 | async-start | bytes 131072 | tf_op jit(solution)/shard_map/all_to_all | solution.py:58
  45.0 11.0 %all-to-all-done.1 = f32[64,2,128]{2,1,0:T(2,128)S(1)} async-done(((f32[64,2,128]{2,1,0:T(2,128)}), f32[64,2,128]{2,1,0:T(2,128)S(1)}, u32[]{:S(2)}, u32[]{:S(2)}) %all-to-all-start.1) | async-done | bytes 65568 | tf_op jit(solution)/shard_map/all_to_all | solution.py:58
  55.9 0.2 reshape.278
  56.2 1.1 %fusion.7 = f32[64,16]{1,0:T(8,128)S(1)} fusion(s32[64,8]{1,0:T(8,128)S(1)} %fusion.29, f32[1024,16]{1,0:T(8,128)S(1)} %reshape.278), kind=kOutput, calls=%fused_computation.10 | convolution fusion | flops 101194752 | bytes 71680 | tf_op jit(solution)/shard_map/dot_general | solution.py:63
  57.6 0.9 broadcast_in_dim.66
  58.5 7.5 %all-to-all-start.2 = ((bf16[8,280,128]{2,1,0:T(8,128)(2,1)}), bf16[8,280,128]{2,1,0:T(8,128)(2,1)S(1)}, u32[]{:S(2)}, u32[]{:S(2)}) async-start(bf16[8,280,128]{2,1,0:T(8,128)(2,1)} %broadcast_in_dim.66), calls=%async_computation.2 | async-start | bytes 1146880 | tf_op jit(solution)/shard_map/all_to_all | solution.py:74
  66.2 9.9 %all-to-all-done.2 = bf16[8,280,128]{2,1,0:T(8,128)(2,1)S(1)} async-done(((bf16[8,280,128]{2,1,0:T(8,128)(2,1)}), bf16[8,280,128]{2,1,0:T(8,128)(2,1)S(1)}, u32[]{:S(2)}, u32[]{:S(2)}) %all-to-all-start.2) | async-done | bytes 573472 | tf_op jit(solution)/shard_map/all_to_all | solution.py:74
  76.0 0.2 reshape.284
  76.4 1.0 %fusion = f32[1024,16]{1,0:T(8,128)S(1)} fusion(s32[512]{0:T(512)S(1)} %get-tuple-element.20, f32[64,16]{1,0:T(8,128)S(1)} %broadcast_multiply_fusion.1), kind=kOutput, calls=%fused_computation.2 | convolution fusion | flops 101187584 | bytes 71680 | tf_op jit(solution)/shard_map/dot_general | solution.py:82
  77.5 0.9 reshape.280
  78.3 4.6 %all-to-all-start.3 = ((f32[64,2,128]{2,1,0:T(2,128)}), f32[64,2,128]{2,1,0:T(2,128)S(1)}, u32[]{:S(2)}, u32[]{:S(2)}) async-start(f32[64,2,128]{2,1,0:T(2,128)} %reshape.280), calls=%async_computation.3 | async-start | bytes 131072 | tf_op jit(solution)/shard_map/all_to_all | solution.py:85
  83.0 0.7 copy.113
  83.8 0.3 reshape.282
  84.1 10.0 %all-to-all-done.3 = f32[64,2,128]{2,1,0:T(2,128)S(1)} async-done(((f32[64,2,128]{2,1,0:T(2,128)}), f32[64,2,128]{2,1,0:T(2,128)S(1)}, u32[]{:S(2)}, u32[]{:S(2)}) %all-to-all-start.3) | async-done | bytes 65568 | tf_op jit(solution)/shard_map/all_to_all | solution.py:85
  94.4 0.3 broadcast_multiply_fusion
  94.7 0.4 mul.87
  95.1 0.6 fusion.37
  95.7 1.3 %convolution_add_fusion = f32[4,16,512]{2,0,1:T(4,128)S(1)} fusion(bf16[32,16,512]{2,1,0:T(8,128)(2,1)S(1)} %reshape.282, f32[4,16,512]{2,1,0:T(8,128)S(1)} %reshape.281, f32[32,32]{1,0:T(8,128)} %param.15, s32[]{:T(128)S(6)} %select_n.44), kind=kOutput, calls=%fused_computation.11 | convolution fusion | flops 12615680 | bytes 788484 | tf_op jit(solution)/shard_map/ts,skn->tkn/dot_general | solution.py:84
  97.0 0.7 copy.114
  (48 shorter events, 2.7 us)
Async XLA Ops:
  0.6 4.1 %copy-start = (bf16[64,8,128]{2,1,0:T(8,128)(2,1)S(1)}, bf16[64,8,128]{2,1,0:T(8,128)(2,1)}, u32[]{:S(2)}) copy-start(bf16[64,8,128]{2,1,0:T(8,128)(2,1)} %param.9) | copy-start | bytes 393220
  5.2 18.8 %copy-start.1 = (bf16[4,16,512]{2,1,0:T(8,128)(2,1)S(1)}, bf16[4,16,512]{2,1,0:T(8,128)(2,1)}, u32[]{:S(2)}) copy-start(bf16[4,16,512]{2,1,0:T(8,128)(2,1)} %param.8) | copy-start | bytes 196612
  6.8 30.4 %all-to-all-start = ((bf16[64,2,1088]{2,1,0:T(2,128)(2,1)}), bf16[64,2,1088]{2,1,0:T(2,128)(2,1)S(1)}, u32[]{:S(2)}, u32[]{:S(2)}) async-start(bf16[64,2,1088]{2,1,0:T(2,128)(2,1)} %reshape.272), calls=%async_computation | async-start | bytes 589824 | tf_op jit(solution)/shard_map/all_to_all | solution.py:46
  37.7 7.2 %copy-start.2 = (s32[64,1]{0,1:T(1,128)S(1)}, s32[64,1]{0,1:T(1,128)}, u32[]{:S(2)}) copy-start(s32[64,1]{0,1:T(1,128)} %param.12) | copy-start | bytes 772
  39.0 16.9 %all-to-all-start.1 = ((f32[64,2,128]{2,1,0:T(2,128)}), f32[64,2,128]{2,1,0:T(2,128)S(1)}, u32[]{:S(2)}, u32[]{:S(2)}) async-start(f32[64,2,128]{2,1,0:T(2,128)} %reshape.277), calls=%async_computation.1 | async-start | bytes 131072 | tf_op jit(solution)/shard_map/all_to_all | solution.py:58
  58.5 17.5 %all-to-all-start.2 = ((bf16[8,280,128]{2,1,0:T(8,128)(2,1)}), bf16[8,280,128]{2,1,0:T(8,128)(2,1)S(1)}, u32[]{:S(2)}, u32[]{:S(2)}) async-start(bf16[8,280,128]{2,1,0:T(8,128)(2,1)} %broadcast_in_dim.66), calls=%async_computation.2 | async-start | bytes 1146880 | tf_op jit(solution)/shard_map/all_to_all | solution.py:74
  66.2 10.2 %copy-start.3 = (f32[64]{0:T(128)S(1)}, f32[64]{0:T(128)}, u32[]{:S(2)}) copy-start(f32[64]{0:T(128)} %param.14) | copy-start | bytes 772
  78.3 15.7 %all-to-all-start.3 = ((f32[64,2,128]{2,1,0:T(2,128)}), f32[64,2,128]{2,1,0:T(2,128)S(1)}, u32[]{:S(2)}, u32[]{:S(2)}) async-start(f32[64,2,128]{2,1,0:T(2,128)} %reshape.280), calls=%async_computation.3 | async-start | bytes 131072 | tf_op jit(solution)/shard_map/all_to_all | solution.py:85

commit v20 on v19

--- a/solution.py
+++ b/solution.py
@@ -23,9 +23,10 @@
     slot_ids = block_slot.reshape(n_blocks)
     source = slot_ids // per_source
     position = slot_ids % per_source
-    table = request_tiles[0].reshape(n_source * per_source)
-    pick = slot_ids[:, None] == jnp.arange(n_source * per_source, dtype=jnp.int32)[None, :]
-    local_tile = jnp.sum(jnp.where(pick, table[None, :], 0), axis=1)
+    table = request_tiles[0]
+    chosen = jnp.where(position[:, None] == 0, table[None, :, 0], table[None, :, per_source - 1])
+    pick = source[:, None] == jnp.arange(n_source, dtype=jnp.int32)[None, :]
+    local_tile = jnp.sum(jnp.where(pick, chosen, 0), axis=1)
     meta = local_tile * slices + block_time.reshape(n_blocks)
     src_hot = (source[:, None] == jnp.arange(n_source, dtype=jnp.int32)[None, :]) & live[:, None]
     src_hot_b = src_hot.astype(jnp.bfloat16)

time: 98.1 us -> 97.8 us (level)
    unnamed x13 -> x12, local copies, waits for them, and re-layouts: 3.75 us -> 2.98 us
where the time goes in v20:
time: 97.8 us; the launch traced here: 97.4 us
  waiting for transfers between devices  43.8 us (45%)
  starting transfers between devices  35 us (36%)
  local copies, waits for them, and re-layouts  10.7 us (11%)
  matrix products  5.09 us (5%)
  other arithmetic  1.77 us (2%)
  between operations  0.99 us (1%)
    all_to_all x1, starting transfers between devices, local(): recv = lax.all_to_all(send, 'cell', split_axis=0, concat_axis=0, tiled=True)  17.1 us
    all_to_all x1, waiting for transfers between devices, local(): recv = lax.all_to_all(send, 'cell', split_axis=0, concat_axis=0, tiled=True)  13 us
    all_to_all x1, waiting for transfers between devices, local(): lax.all_to_all(partial.reshape(n_source, 2, cap * directions // 2), 'cell...  11 us
    all_to_all x1, waiting for transfers between devices, local(): lax.all_to_all(w_send.reshape(n_source, 2, cap * directions // 2), 'cell'...  9.96 us
    all_to_all x1, waiting for transfers between devices, local(): lax.all_to_all(copies, 'tm', split_axis=0, concat_axis=0, tiled=True)  9.86 us
    all_to_all x1, starting transfers between devices, local(): lax.all_to_all(copies, 'tm', split_axis=0, concat_axis=0, tiled=True)  7.48 us
    all_to_all x1, starting transfers between devices, local(): lax.all_to_all(partial.reshape(n_source, 2, cap * directions // 2), 'cell...  5.81 us
    all_to_all x1, starting transfers between devices, local(): lax.all_to_all(w_send.reshape(n_source, 2, cap * directions // 2), 'cell'...  4.62 us
  transfers between devices with their start and end apart: 4, of which 4 were waited for; matrix products, arithmetic and copies ran while one was open for 2% of the time, Pallas kernels for 0%

profile of v20, /device:TPU:1, one launch (start us, length us, event | category | flops | bytes accessed | tf_op | source)
XLA Modules:
  0.0 97.4 jit_solution(9895130360492463876)
XLA Ops:
  0.6 0.8 copy.91
  1.6 0.7 iota_compare_fusion.10
  2.4 0.8 copy.96
  3.3 0.8 slice_bitcast_fusion.1
  4.0 0.3 fusion.10
  4.5 0.5 fusion.6
  5.1 0.3 select_reduce_fusion
  5.6 1.0 %reshape.295 = bf16[64,2,1088]{2,1,0:T(2,128)(2,1)} reshape(bf16[64,2176]{1,0:T(8,128)(2,1)S(1)} %concatenate.6) | data formatting | bytes 557056 | tf_op jit(solution)/shard_map/reshape | solution.py:46
  6.6 17.1 %all-to-all-start = ((bf16[64,2,1088]{2,1,0:T(2,128)(2,1)}), bf16[64,2,1088]{2,1,0:T(2,128)(2,1)S(1)}, u32[]{:S(2)}, u32[]{:S(2)}) async-start(bf16[64,2,1088]{2,1,0:T(2,128)(2,1)} %reshape.295), calls=%async_computation | async-start | bytes 589824 | tf_op jit(solution)/shard_map/all_to_all | solution.py:47
  23.9 13.0 %all-to-all-done = bf16[64,2,1088]{2,1,0:T(2,128)(2,1)S(1)} async-done(((bf16[64,2,1088]{2,1,0:T(2,128)(2,1)}), bf16[64,2,1088]{2,1,0:T(2,128)(2,1)S(1)}, u32[]{:S(2)}, u32[]{:S(2)}) %all-to-all-start) | async-done | bytes 278560 | tf_op jit(solution)/shard_map/all_to_all | solution.py:47
  37.4 0.3 fusion.5
  37.9 0.9 reshape.300
  38.8 5.8 %all-to-all-start.1 = ((f32[64,2,128]{2,1,0:T(2,128)}), f32[64,2,128]{2,1,0:T(2,128)S(1)}, u32[]{:S(2)}, u32[]{:S(2)}) async-start(f32[64,2,128]{2,1,0:T(2,128)} %reshape.300), calls=%async_computation.1 | async-start | bytes 131072 | tf_op jit(solution)/shard_map/all_to_all | solution.py:59
  44.7 11.0 %all-to-all-done.1 = f32[64,2,128]{2,1,0:T(2,128)S(1)} async-done(((f32[64,2,128]{2,1,0:T(2,128)}), f32[64,2,128]{2,1,0:T(2,128)S(1)}, u32[]{:S(2)}, u32[]{:S(2)}) %all-to-all-start.1) | async-done | bytes 65568 | tf_op jit(solution)/shard_map/all_to_all | solution.py:59
  55.7 0.2 reshape.301
  55.9 1.1 %fusion.7 = f32[64,16]{1,0:T(8,128)S(1)} fusion(s32[64,8]{1,0:T(8,128)S(1)} %fusion.29, f32[1024,16]{1,0:T(8,128)S(1)} %reshape.301), kind=kOutput, calls=%fused_computation.10 | convolution fusion | flops 101194752 | bytes 71680 | tf_op jit(solution)/shard_map/dot_general | solution.py:64
  57.4 0.9 broadcast_in_dim.89
  58.3 7.5 %all-to-all-start.2 = ((bf16[8,280,128]{2,1,0:T(8,128)(2,1)}), bf16[8,280,128]{2,1,0:T(8,128)(2,1)S(1)}, u32[]{:S(2)}, u32[]{:S(2)}) async-start(bf16[8,280,128]{2,1,0:T(8,128)(2,1)} %broadcast_in_dim.89), calls=%async_computation.2 | async-start | bytes 1146880 | tf_op jit(solution)/shard_map/all_to_all | solution.py:75
  65.9 9.9 %all-to-all-done.2 = bf16[8,280,128]{2,1,0:T(8,128)(2,1)S(1)} async-done(((bf16[8,280,128]{2,1,0:T(8,128)(2,1)}), bf16[8,280,128]{2,1,0:T(8,128)(2,1)S(1)}, u32[]{:S(2)}, u32[]{:S(2)}) %all-to-all-start.2) | async-done | bytes 573472 | tf_op jit(solution)/shard_map/all_to_all | solution.py:75
  75.8 0.2 reshape.307
  76.1 1.0 %fusion = f32[1024,16]{1,0:T(8,128)S(1)} fusion(s32[512]{0:T(512)S(1)} %get-tuple-element.22, f32[64,16]{1,0:T(8,128)S(1)} %broadcast_multiply_fusion.1), kind=kOutput, calls=%fused_computation.2 | convolution fusion | flops 101187584 | bytes 71680 | tf_op jit(solution)/shard_map/dot_general | solution.py:83
  77.2 0.9 reshape.303
  78.1 4.6 %all-to-all-start.3 = ((f32[64,2,128]{2,1,0:T(2,128)}), f32[64,2,128]{2,1,0:T(2,128)S(1)}, u32[]{:S(2)}, u32[]{:S(2)}) async-start(f32[64,2,128]{2,1,0:T(2,128)} %reshape.303), calls=%async_computation.3 | async-start | bytes 131072 | tf_op jit(solution)/shard_map/all_to_all | solution.py:86
  82.8 0.7 copy.106
  83.5 0.3 reshape.305
  83.8 10.0 %all-to-all-done.3 = f32[64,2,128]{2,1,0:T(2,128)S(1)} async-done(((f32[64,2,128]{2,1,0:T(2,128)}), f32[64,2,128]{2,1,0:T(2,128)S(1)}, u32[]{:S(2)}, u32[]{:S(2)}) %all-to-all-start.3) | async-done | bytes 65568 | tf_op jit(solution)/shard_map/all_to_all | solution.py:86
  93.8 0.2 mul.84
  94.1 0.3 broadcast_multiply_fusion
  94.4 0.4 mul.87
  94.8 0.6 fusion.37
  95.4 1.3 %convolution_add_fusion = f32[4,16,512]{2,0,1:T(4,128)S(1)} fusion(bf16[32,16,512]{2,1,0:T(8,128)(2,1)S(1)} %reshape.305, f32[4,16,512]{2,1,0:T(8,128)S(1)} %reshape.304, f32[32,32]{1,0:T(8,128)} %param.15, s32[]{:T(128)S(6)} %select_n.61), kind=kOutput, calls=%fused_computation.11 | convolution fusion | flops 12615680 | bytes 788484 | tf_op jit(solution)/shard_map/ts,skn->tkn/dot_general | solution.py:85
  96.7 0.7 copy.107
  (48 shorter events, 2.5 us)
Async XLA Ops:
  0.6 3.8 %copy-start = (bf16[64,8,128]{2,1,0:T(8,128)(2,1)S(1)}, bf16[64,8,128]{2,1,0:T(8,128)(2,1)}, u32[]{:S(2)}) copy-start(bf16[64,8,128]{2,1,0:T(8,128)(2,1)} %param.9) | copy-start | bytes 393220
  4.9 18.8 %copy-start.1 = (bf16[4,16,512]{2,1,0:T(8,128)(2,1)S(1)}, bf16[4,16,512]{2,1,0:T(8,128)(2,1)}, u32[]{:S(2)}) copy-start(bf16[4,16,512]{2,1,0:T(8,128)(2,1)} %param.8) | copy-start | bytes 196612
  6.6 30.4 %all-to-all-start = ((bf16[64,2,1088]{2,1,0:T(2,128)(2,1)}), bf16[64,2,1088]{2,1,0:T(2,128)(2,1)S(1)}, u32[]{:S(2)}, u32[]{:S(2)}) async-start(bf16[64,2,1088]{2,1,0:T(2,128)(2,1)} %reshape.295), calls=%async_computation | async-start | bytes 589824 | tf_op jit(solution)/shard_map/all_to_all | solution.py:47
  37.4 7.2 %copy-start.2 = (s32[64,1]{0,1:T(1,128)S(1)}, s32[64,1]{0,1:T(1,128)}, u32[]{:S(2)}) copy-start(s32[64,1]{0,1:T(1,128)} %param.12) | copy-start | bytes 772
  38.8 16.9 %all-to-all-start.1 = ((f32[64,2,128]{2,1,0:T(2,128)}), f32[64,2,128]{2,1,0:T(2,128)S(1)}, u32[]{:S(2)}, u32[]{:S(2)}) async-start(f32[64,2,128]{2,1,0:T(2,128)} %reshape.300), calls=%async_computation.1 | async-start | bytes 131072 | tf_op jit(solution)/shard_map/all_to_all | solution.py:59
  58.3 17.5 %all-to-all-start.2 = ((bf16[8,280,128]{2,1,0:T(8,128)(2,1)}), bf16[8,280,128]{2,1,0:T(8,128)(2,1)S(1)}, u32[]{:S(2)}, u32[]{:S(2)}) async-start(bf16[8,280,128]{2,1,0:T(8,128)(2,1)} %broadcast_in_dim.89), calls=%async_computation.2 | async-start | bytes 1146880 | tf_op jit(solution)/shard_map/all_to_all | solution.py:75
  65.9 10.2 %copy-start.3 = (f32[64]{0:T(128)S(1)}, f32[64]{0:T(128)}, u32[]{:S(2)}) copy-start(f32[64]{0:T(128)} %param.14) | copy-start | bytes 772
  78.1 15.7 %all-to-all-start.3 = ((f32[64,2,128]{2,1,0:T(2,128)}), f32[64,2,128]{2,1,0:T(2,128)S(1)}, u32[]{:S(2)}, u32[]{:S(2)}) async-start(f32[64,2,128]{2,1,0:T(2,128)} %reshape.303), calls=%async_computation.3 | async-start | bytes 131072 | tf_op jit(solution)/shard_map/all_to_all | solution.py:86

commit v21 on v20

--- a/solution.py
+++ b/solution.py
@@ -27,7 +27,7 @@
     chosen = jnp.where(position[:, None] == 0, table[None, :, 0], table[None, :, per_source - 1])
     pick = source[:, None] == jnp.arange(n_source, dtype=jnp.int32)[None, :]
     local_tile = jnp.sum(jnp.where(pick, chosen, 0), axis=1)
-    meta = local_tile * slices + block_time.reshape(n_blocks)
+    meta = (local_tile.reshape(sounds, nb) * slices + block_time).reshape(n_blocks)
     src_hot = (source[:, None] == jnp.arange(n_source, dtype=jnp.int32)[None, :]) & live[:, None]
     src_hot_b = src_hot.astype(jnp.bfloat16)
     row = jnp.arange(n_blocks, dtype=jnp.int32)

time: 97.8 us -> 96.5 us (0.987)
  local copies, waits for them, and re-layouts: 10.7 us -> 9.32 us
    unnamed x12 -> x16, local copies, waits for them, and re-layouts: 2.98 us -> 2.3 us
where the time goes in v21:
time: 96.5 us; the launch traced here: 96.1 us
  waiting for transfers between devices  43.8 us (45%)
  starting transfers between devices  35.1 us (36%)
  local copies, waits for them, and re-layouts  9.32 us (10%)
  matrix products  5.08 us (5%)
  other arithmetic  1.78 us (2%)
  between operations  1.05 us (1%)
    all_to_all x1, starting transfers between devices, local(): recv = lax.all_to_all(send, 'cell', split_axis=0, concat_axis=0, tiled=True)  17.1 us
    all_to_all x1, waiting for transfers between devices, local(): recv = lax.all_to_all(send, 'cell', split_axis=0, concat_axis=0, tiled=True)  13 us
    all_to_all x1, waiting for transfers between devices, local(): lax.all_to_all(partial.reshape(n_source, 2, cap * directions // 2), 'cell...  11 us
    all_to_all x1, waiting for transfers between devices, local(): lax.all_to_all(w_send.reshape(n_source, 2, cap * directions // 2), 'cell'...  9.96 us
    all_to_all x1, waiting for transfers between devices, local(): lax.all_to_all(copies, 'tm', split_axis=0, concat_axis=0, tiled=True)  9.86 us
    all_to_all x1, starting transfers between devices, local(): lax.all_to_all(copies, 'tm', split_axis=0, concat_axis=0, tiled=True)  7.51 us
    all_to_all x1, starting transfers between devices, local(): lax.all_to_all(partial.reshape(n_source, 2, cap * directions // 2), 'cell...  5.82 us
    all_to_all x1, starting transfers between devices, local(): lax.all_to_all(w_send.reshape(n_source, 2, cap * directions // 2), 'cell'...  4.62 us
  transfers between devices with their start and end apart: 4, of which 4 were waited for; matrix products, arithmetic and copies ran while one was open for 2% of the time, Pallas kernels for 0%

profile of v21, /device:TPU:1, one launch (start us, length us, event | category | flops | bytes accessed | tf_op | source)
XLA Modules:
  0.0 96.1 jit_solution(12792210115372333872)
XLA Ops:
  0.6 0.8 copy.91
  1.6 0.7 iota_compare_fusion.10
  2.4 0.3 fusion.10
  2.8 0.5 fusion.6
  3.8 0.3 select_reduce_fusion
  4.3 1.0 %reshape.287 = bf16[64,2,1088]{2,1,0:T(2,128)(2,1)} reshape(bf16[64,2176]{1,0:T(8,128)(2,1)S(1)} %concatenate.6) | data formatting | bytes 557056 | tf_op jit(solution)/shard_map/reshape | solution.py:46
  5.3 17.1 %all-to-all-start = ((bf16[64,2,1088]{2,1,0:T(2,128)(2,1)}), bf16[64,2,1088]{2,1,0:T(2,128)(2,1)S(1)}, u32[]{:S(2)}, u32[]{:S(2)}) async-start(bf16[64,2,1088]{2,1,0:T(2,128)(2,1)} %reshape.287), calls=%async_computation | async-start | bytes 589824 | tf_op jit(solution)/shard_map/all_to_all | solution.py:47
  22.6 13.0 %all-to-all-done = bf16[64,2,1088]{2,1,0:T(2,128)(2,1)S(1)} async-done(((bf16[64,2,1088]{2,1,0:T(2,128)(2,1)}), bf16[64,2,1088]{2,1,0:T(2,128)(2,1)S(1)}, u32[]{:S(2)}, u32[]{:S(2)}) %all-to-all-start) | async-done | bytes 278560 | tf_op jit(solution)/shard_map/all_to_all | solution.py:47
  35.6 0.2 reshape.288
  36.1 0.3 fusion.5
  36.4 0.2 copy.98
  36.6 0.9 reshape.292
  37.5 5.8 %all-to-all-start.1 = ((f32[64,2,128]{2,1,0:T(2,128)}), f32[64,2,128]{2,1,0:T(2,128)S(1)}, u32[]{:S(2)}, u32[]{:S(2)}) async-start(f32[64,2,128]{2,1,0:T(2,128)} %reshape.292), calls=%async_computation.1 | async-start | bytes 131072 | tf_op jit(solution)/shard_map/all_to_all | solution.py:59
  43.4 11.0 %all-to-all-done.1 = f32[64,2,128]{2,1,0:T(2,128)S(1)} async-done(((f32[64,2,128]{2,1,0:T(2,128)}), f32[64,2,128]{2,1,0:T(2,128)S(1)}, u32[]{:S(2)}, u32[]{:S(2)}) %all-to-all-start.1) | async-done | bytes 65568 | tf_op jit(solution)/shard_map/all_to_all | solution.py:59
  54.4 0.2 reshape.293
  54.6 1.1 %fusion.7 = f32[64,16]{1,0:T(8,128)S(1)} fusion(s32[64,8]{1,0:T(8,128)S(1)} %fusion.29, f32[1024,16]{1,0:T(8,128)S(1)} %reshape.293), kind=kOutput, calls=%fused_computation.10 | convolution fusion | flops 101194752 | bytes 71680 | tf_op jit(solution)/shard_map/dot_general | solution.py:64
  56.1 0.9 broadcast_in_dim.91
  57.0 7.5 %all-to-all-start.2 = ((bf16[8,280,128]{2,1,0:T(8,128)(2,1)}), bf16[8,280,128]{2,1,0:T(8,128)(2,1)S(1)}, u32[]{:S(2)}, u32[]{:S(2)}) async-start(bf16[8,280,128]{2,1,0:T(8,128)(2,1)} %broadcast_in_dim.91), calls=%async_computation.2 | async-start | bytes 1146880 | tf_op jit(solution)/shard_map/all_to_all | solution.py:75
  64.6 9.9 %all-to-all-done.2 = bf16[8,280,128]{2,1,0:T(8,128)(2,1)S(1)} async-done(((bf16[8,280,128]{2,1,0:T(8,128)(2,1)}), bf16[8,280,128]{2,1,0:T(8,128)(2,1)S(1)}, u32[]{:S(2)}, u32[]{:S(2)}) %all-to-all-start.2) | async-done | bytes 573472 | tf_op jit(solution)/shard_map/all_to_all | solution.py:75
  74.5 0.2 reshape.299
  74.9 1.0 %fusion = f32[1024,16]{1,0:T(8,128)S(1)} fusion(s32[512]{0:T(512)S(1)} %add_select_fusion.3, f32[64,16]{1,0:T(8,128)S(1)} %broadcast_multiply_fusion.1), kind=kOutput, calls=%fused_computation.2 | convolution fusion | flops 101187584 | bytes 71680 | tf_op jit(solution)/shard_map/dot_general | solution.py:83
  75.9 0.9 reshape.295
  76.8 4.6 %all-to-all-start.3 = ((f32[64,2,128]{2,1,0:T(2,128)}), f32[64,2,128]{2,1,0:T(2,128)S(1)}, u32[]{:S(2)}, u32[]{:S(2)}) async-start(f32[64,2,128]{2,1,0:T(2,128)} %reshape.295), calls=%async_computation.3 | async-start | bytes 131072 | tf_op jit(solution)/shard_map/all_to_all | solution.py:86
  81.5 0.7 copy.106
  82.2 0.3 reshape.297
  82.5 10.0 %all-to-all-done.3 = f32[64,2,128]{2,1,0:T(2,128)S(1)} async-done(((f32[64,2,128]{2,1,0:T(2,128)}), f32[64,2,128]{2,1,0:T(2,128)S(1)}, u32[]{:S(2)}, u32[]{:S(2)}) %all-to-all-start.3) | async-done | bytes 65568 | tf_op jit(solution)/shard_map/all_to_all | solution.py:86
  92.5 0.2 mul.84
  92.9 0.3 broadcast_multiply_fusion
  93.1 0.4 mul.87
  93.5 0.6 fusion.37
  94.1 1.3 %convolution_add_fusion = f32[4,16,512]{2,0,1:T(4,128)S(1)} fusion(bf16[32,16,512]{2,1,0:T(8,128)(2,1)S(1)} %reshape.297, f32[4,16,512]{2,1,0:T(8,128)S(1)} %reshape.296, f32[32,32]{1,0:T(8,128)} %param.15, s32[]{:T(128)S(6)} %select_n.61), kind=kOutput, calls=%fused_computation.11 | convolution fusion | flops 12615680 | bytes 788484 | tf_op jit(solution)/shard_map/ts,skn->tkn/dot_general | solution.py:85
  95.4 0.7 copy.107
  (55 shorter events, 2.3 us)
Async XLA Ops:
  0.6 2.1 %copy-start = (bf16[64,8,128]{2,1,0:T(8,128)(2,1)S(1)}, bf16[64,8,128]{2,1,0:T(8,128)(2,1)}, u32[]{:S(2)}) copy-start(bf16[64,8,128]{2,1,0:T(8,128)(2,1)} %param.9) | copy-start | bytes 393220
  1.5 1.8 %copy-start.4 = (s32[1,64,2]{1,2,0:T(2,128)S(1)}, s32[1,64,2]{1,2,0:T(2,128)}, u32[]{:S(2)}) copy-start(s32[1,64,2]{1,2,0:T(2,128)} %param.13) | copy-start | bytes 1540
  2.4 1.2 %copy-start.2 = (s32[64,8]{0,1:T(8,128)S(1)}, s32[64,8]{0,1:T(8,128)}, u32[]{:S(2)}) copy-start(s32[64,8]{0,1:T(8,128)} %param.11) | copy-start | bytes 6148
  3.3 19.1 %copy-start.1 = (bf16[4,16,512]{2,1,0:T(8,128)(2,1)S(1)}, bf16[4,16,512]{2,1,0:T(8,128)(2,1)}, u32[]{:S(2)}) copy-start(bf16[4,16,512]{2,1,0:T(8,128)(2,1)} %param.8) | copy-start | bytes 196612
  5.3 30.4 %all-to-all-start = ((bf16[64,2,1088]{2,1,0:T(2,128)(2,1)}), bf16[64,2,1088]{2,1,0:T(2,128)(2,1)S(1)}, u32[]{:S(2)}, u32[]{:S(2)}) async-start(bf16[64,2,1088]{2,1,0:T(2,128)(2,1)} %reshape.287), calls=%async_computation | async-start | bytes 589824 | tf_op jit(solution)/shard_map/all_to_all | solution.py:47
  36.1 7.2 %copy-start.3 = (s32[64,1]{0,1:T(1,128)S(1)}, s32[64,1]{0,1:T(1,128)}, u32[]{:S(2)}) copy-start(s32[64,1]{0,1:T(1,128)} %param.12) | copy-start | bytes 772
  37.5 16.9 %all-to-all-start.1 = ((f32[64,2,128]{2,1,0:T(2,128)}), f32[64,2,128]{2,1,0:T(2,128)S(1)}, u32[]{:S(2)}, u32[]{:S(2)}) async-start(f32[64,2,128]{2,1,0:T(2,128)} %reshape.292), calls=%async_computation.1 | async-start | bytes 131072 | tf_op jit(solution)/shard_map/all_to_all | solution.py:59
  57.0 17.5 %all-to-all-start.2 = ((bf16[8,280,128]{2,1,0:T(8,128)(2,1)}), bf16[8,280,128]{2,1,0:T(8,128)(2,1)S(1)}, u32[]{:S(2)}, u32[]{:S(2)}) async-start(bf16[8,280,128]{2,1,0:T(8,128)(2,1)} %broadcast_in_dim.91), calls=%async_computation.2 | async-start | bytes 1146880 | tf_op jit(solution)/shard_map/all_to_all | solution.py:75
  64.6 10.2 %copy-start.5 = (f32[64]{0:T(128)S(1)}, f32[64]{0:T(128)}, u32[]{:S(2)}) copy-start(f32[64]{0:T(128)} %param.14) | copy-start | bytes 772
  76.8 15.7 %all-to-all-start.3 = ((f32[64,2,128]{2,1,0:T(2,128)}), f32[64,2,128]{2,1,0:T(2,128)S(1)}, u32[]{:S(2)}, u32[]{:S(2)}) async-start(f32[64,2,128]{2,1,0:T(2,128)} %reshape.295), calls=%async_computation.3 | async-start | bytes 131072 | tf_op jit(solution)/shard_map/all_to_all | solution.py:86
